TPU v7x, 128 devices: a whole 4x4x4 slice. The times are simulated.
128 devices in a mesh: dp: 8 (over x, core), fsdp: 16 (over y, z).
Axes of the slice: x: 4, y: 4, z: 4, core: 2. Of those that a mesh axis runs over, the one named last changes fastest.
Arguments:
- tokens: bfloat16 [65536, 8192], P(('dp', 'fsdp')), may hold values from -6 to 6
- frozen_value_matrix: bfloat16 [8192, 1024], P('fsdp'), may hold values from -0.0625 to 0.0625
- adapter_down_maps: bfloat16 [512, 64, 8192], P('dp', None, 'fsdp'), may hold values from -0.0625 to 0.0625
- adapter_up_maps: bfloat16 [512, 64, 1024], P('dp', None, 'fsdp'), may hold values from -0.375 to 0.375
- value_output_gradient: bfloat16 [65536, 1024], P(('dp', 'fsdp')), may hold values from -0.125 to 0.125
- window_composer_position: int32 [8, 64], P('dp'), may hold values from 0 to 3
- needed_composers: int32 [8, 4], replicated, may hold values from 0 to 511, as said below
- composer_storage_index: int32 [512], replicated, may hold values from 0 to 511, as said below
Outputs:
- value: bfloat16 [65536, 1024], P(('dp', 'fsdp'))
- grad_down: float32 [512, 64, 8192], P('dp', None, 'fsdp')
- grad_up: float32 [512, 64, 1024], P('dp', None, 'fsdp')
Inputs may be any that keep to these rules, and one draw needn't show every extreme that they name: Every storage index appears once: the adapters and gradients of composer c lie at index composer_storage_index[c]; composer c is owned by index composer_storage_index[c] // 64 of dp. `needed_composers`: the 4 composers of one row have 4 different owners along dp.
All inputs are finite; a program needn't handle non-finite values.
Results may differ from a plain program's by a relative error of at most 0.004.
Values may be sent and summed in bfloat16 or wider, within the bound.
No kernel may reach another device: no remote copies, remote signals or barrier semaphores. Data moves between devices by JAX's collectives and lax.ppermute only.
A program may use at most 128 MiB of HBM per device.

v0:
```python
import jax
import jax.numpy as jnp
from jax import lax
from jax.sharding import PartitionSpec as P

WIN = 128


ADAPTER_SCALE = 2.0


def body(
    tokens,
    frozen_value_matrix,
    adapter_down_maps,
    adapter_up_maps,
    value_output_gradient,
    window_composer_position,
    needed_composers,
    composer_storage_index,
):
    dp_count = lax.axis_size("dp")
    group_index = lax.axis_index("dp")
    member_index = lax.axis_index("fsdp")
    tok_rows = tokens.shape[0]
    down_cols = frozen_value_matrix.shape[0]
    up_matrix_columns = adapter_up_maps.shape[2]
    adapter_rank_width = adapter_down_maps.shape[1]
    each_owner_rows = adapter_down_maps.shape[0]
    list_len = needed_composers.shape[1]
    windows = tok_rows // WIN
    total_comp = composer_storage_index.shape[0]
    contract = (((0,), (0,)), ((), ()))
    frozen_value_output = jnp.dot(
        tokens,
        lax.all_gather(frozen_value_matrix, "fsdp", axis=0, tiled=True),
        preferred_element_type=jnp.float32,
    )
    catalog = jnp.arange(total_comp, dtype=jnp.int32)
    matches = needed_composers[:, :, None] == catalog[None, None, :]
    list_slot = jnp.sum(jnp.where(matches, composer_storage_index[None, None, :], 0), axis=2)
    list_owner = list_slot // each_owner_rows
    list_local = list_slot % each_owner_rows
    owned_here = list_owner == group_index
    locally_owned_slots = jnp.sum(jnp.where(owned_here, list_local, 0), axis=1)
    owned_any = jnp.any(owned_here, axis=1)
    send_down = jnp.where(
        owned_any[:, None, None],
        jnp.take(adapter_down_maps, locally_owned_slots, axis=0),
        jnp.zeros((), adapter_down_maps.dtype),
    )
    send_up = jnp.where(
        owned_any[:, None, None],
        jnp.take(adapter_up_maps, locally_owned_slots, axis=0),
        jnp.zeros((), adapter_up_maps.dtype),
    )
    got_down, got_up = (
        lax.all_to_all(send_down, "dp", split_axis=0, concat_axis=0, tiled=True),
        lax.all_to_all(send_up, "dp", split_axis=0, concat_axis=0, tiled=True),
    )
    my_owner = lax.dynamic_index_in_dim(list_owner, group_index, 0, keepdims=False)
    slab_down = jnp.take(got_down, my_owner, axis=0)
    slab_up = jnp.take(got_up, my_owner, axis=0)
    full_down, full_up = (
        lax.all_gather(slab_down, "fsdp", axis=2, tiled=True),
        lax.all_gather(slab_up, "fsdp", axis=2, tiled=True),
    )
    group_picks = window_composer_position[0]
    my_picks = lax.dynamic_slice_in_dim(group_picks, member_index * windows, windows, 0)
    slot_range = jnp.arange(list_len, dtype=jnp.int32)
    token_hot = jnp.broadcast_to(
        my_picks[:, None, None] == slot_range[None, None, :], (windows, WIN, list_len)
    ).reshape(tok_rows, list_len)
    onehot_float_matrix = token_hot.astype(jnp.float32)
    low_all = jnp.einsum("td,krd->tkr", tokens, full_down, preferred_element_type=jnp.float32)
    rank_projected = jnp.sum(low_all * onehot_float_matrix[:, :, None], axis=1).astype(jnp.bfloat16)
    delta_all = jnp.einsum(
        "tr,krc->tkc", rank_projected, full_up, preferred_element_type=jnp.float32
    )
    adapter_change = jnp.sum(delta_all * onehot_float_matrix[:, :, None], axis=1)
    backward_everything = jnp.einsum(
        "tc,krc->tkr", value_output_gradient, full_up, preferred_element_type=jnp.float32
    )
    backward_rank_rows = (
        ADAPTER_SCALE * jnp.sum(backward_everything * onehot_float_matrix[:, :, None], axis=1)
    ).astype(jnp.bfloat16)
    value = (frozen_value_output + ADAPTER_SCALE * adapter_change).astype(jnp.bfloat16)
    scaled_rank_rows = rank_projected * jnp.asarray(ADAPTER_SCALE, jnp.bfloat16)
    hot_half = token_hot.astype(jnp.bfloat16)
    masked_back = (hot_half[:, :, None] * backward_rank_rows[:, None, :]).reshape(
        tok_rows, list_len * adapter_rank_width
    )
    masked_low = (hot_half[:, :, None] * scaled_rank_rows[:, None, :]).reshape(
        tok_rows, list_len * adapter_rank_width
    )
    block_rows = down_cols + up_matrix_columns
    shards = lax.axis_size("fsdp") * block_rows // block_rows
    down_part = lax.dot_general(tokens, masked_back, contract, preferred_element_type=jnp.float32)
    up_part = lax.dot_general(
        value_output_gradient, masked_low, contract, preferred_element_type=jnp.float32
    )
    down_part = down_part.reshape(shards, down_cols, list_len * adapter_rank_width)
    up_part = up_part.reshape(shards, up_matrix_columns, list_len * adapter_rank_width)
    summed = lax.psum_scatter(
        jnp.concatenate([down_part, up_part], axis=1).reshape(
            lax.axis_size("fsdp") * block_rows, list_len * adapter_rank_width
        ),
        "fsdp",
        scatter_dimension=0,
        tiled=True,
    )
    part_down = summed[:down_cols]
    part_up = summed[down_cols:]
    rows_down = part_down.reshape(down_cols, list_len, adapter_rank_width).transpose(1, 2, 0)
    rows_up = part_up.reshape(up_matrix_columns, list_len, adapter_rank_width).transpose(1, 2, 0)
    owner_range = jnp.arange(dp_count, dtype=jnp.int32)
    to_owner = my_owner[None, :] == owner_range[:, None]
    pick_index = jnp.sum(jnp.where(to_owner, slot_range[None, :], 0), axis=1)
    owner_has = jnp.any(to_owner, axis=1)
    send_grad_down = jnp.where(
        owner_has[:, None, None], jnp.take(rows_down, pick_index, axis=0), 0.0
    )
    send_grad_up = jnp.where(owner_has[:, None, None], jnp.take(rows_up, pick_index, axis=0), 0.0)
    back_down, back_up = (
        lax.all_to_all(send_grad_down, "dp", split_axis=0, concat_axis=0, tiled=True),
        lax.all_to_all(send_grad_up, "dp", split_axis=0, concat_axis=0, tiled=True),
    )
    local_range = jnp.arange(each_owner_rows, dtype=jnp.int32)
    arrivals = (owned_any[:, None] & (locally_owned_slots[:, None] == local_range[None, :])).astype(
        jnp.float32
    )
    grad_down = jnp.einsum("sc,srd->crd", arrivals, back_down, precision=lax.Precision.HIGHEST)
    grad_up = jnp.einsum("sc,srv->crv", arrivals, back_up, precision=lax.Precision.HIGHEST)
    return (value, grad_down, grad_up)


def solution(mesh):
    return jax.shard_map(
        body,
        mesh=mesh,
        in_specs=(
            P(("dp", "fsdp"), None),
            P("fsdp", None),
            P("dp", None, "fsdp"),
            P("dp", None, "fsdp"),
            P(("dp", "fsdp"), None),
            P("dp", None),
            P(),
            P(),
        ),
        out_specs=(P(("dp", "fsdp"), None), P("dp", None, "fsdp"), P("dp", None, "fsdp")),
        check_vma=False,
    )
```

profile of v0, /device:TPU:1, one launch (start us, length us, event | category | flops | bytes accessed | tf_op | source)
XLA Modules:
  0.0 344.4 jit_solution(10557141637348160888)
XLA Ops:
  7.2 0.0 copy-start
  7.2 1.0 select_reduce_fusion
  8.3 2.8 gather_fusion
  11.1 0.9 select_select_fusion.1
  12.0 5.8 %all-to-all-start = ((bf16[8,64,512]{2,1,0:T(8,128)(2,1)}), bf16[8,64,512]{2,1,0:T(8,128)(2,1)S(1)}, u32[]{:S(2)}, u32[]{:S(2)}) async-start(bf16[8,64,512]{2,1,0:T(8,128)(2,1)} %select_select_fusion.1), calls=%async_computation | async-start | bytes 1048576 | tf_op jit(solution)/shard_map/all_to_all | solution.py:58
  17.8 0.0 all-gather.5.cloned.1.call-start
  17.8 0.2 dynamic-slice_reduce_fusion
  18.0 9.3 %all-to-all-done = bf16[8,64,512]{2,1,0:T(8,128)(2,1)S(1)} async-done(((bf16[8,64,512]{2,1,0:T(8,128)(2,1)}), bf16[8,64,512]{2,1,0:T(8,128)(2,1)S(1)}, u32[]{:S(2)}, u32[]{:S(2)}) %all-to-all-start) | async-done | bytes 524320 | tf_op jit(solution)/shard_map/all_to_all | solution.py:58
  27.3 0.6 gather_fusion.1
  27.8 0.8 broadcast_select_fusion
  28.6 0.0 all-gather.5.cloned.1.call-update
  28.7 1.8 gather_fusion.2
  30.5 0.1 select_select_fusion.3
  30.6 0.8 reshape.211
  31.4 4.1 %all-to-all-start.1 = ((bf16[8,2,2048]{2,1,0:T(2,128)(2,1)}), bf16[8,2,2048]{2,1,0:T(2,128)(2,1)S(1)}, u32[]{:S(2)}, u32[]{:S(2)}) async-start(bf16[8,2,2048]{2,1,0:T(2,128)(2,1)} %reshape.211), calls=%async_computation.1 | async-start | bytes 131072 | tf_op jit(solution)/shard_map/all_to_all | solution.py:59
  35.5 0.0 reduce-scatter.2.cloned.1.call-start
  35.5 0.7 dynamic-slice_bitcast_fusion
  36.2 0.1 broadcast_bitcast_fusion
  36.3 0.1 broadcast_bitcast_fusion.1
  36.4 4.0 %all-to-all-done.1 = bf16[8,2,2048]{2,1,0:T(2,128)(2,1)S(1)} async-done(((bf16[8,2,2048]{2,1,0:T(2,128)(2,1)}), bf16[8,2,2048]{2,1,0:T(2,128)(2,1)S(1)}, u32[]{:S(2)}, u32[]{:S(2)}) %all-to-all-start.1) | async-done | bytes 65568 | tf_op jit(solution)/shard_map/all_to_all | solution.py:59
  40.4 0.1 reshape.212
  40.5 0.6 gather_fusion.3
  41.1 0.1 broadcast_select_fusion.1
  41.1 0.1 copy.59
  41.3 22.7 %all_gather.11 = bf16[4,64,1024]{1,0,2:T(4,128)(2,1)S(1)} all-gather(bf16[4,64,64]{1,0,2:T(4,128)(2,1)S(1)} %copy.59), channel_id=1, replica_groups=mesh['dp'=8,'fsdp'=16] {'fsdp'}, dimensions={2}, use_global_device_ids=true | all-gather | bytes 557056 | tf_op jit(solution)/shard_map/all_gather | solution.py:66
  63.9 0.6 copy.60
  64.6 0.0 copy-done
  64.6 0.5 fusion.12
  65.1 22.3 %all-gather.5.cloned.1.call-done = bf16[4,64,8192]{2,1,0:T(8,128)(2,1)} async-done(((bf16[4,64,512]{2,1,0:T(8,128)(2,1)}), bf16[4,64,8192]{2,1,0:T(8,128)(2,1)}) %all-gather.5.cloned.1.call-update) | async-done | bytes 4194320 | tf_op jit(solution)/shard_map/all_gather | solution.py:65
  87.4 7.0 %fusion.9 = bf16[512,64]{0,1:T(8,128)(2,1)S(1)} fusion(bf16[4,64,8192]{2,1,0:T(8,128)(2,1)} %all-gather.5.cloned.1.call-done, bf16[512,8192]{1,0:T(8,128)(2,1)} %param.8, f32[512,4]{0,1:T(4,128)S(1)} %bitcast.92), kind=kOutput, calls=%fused_computation.17 | convolution fusion | flops 2147713024 | bytes 12656640 | tf_op jit(solution)/shard_map/td,krd->tkr/dot_general | solution.py:75
  94.5 0.5 convolution_bitcast_fusion.1
  95.0 0.3 copy.62
  95.3 9.1 %convolution_bitcast_fusion = f32[8192,256]{0,1:T(8,128)} fusion(bf16[512,256]{0,1:T(8,128)(2,1)S(1)} %bitcast.88, bf16[512,8192]{1,0:T(8,128)(2,1)} %param.8), kind=kOutput, calls=%fused_computation.6 | convolution fusion | flops 2147483648 | bytes 17039360 | tf_op jit(solution)/shard_map/dot_general | solution.py:98
  104.4 9.0 %copy.70 = f32[8192,256]{1,0:T(8,128)} copy(f32[8192,256]{0,1:T(8,128)} %convolution_bitcast_fusion) | data formatting | bytes 16777216 | tf_op jit(solution)/shard_map/reshape | solution.py:102
  113.4 7.8 %pad_maximum_fusion = f32[16,576,256]{2,1,0:T(8,128)} fusion(f32[16,64,256]{2,1,0:T(8,128)S(1)} %bitcast.86, f32[16,512,256]{2,1,0:T(8,128)} %bitcast.84), kind=kLoop, calls=%fused_computation.7 | loop fusion | flops 2359296 | bytes 18874368 | tf_op jit(solution)/shard_map/concatenate | solution.py:105
  121.3 0.0 reduce-scatter.2.cloned.1.call-update
  121.3 0.0 all-gather.3.cloned.1.call-start
  121.3 0.7 all-gather.3.cloned.1.call-update
  122.0 0.1 select_reduce_fusion.1
  122.1 0.1 fusion.26
  122.2 86.1 %reduce-scatter.2.cloned.1.call-done = f32[576,256]{1,0:T(8,128)} async-done(((f32[9216,256]{1,0:T(8,128)}), f32[576,256]{1,0:T(8,128)}) %reduce-scatter.2.cloned.1.call-update) | async-done | bytes 589840 | tf_op jit(solution)/shard_map/reduce_scatter | solution.py:104
  208.4 1.1 slice.20
  209.4 0.2 copy.64
  209.6 0.8 slice.21
  210.5 0.1 copy.66
  210.6 0.6 gather_fusion.4
  211.2 0.6 gather_fusion.5
  211.8 0.1 select_select_fusion.2
  211.9 0.8 reshape.213
  212.7 6.0 %all-to-all-start.3 = ((f32[8,1,4096]{2,1,0:T(1,128)}), f32[8,1,4096]{2,1,0:T(1,128)S(1)}, u32[]{:S(2)}, u32[]{:S(2)}) async-start(f32[8,1,4096]{2,1,0:T(1,128)} %reshape.213), calls=%async_computation.4 | async-start | bytes 262144 | tf_op jit(solution)/shard_map/all_to_all | solution.py:126
  218.7 1.2 select_select_fusion
  219.9 4.1 %all-to-all-done.3 = f32[8,1,4096]{2,1,0:T(1,128)S(1)} async-done(((f32[8,1,4096]{2,1,0:T(1,128)}), f32[8,1,4096]{2,1,0:T(1,128)S(1)}, u32[]{:S(2)}, u32[]{:S(2)}) %all-to-all-start.3) | async-done | bytes 131104 | tf_op jit(solution)/shard_map/all_to_all | solution.py:126
  224.0 4.3 %all-to-all-start.2 = ((f32[8,64,512]{2,1,0:T(8,128)}), f32[8,64,512]{2,1,0:T(8,128)S(1)}, u32[]{:S(2)}, u32[]{:S(2)}) async-start(f32[8,64,512]{2,1,0:T(8,128)} %select_select_fusion), calls=%async_computation.3 | async-start | bytes 2097152 | tf_op jit(solution)/shard_map/all_to_all | solution.py:125
  228.3 2.6 multiply_reduce_fusion
  231.0 0.5 broadcast.198
  231.5 1.0 reduce.3
  232.4 0.1 reshape.214
  232.5 1.1 fusion.16
  233.6 2.5 copy.69
  236.2 7.3 %all-to-all-done.2 = f32[8,64,512]{2,1,0:T(8,128)S(1)} async-done(((f32[8,64,512]{2,1,0:T(8,128)}), f32[8,64,512]{2,1,0:T(8,128)S(1)}, u32[]{:S(2)}, u32[]{:S(2)}) %all-to-all-start.2) | async-done | bytes 1048608 | tf_op jit(solution)/shard_map/all_to_all | solution.py:125
  243.4 3.6 %fusion.14 = f32[64,64,512]{2,0,1:T(8,128)S(1)} fusion(f32[8,64,512]{2,1,0:T(8,128)S(1)} %all-to-all-done.2, s32[8]{0:T(128)S(1)} %fusion.25, pred[8]{0:T(512)(128)(4,1)S(1)} %get-tuple-element.21), kind=kOutput, calls=%fused_computation.20 | convolution fusion | flops 201327616 | bytes 9437224 | tf_op jit(solution)/shard_map/sc,srd->crd/dot_general | solution.py:132
  247.0 8.5 %copy.68 = f32[64,64,512]{2,1,0:T(8,128)} copy(f32[64,64,512]{2,0,1:T(8,128)S(1)} %fusion.14) | data formatting | bytes 16777216
  255.5 66.7 %all-gather.3.cloned.1.call-done = bf16[8192,1024]{1,0:T(8,128)(2,1)} async-done(((bf16[512,1024]{1,0:T(8,128)(2,1)}), bf16[8192,1024]{1,0:T(8,128)(2,1)}) %all-gather.3.cloned.1.call-update) | async-done | bytes 16777232 | tf_op jit(solution)/shard_map/all_gather | solution.py:36
  322.3 15.6 %add_convert_fusion = bf16[512,1024]{1,0:T(8,128)(2,1)} fusion(f32[512,1024]{1,0:T(8,128)S(1)} %copy-done.2, bf16[512,8192]{1,0:T(8,128)(2,1)} %param.8, bf16[8192,1024]{1,0:T(8,128)(2,1)} %all-gather.3.cloned.1.call-done), kind=kOutput, calls=%fused_computation.11 | convolution fusion | flops 8591507456 | bytes 28311552 | tf_op jit(solution)/shard_map/dot_general | solution.py:34
  (21 shorter events, 0.2 us)
Async XLA Ops:
  7.2 57.4 %copy-start = (bf16[512,1024]{1,0:T(8,128)(2,1)S(1)}, bf16[512,1024]{1,0:T(8,128)(2,1)}, u32[]{:S(2)}) copy-start(bf16[512,1024]{1,0:T(8,128)(2,1)} %param.12) | copy-start | bytes 3145732
  12.0 15.3 %all-to-all-start = ((bf16[8,64,512]{2,1,0:T(8,128)(2,1)}), bf16[8,64,512]{2,1,0:T(8,128)(2,1)S(1)}, u32[]{:S(2)}, u32[]{:S(2)}) async-start(bf16[8,64,512]{2,1,0:T(8,128)(2,1)} %select_select_fusion.1), calls=%async_computation | async-start | bytes 1048576 | tf_op jit(solution)/shard_map/all_to_all | solution.py:58
  17.8 69.6 %all-gather.5.cloned.1.call-start = ((), (), s32[]{:S(2)}) async-start(), calls=%async_computation.6 | async-start | bytes 4456448 | tf_op jit(solution)/shard_map/all_gather | solution.py:65
  31.4 9.0 %all-to-all-start.1 = ((bf16[8,2,2048]{2,1,0:T(2,128)(2,1)}), bf16[8,2,2048]{2,1,0:T(2,128)(2,1)S(1)}, u32[]{:S(2)}, u32[]{:S(2)}) async-start(bf16[8,2,2048]{2,1,0:T(2,128)(2,1)} %reshape.211), calls=%async_computation.1 | async-start | bytes 131072 | tf_op jit(solution)/shard_map/all_to_all | solution.py:59
  35.5 172.9 %reduce-scatter.2.cloned.1.call-start = ((), (), s32[]{:S(2)}) async-start(), calls=%async_computation.7 | async-start | bytes 10027008 | tf_op jit(solution)/shard_map/reduce_scatter | solution.py:104
  121.3 201.0 %all-gather.3.cloned.1.call-start = ((), (), s32[]{:S(2)}) async-start(), calls=%async_computation.5 | async-start | bytes 17825792 | tf_op jit(solution)/shard_map/all_gather | solution.py:36
  212.7 11.3 %all-to-all-start.3 = ((f32[8,1,4096]{2,1,0:T(1,128)}), f32[8,1,4096]{2,1,0:T(1,128)S(1)}, u32[]{:S(2)}, u32[]{:S(2)}) async-start(f32[8,1,4096]{2,1,0:T(1,128)} %reshape.213), calls=%async_computation.4 | async-start | bytes 262144 | tf_op jit(solution)/shard_map/all_to_all | solution.py:126
  224.0 19.4 %all-to-all-start.2 = ((f32[8,64,512]{2,1,0:T(8,128)}), f32[8,64,512]{2,1,0:T(8,128)S(1)}, u32[]{:S(2)}, u32[]{:S(2)}) async-start(f32[8,64,512]{2,1,0:T(8,128)} %select_select_fusion), calls=%async_computation.3 | async-start | bytes 2097152 | tf_op jit(solution)/shard_map/all_to_all | solution.py:125
  247.0 75.2 %copy-start.2 = (f32[512,1024]{1,0:T(8,128)S(1)}, f32[512,1024]{1,0:T(8,128)}, u32[]{:S(2)}) copy-start(f32[512,1024]{1,0:T(8,128)} %multiply_reduce_fusion) | copy-start | bytes 6291460
  322.3 15.7 %copy-start.1 = (bf16[512,1024]{1,0:T(8,128)(2,1)S(1)}, bf16[512,1024]{1,0:T(8,128)(2,1)}, u32[]{:S(2)}) copy-start(bf16[512,1024]{1,0:T(8,128)(2,1)} %param.12) | copy-start | bytes 3145732
Sparse Core Ops, SparseCore 0:
  28.8 58.5 all-gather.4
  121.4 86.9 reduce-scatter.1
  210.7 111.4 all-gather.2
where the time goes:
time: 345 us; the launch traced here: 344 us
  waiting for transfers between devices  200 us (58%)
  matrix products  40 us (12%)
  local copies, waits for them, and re-layouts  33.6 us (10%)
  blocking collectives  22.7 us (7%)
  starting transfers between devices  20.3 us (6%)
  between operations  14 us (4%)
  other arithmetic  13.4 us (4%)
    reduce_scatter x1, waiting for transfers between devices, body(): lax.psum_scatter(jnp.concatenate([down_part, up_part], axis=1).reshape(la...  86.1 us
    all_gather x1, waiting for transfers between devices, body(): lax.all_gather(frozen_value_matrix, 'fsdp', axis=0, tiled=True)  66.7 us
    all_gather x1, blocking collectives, body(): lax.all_gather(slab_up, 'fsdp', axis=2, tiled=True)  22.7 us
    all_gather x1, waiting for transfers between devices, body(): lax.all_gather(slab_down, 'fsdp', axis=2, tiled=True)  22.3 us
    dot_general x1, matrix products, body(): jnp.dot(tokens, lax.all_gather(frozen_value_matrix, 'fsdp', axis=0, tiled...  15.6 us
    unnamed x16, local copies, waits for them, and re-layouts  13.1 us
    all_to_all x1, waiting for transfers between devices, body(): lax.all_to_all(send_down, 'dp', split_axis=0, concat_axis=0, tiled=True)  9.26 us
    dot_general x1, matrix products, body(): lax.dot_general(tokens, masked_back, contract, preferred_element_type=jnp...  9.13 us
  transfers between devices with their start and end apart: 7, of which 7 were waited for; matrix products, arithmetic and copies ran while one was open for 9% of the time, Pallas kernels for 0%

commit v1 on v0

v1 whole, which is shorter than its diff:
```python
import jax
import jax.numpy as jnp
from jax import lax
from jax.sharding import PartitionSpec as P

WIN = 128


ADAPTER_SCALE = 2.0


def body(
    tokens,
    frozen_value_matrix,
    adapter_down_maps,
    adapter_up_maps,
    value_output_gradient,
    window_composer_position,
    needed_composers,
    composer_storage_index,
):
    f32, bf16 = jnp.float32, jnp.bfloat16
    dp_count = lax.axis_size("dp")
    fsdp_count = lax.axis_size("fsdp")
    group_index = lax.axis_index("dp")
    member_index = lax.axis_index("fsdp")
    tok_rows, width = tokens.shape
    value_cols = frozen_value_matrix.shape[1]
    rank = adapter_down_maps.shape[1]
    each_owner_rows = adapter_down_maps.shape[0]
    down_cols = adapter_down_maps.shape[2]
    up_cols = adapter_up_maps.shape[2]
    list_len = needed_composers.shape[1]
    windows = tok_rows // WIN

    core = group_index % 2
    half = value_cols // 2
    w_mine = lax.dynamic_slice_in_dim(frozen_value_matrix, core * half, half, axis=1)
    w_mine_full = lax.all_gather(w_mine, "fsdp", axis=0, tiled=True)
    w_other_full = lax.ppermute(w_mine_full, "dp", [(i, i ^ 1) for i in range(dp_count)])
    out_mine = jnp.dot(tokens, w_mine_full, preferred_element_type=f32)
    out_other = jnp.dot(tokens, w_other_full, preferred_element_type=f32)
    frozen_rows = jnp.where(
        core == 0,
        jnp.concatenate([out_mine, out_other], axis=1),
        jnp.concatenate([out_other, out_mine], axis=1),
    )

    list_slot = jnp.take(composer_storage_index, needed_composers, axis=0)
    list_owner = list_slot // each_owner_rows
    list_local = list_slot % each_owner_rows
    owned_here = list_owner == group_index
    locally_owned_slots = jnp.sum(jnp.where(owned_here, list_local, 0), axis=1)
    owned_any = jnp.any(owned_here, axis=1)
    send = jnp.concatenate(
        [
            jnp.take(adapter_down_maps, locally_owned_slots, axis=0),
            jnp.take(adapter_up_maps, locally_owned_slots, axis=0),
        ],
        axis=2,
    )
    send = jnp.where(owned_any[:, None, None], send, jnp.zeros((), send.dtype))
    got = lax.all_to_all(send, "dp", split_axis=0, concat_axis=0, tiled=True)
    my_owner = lax.dynamic_index_in_dim(list_owner, group_index, 0, keepdims=False)
    slab = jnp.take(got, my_owner, axis=0)
    shares = lax.all_gather(slab, "fsdp", axis=0, tiled=False)
    full_down = shares[..., :down_cols].transpose(1, 2, 0, 3).reshape(list_len, rank, width)
    full_up = shares[..., down_cols:].transpose(1, 2, 0, 3).reshape(list_len, rank, value_cols)

    group_picks = window_composer_position[0]
    my_picks = lax.dynamic_slice_in_dim(group_picks, member_index * windows, windows, 0)
    slot_range = jnp.arange(list_len, dtype=jnp.int32)
    token_hot = jnp.broadcast_to(
        my_picks[:, None, None] == slot_range[None, None, :], (windows, WIN, list_len)
    ).reshape(tok_rows, list_len)
    hot_f = token_hot.astype(f32)

    down_flat = full_down.reshape(list_len * rank, width)
    up_flat = full_up.reshape(list_len * rank, value_cols)
    low_all = lax.dot_general(
        tokens, down_flat, (((1,), (1,)), ((), ())), preferred_element_type=f32
    ).reshape(tok_rows, list_len, rank)
    low = jnp.sum(low_all * hot_f[:, :, None], axis=1).astype(bf16)
    hot_h = token_hot.astype(bf16)
    masked_low = (hot_h[:, :, None] * low[:, None, :]).reshape(tok_rows, list_len * rank)
    adapter_change = jnp.dot(masked_low, up_flat, preferred_element_type=f32)
    value = (frozen_rows + ADAPTER_SCALE * adapter_change).astype(bf16)

    back_all = lax.dot_general(
        value_output_gradient, up_flat, (((1,), (1,)), ((), ())), preferred_element_type=f32
    ).reshape(tok_rows, list_len, rank)
    back = (ADAPTER_SCALE * jnp.sum(back_all * hot_f[:, :, None], axis=1)).astype(bf16)
    masked_back = (hot_h[:, :, None] * back[:, None, :]).reshape(tok_rows, list_len * rank)
    scaled_masked_low = masked_low * jnp.asarray(ADAPTER_SCALE, bf16)

    contract = (((0,), (0,)), ((), ()))
    part_down = lax.dot_general(masked_back, tokens, contract, preferred_element_type=f32)
    part_up = lax.dot_general(
        scaled_masked_low, value_output_gradient, contract, preferred_element_type=f32
    )
    rows = list_len * rank
    part_down = part_down.reshape(rows, fsdp_count, down_cols).transpose(1, 0, 2)
    part_up = part_up.reshape(rows, fsdp_count, up_cols).transpose(1, 0, 2)
    summed = lax.psum_scatter(
        jnp.concatenate([part_down, part_up], axis=2), "fsdp", scatter_dimension=0, tiled=True
    )[0]

    owner_range = jnp.arange(dp_count, dtype=jnp.int32)
    to_owner = my_owner[None, :] == owner_range[:, None]
    pick_index = jnp.sum(jnp.where(to_owner, slot_range[None, :], 0), axis=1)
    owner_has = jnp.any(to_owner, axis=1)
    send_grad = jnp.take(summed.reshape(list_len, rank, down_cols + up_cols), pick_index, axis=0)
    send_grad = jnp.where(owner_has[:, None, None], send_grad, 0.0)
    back_grad = lax.all_to_all(send_grad, "dp", split_axis=0, concat_axis=0, tiled=True)
    local_range = jnp.arange(each_owner_rows, dtype=jnp.int32)
    arrivals = owned_any[:, None] & (locally_owned_slots[:, None] == local_range[None, :])
    arrive_f = arrivals.astype(f32)
    grad_down = jnp.sum(
        arrive_f[:, :, None, None] * back_grad[:, None, :, :down_cols], axis=0
    )
    grad_up = jnp.sum(arrive_f[:, :, None, None] * back_grad[:, None, :, down_cols:], axis=0)
    return (value, grad_down, grad_up)


def solution(mesh):
    return jax.shard_map(
        body,
        mesh=mesh,
        in_specs=(
            P(("dp", "fsdp"), None),
            P("fsdp", None),
            P("dp", None, "fsdp"),
            P("dp", None, "fsdp"),
            P(("dp", "fsdp"), None),
            P("dp", None),
            P(),
            P(),
        ),
        out_specs=(P(("dp", "fsdp"), None), P("dp", None, "fsdp"), P("dp", None, "fsdp")),
        check_vma=False,
    )
```

time: 345 us -> 314 us (0.910)
  waiting for transfers between devices: 200 us -> 176 us
  blocking collectives: 22.7 us -> 0 us
  other arithmetic: 13.4 us -> 34.1 us
  local copies, waits for them, and re-layouts: 33.6 us -> 48.7 us
  matrix products: 40 us -> 27.6 us
  starting transfers between devices: 20.3 us -> 12.5 us
    reduce_scatter x1 -> x0, waiting for transfers between devices: 86.1 us -> none  [body(): lax.psum_scatter(jnp.concatenate([down_part, up_part], axis=1).reshape(la...]
    unnamed x3 -> x4, waiting for transfers between devices: 0.71 us -> 77.7 us
    reduce_sum x1 -> x3, other arithmetic: 1 us -> 24.9 us  [the longest x1 21.7 us: body(): jnp.sum(arrive_f[:, :, None, None] * back_grad[:, None, :, :down_cols], a...]
    all_gather x1 -> x0, blocking collectives: 22.7 us -> none  [body(): lax.all_gather(slab_up, 'fsdp', axis=2, tiled=True)]
    dot_general x8 -> x7, matrix products: 40 us -> 27.6 us  [the longest x1 11.3 us: body(): out_mine = jnp.dot(tokens, w_mine_full, preferred_element_type=f32)]
    dot_general x1, local copies, waits for them, and re-layouts: 0.33 us -> 11.9 us  [body(): lax.dot_general(masked_back, tokens, contract, preferred_element_type=f32)]
    concatenate x0 -> x1, local copies, waits for them, and re-layouts: none -> 10.9 us  [body(): jnp.concatenate([part_down, part_up], axis=2)]
    reshape x1 -> x0, local copies, waits for them, and re-layouts: 9 us -> none  [body(): down_part.reshape(shards, down_cols, list_len * adapter_rank_width)]
  transfers between devices with their start and end apart: 7 -> 6, of which waited for: 7 -> 5; matrix products, arithmetic and copies ran while one was open for 9% -> 24% of each run, Pallas kernels for 0% -> 0%
where the time goes in v1:
time: 314 us; the launch traced here: 313 us
  waiting for transfers between devices  176 us (56%)
  local copies, waits for them, and re-layouts  48.7 us (16%)
  other arithmetic  34.1 us (11%)
  matrix products  27.6 us (9%)
  between operations  14.1 us (4%)
  starting transfers between devices  12.5 us (4%)
    unnamed x4, waiting for transfers between devices  77.7 us
    all_gather x1, waiting for transfers between devices, body(): shares = lax.all_gather(slab, 'fsdp', axis=0, tiled=False)  42.8 us
    all_gather x1, waiting for transfers between devices, body(): w_mine_full = lax.all_gather(w_mine, 'fsdp', axis=0, tiled=True)  38 us
    reduce_sum x1, other arithmetic, body(): jnp.sum(arrive_f[:, :, None, None] * back_grad[:, None, :, :down_cols], a...  21.7 us
    dot_general x1, local copies, waits for them, and re-layouts, body(): lax.dot_general(masked_back, tokens, contract, preferred_element_type=f32)  11.9 us
    dot_general x1, matrix products, body(): out_mine = jnp.dot(tokens, w_mine_full, preferred_element_type=f32)  11.3 us
    concatenate x1, local copies, waits for them, and re-layouts, body(): jnp.concatenate([part_down, part_up], axis=2)  10.9 us
    all_to_all x1, waiting for transfers between devices, body(): got = lax.all_to_all(send, 'dp', split_axis=0, concat_axis=0, tiled=True)  10.9 us
  transfers between devices with their start and end apart: 6, of which 5 were waited for; matrix products, arithmetic and copies ran while one was open for 24% of the time, Pallas kernels for 0%

profile of v1, /device:TPU:1, one launch (start us, length us, event | category | flops | bytes accessed | tf_op | source)
XLA Modules:
  0.0 312.9 jit_solution(977351093186361105)
XLA Ops:
  7.2 0.0 copy-start
  7.2 0.8 copy.59
  8.0 0.1 reshape.226
  8.1 1.4 gather_fusion
  9.5 0.1 reshape.225
  9.6 0.1 fusion.17
  9.7 0.1 fusion.3
  9.9 0.1 select_reduce_fusion
  10.0 1.8 gather_fusion.2
  11.8 2.8 gather_fusion.1
  14.6 0.1 broadcast_select_fusion.1
  14.7 0.1 broadcast_select_fusion
  14.8 1.1 maximum_select_fusion.1
  15.9 5.8 %all-to-all-start = ((bf16[8,64,576]{2,1,0:T(8,128)(2,1)}), bf16[8,64,576]{2,1,0:T(8,128)(2,1)S(1)}, u32[]{:S(2)}, u32[]{:S(2)}) async-start(bf16[8,64,576]{2,1,0:T(8,128)(2,1)} %maximum_select_fusion.1), calls=%async_computation | async-start | bytes 1310720 | tf_op jit(solution)/shard_map/all_to_all | solution.py:63
  21.7 10.9 %all-to-all-done = bf16[8,64,576]{2,1,0:T(8,128)(2,1)S(1)} async-done(((bf16[8,64,576]{2,1,0:T(8,128)(2,1)}), bf16[8,64,576]{2,1,0:T(8,128)(2,1)S(1)}, u32[]{:S(2)}, u32[]{:S(2)}) %all-to-all-start) | async-done | bytes 589856 | tf_op jit(solution)/shard_map/all_to_all | solution.py:63
  32.6 0.6 gather_fusion.3
  33.2 0.8 bitcast_select_fusion
  34.0 0.0 all-gather.5.cloned.1.call-update
  34.1 0.0 all-gather.3.cloned.1.call-start
  34.1 0.8 constant_dynamic-slice_fusion.2
  35.0 0.0 all-gather.3.cloned.1.call-update
  35.0 0.0 reduce-scatter.4.cloned.1.call-start
  35.1 0.1 fusion.11
  35.1 0.1 broadcast_bitcast_fusion
  35.2 0.1 broadcast_bitcast_fusion.1
  35.3 1.3 copy.66
  36.6 11.9 %copy.75 = bf16[8192,512]{1,0:T(8,128)(2,1)} copy(bf16[8192,512]{0,1:T(8,128)(2,1)} %bitcast.88) | data formatting | bytes 16777216 | tf_op jit(solution)/shard_map/dot_general | solution.py:97
  48.6 42.8 %all-gather.5.cloned.1.call-done = bf16[16,4,64,576]{3,2,1,0:T(8,128)(2,1)} async-done(((bf16[1,4,64,576]{3,2,1,0:T(8,128)(2,1)}), bf16[16,4,64,576]{3,2,1,0:T(8,128)(2,1)}) %all-gather.5.cloned.1.call-update) | async-done | bytes 4718608 | tf_op jit(solution)/shard_map/all_gather | solution.py:66
  91.4 1.3 slice_bitcast_fusion.1
  92.7 0.7 copy.63
  93.4 0.7 reshape_reshape.7
  94.1 2.7 slice_bitcast_fusion
  96.8 0.0 slice-start.2
  96.8 2.4 copy.62
  99.3 0.0 slice-start.3
  99.3 4.4 %copy.78 = bf16[32,8,16,512]{3,1,2,0:T(8,128)(2,1)S(1)} copy(bf16[32,8,16,512]{3,2,1,0:T(8,128)(2,1)S(1)} %bitcast.87) | data formatting | bytes 8388608
  103.7 0.5 fusion.19
  104.2 0.0 slice-start.1
  104.2 2.4 fusion.18
  106.6 0.1 multiply_reduce_fusion.2
  106.7 0.1 broadcast_multiply_fusion
  106.8 0.9 convolution_bitcast_fusion.1
  107.8 0.3 slice-done.1
  108.1 2.4 convolution_bitcast_fusion
  110.5 5.2 %pad_maximum_fusion = f32[16,256,576]{2,1,0:T(8,128)} fusion(f32[16,256,64]{2,1,0:T(8,128)S(1)} %convolution_bitcast_fusion.1, f32[16,256,512]{2,1,0:T(8,128)S(1)} %convolution_bitcast_fusion), kind=kLoop, calls=%fused_computation.7 | loop fusion | flops 2359296 | bytes 18874368 | tf_op jit(solution)/shard_map/concatenate | solution.py:105
  115.7 10.9 %copy.69 = f32[16,256,576]{1,2,0:T(8,128)} copy(f32[16,256,576]{2,1,0:T(8,128)} %pad_maximum_fusion) | data formatting | bytes 18874368 | tf_op jit(solution)/shard_map/concatenate | solution.py:105
  126.6 0.0 reduce-scatter.4.cloned.1.call-update
  126.6 38.0 %all-gather.3.cloned.1.call-done = bf16[8192,512]{1,0:T(8,128)(2,1)} async-done(((bf16[512,512]{1,0:T(8,128)(2,1)}), bf16[8192,512]{1,0:T(8,128)(2,1)}) %all-gather.3.cloned.1.call-update) | async-done | bytes 8388624 | tf_op jit(solution)/shard_map/all_gather | solution.py:39
  164.6 0.7 collective-permute-start
  165.3 0.1 fusion.4
  165.4 0.1 fusion.7
  165.5 11.3 %convolution_bitcast_fusion.3 = f32[512,512]{0,1:T(8,128)} fusion(bf16[8192,512]{1,0:T(8,128)(2,1)} %all-gather.3.cloned.1.call-done, bf16[512,8192]{1,0:T(8,128)(2,1)} %param.8), kind=kOutput, calls=%fused_computation.15 | convolution fusion | flops 4294967296 | bytes 17825792 | tf_op jit(solution)/shard_map/dot_general | solution.py:41
  176.8 77.6 %reduce-scatter.4.cloned.1.call-done = f32[1,256,576]{1,2,0:T(8,128)} async-done(((f32[16,256,576]{1,2,0:T(8,128)}), f32[1,256,576]{1,2,0:T(8,128)}) %reduce-scatter.4.cloned.1.call-update) | async-done | bytes 589840
  254.4 1.3 copy.70
  255.7 0.6 gather_fusion.4
  256.4 1.2 select_select_fusion
  257.6 6.0 %all-to-all-start.1 = ((f32[8,64,576]{2,1,0:T(8,128)}), f32[8,64,576]{2,1,0:T(8,128)S(1)}, u32[]{:S(2)}, u32[]{:S(2)}) async-start(f32[8,64,576]{2,1,0:T(8,128)} %select_select_fusion), calls=%async_computation.1 | async-start | bytes 2621440 | tf_op jit(solution)/shard_map/all_to_all | solution.py:114
  263.6 9.6 %convolution_bitcast_fusion.2 = f32[512,512]{0,1:T(8,128)S(1)} fusion(bf16[8192,512]{1,0:T(8,128)(2,1)} %collective-permute-done, bf16[512,8192]{1,0:T(8,128)(2,1)} %param.8), kind=kOutput, calls=%fused_computation.14 | convolution fusion | flops 4294967296 | bytes 17825792 | tf_op jit(solution)/shard_map/dot_general | solution.py:42
  273.2 0.5 fusion.1
  273.7 1.3 copy.71
  275.1 6.4 %all-to-all-done.1 = f32[8,64,576]{2,1,0:T(8,128)S(1)} async-done(((f32[8,64,576]{2,1,0:T(8,128)}), f32[8,64,576]{2,1,0:T(8,128)S(1)}, u32[]{:S(2)}, u32[]{:S(2)}) %all-to-all-start.1) | async-done | bytes 1179680 | tf_op jit(solution)/shard_map/all_to_all | solution.py:114
  281.5 0.1 slice.28
  281.6 21.7 %multiply_reduce_fusion = f32[64,64,512]{2,1,0:T(8,128)} fusion(f32[8,64,512]{2,1,0:T(8,128)S(1)} %slice.28, f32[8,64]{1,0:T(8,128)S(1)} %fusion.7), kind=kLoop, calls=%fused_computation.5 | loop fusion | flops 31457280 | bytes 9439232 | tf_op jit(solution)/shard_map/reduce_sum | solution.py:118
  303.4 3.0 multiply_reduce_fusion.1
  (36 shorter events, 0.2 us)
Async XLA Ops:
  7.2 27.0 %copy-start = (bf16[512,1024]{1,0:T(8,128)(2,1)S(1)}, bf16[512,1024]{1,0:T(8,128)(2,1)}, u32[]{:S(2)}) copy-start(bf16[512,1024]{1,0:T(8,128)(2,1)} %param.9) | copy-start | bytes 3145732
  9.5 25.5 %copy-start.5 = (s32[1,64]{1,0:T(1,128)S(1)}, s32[1,64]{1,0:T(1,128)}, u32[]{:S(2)}) copy-start(s32[1,64]{1,0:T(1,128)} %param.13) | copy-start | bytes 772
  9.5 25.8 %copy-start.2 = (bf16[512,1024]{1,0:T(8,128)(2,1)S(1)}, bf16[512,1024]{1,0:T(8,128)(2,1)}, u32[]{:S(2)}) copy-start(bf16[512,1024]{1,0:T(8,128)(2,1)} %param.12) | copy-start | bytes 3145732
  15.9 16.7 %all-to-all-start = ((bf16[8,64,576]{2,1,0:T(8,128)(2,1)}), bf16[8,64,576]{2,1,0:T(8,128)(2,1)S(1)}, u32[]{:S(2)}, u32[]{:S(2)}) async-start(bf16[8,64,576]{2,1,0:T(8,128)(2,1)} %maximum_select_fusion.1), calls=%async_computation | async-start | bytes 1310720 | tf_op jit(solution)/shard_map/all_to_all | solution.py:63
  21.7 69.7 %all-gather.5.cloned.1.call-start = ((), (), s32[]{:S(2)}) async-start(), calls=%async_computation.4 | async-start | bytes 5570560 | tf_op jit(solution)/shard_map/all_gather | solution.py:66
  34.1 130.5 %all-gather.3.cloned.1.call-start = ((), (), s32[]{:S(2)}) async-start(), calls=%async_computation.3 | async-start | bytes 8912896 | tf_op jit(solution)/shard_map/all_gather | solution.py:39
  35.0 219.4 %reduce-scatter.4.cloned.1.call-start = ((), (), s32[]{:S(2)}) async-start(), calls=%async_computation.5 | async-start | bytes 10027008
  96.8 7.4 %slice-start.2 = ((s8[8388608]{0:T(1024)(128)(4,1)}), s8[4194304]{0:T(1024)(128)(4,1)S(1)}, s32[]{:S(2)}) async-start(s8[8388608]{0:T(1024)(128)(4,1)} %bitcast.89), calls=%async_computation.8 | async-start | bytes 8388608
  99.3 4.4 %copy-start.3 = (bf16[512,1024]{1,0:T(8,128)(2,1)S(1)}, bf16[512,1024]{1,0:T(8,128)(2,1)}, u32[]{:S(2)}) copy-start(bf16[512,1024]{1,0:T(8,128)(2,1)} %param.12) | copy-start | bytes 3145732
  99.3 4.9 %slice-start.3 = ((s8[8388608]{0:T(1024)(128)(4,1)}), s8[4194304]{0:T(1024)(128)(4,1)S(1)}, s32[]{:S(2)}) async-start(s8[8388608]{0:T(1024)(128)(4,1)} %bitcast.89), calls=%async_computation.9 | async-start | bytes 8388608
  104.2 3.6 %slice-start = ((s8[8388608]{0:T(1024)(128)(4,1)}), s8[4194304]{0:T(1024)(128)(4,1)S(1)}, s32[]{:S(2)}) async-start(s8[8388608]{0:T(1024)(128)(4,1)} %bitcast.84), calls=%async_computation.6 | async-start | bytes 8388608
  104.2 2.6 copy-start.4
  104.2 3.9 %slice-start.1 = ((s8[8388608]{0:T(1024)(128)(4,1)}), s8[4194304]{0:T(1024)(128)(4,1)S(1)}, s32[]{:S(2)}) async-start(s8[8388608]{0:T(1024)(128)(4,1)} %bitcast.84), calls=%async_computation.7 | async-start | bytes 8388608
  164.6 99.0 %collective-permute-start = (bf16[8192,512]{1,0:T(8,128)(2,1)}, bf16[8192,512]{1,0:T(8,128)(2,1)}, u32[]{:S(2)}, u32[]{:S(2)}) collective-permute-start(bf16[8192,512]{1,0:T(8,128)(2,1)} %all-gather.3.cloned.1.call-done), channel_id=1, source_target_pairs={{0,16},{16,0},{32,48},{48,32},{64,80},{80,64},{96,112},{112,96},{1... | collective-permute-start | bytes 25165832 | tf_op jit(solution)/shard_map/ppermute | solution.py:40
  257.6 23.9 %all-to-all-start.1 = ((f32[8,64,576]{2,1,0:T(8,128)}), f32[8,64,576]{2,1,0:T(8,128)S(1)}, u32[]{:S(2)}, u32[]{:S(2)}) async-start(f32[8,64,576]{2,1,0:T(8,128)} %select_select_fusion), calls=%async_computation.1 | async-start | bytes 2621440 | tf_op jit(solution)/shard_map/all_to_all | solution.py:114
  263.6 9.6 %copy-start.6 = (f32[512,512]{0,1:T(8,128)S(1)}, f32[512,512]{0,1:T(8,128)}, u32[]{:S(2)}) copy-start(f32[512,512]{0,1:T(8,128)} %convolution_bitcast_fusion.3) | copy-start | bytes 3145732
  281.5 24.9 %copy-start.1 = (bf16[512,1024]{1,0:T(8,128)(2,1)S(1)}, bf16[512,1024]{1,0:T(8,128)(2,1)}, u32[]{:S(2)}) copy-start(bf16[512,1024]{1,0:T(8,128)(2,1)} %param.9) | copy-start | bytes 3145732
Sparse Core Ops, SparseCore 0:
  34.2 57.1 all-gather.4
  94.1 70.4 all-gather.2
  168.1 86.2 reduce-scatter.3

commit v2 on v1

--- a/solution.py
+++ b/solution.py
@@ -33,18 +33,32 @@
     list_len = needed_composers.shape[1]
     windows = tok_rows // WIN
 
-    core = group_index % 2
-    half = value_cols // 2
-    w_mine = lax.dynamic_slice_in_dim(frozen_value_matrix, core * half, half, axis=1)
-    w_mine_full = lax.all_gather(w_mine, "fsdp", axis=0, tiled=True)
-    w_other_full = lax.ppermute(w_mine_full, "dp", [(i, i ^ 1) for i in range(dp_count)])
-    out_mine = jnp.dot(tokens, w_mine_full, preferred_element_type=f32)
-    out_other = jnp.dot(tokens, w_other_full, preferred_element_type=f32)
-    frozen_rows = jnp.where(
-        core == 0,
-        jnp.concatenate([out_mine, out_other], axis=1),
-        jnp.concatenate([out_other, out_mine], axis=1),
+    part_cols = value_cols // dp_count
+    w_part = lax.dynamic_slice_in_dim(
+        frozen_value_matrix, group_index * part_cols, part_cols, axis=1
     )
+    w_part_full = lax.all_gather(w_part, "fsdp", axis=0, tiled=True)
+    same_parity = [w_part_full]
+    for step in range(1, dp_count // 2):
+        same_parity.append(
+            lax.ppermute(
+                w_part_full, "dp", [(i, (i + 2 * step) % dp_count) for i in range(dp_count)]
+            )
+        )
+    w_own = jnp.concatenate(same_parity, axis=1)
+    w_partner = lax.ppermute(w_own, "dp", [(i, i ^ 1) for i in range(dp_count)])
+    out_own = jnp.dot(tokens, w_own, preferred_element_type=f32)
+    out_partner = jnp.dot(tokens, w_partner, preferred_element_type=f32)
+    held = jnp.concatenate([out_own, out_partner], axis=1).reshape(tok_rows, dp_count, part_cols)
+    part_ids = jnp.arange(dp_count, dtype=jnp.int32)
+    partner_index = group_index ^ 1
+    same = (part_ids % 2) == (group_index % 2)
+    where_held = jnp.where(
+        same,
+        ((group_index - part_ids) % dp_count) // 2,
+        dp_count // 2 + ((partner_index - part_ids) % dp_count) // 2,
+    )
+    frozen_rows = jnp.take(held, where_held, axis=1).reshape(tok_rows, value_cols)
 
     list_slot = jnp.take(composer_storage_index, needed_composers, axis=0)
     list_owner = list_slot // each_owner_rows
@@ -112,13 +126,14 @@
     send_grad = jnp.take(summed.reshape(list_len, rank, down_cols + up_cols), pick_index, axis=0)
     send_grad = jnp.where(owner_has[:, None, None], send_grad, 0.0)
     back_grad = lax.all_to_all(send_grad, "dp", split_axis=0, concat_axis=0, tiled=True)
-    local_range = jnp.arange(each_owner_rows, dtype=jnp.int32)
-    arrivals = owned_any[:, None] & (locally_owned_slots[:, None] == local_range[None, :])
-    arrive_f = arrivals.astype(f32)
-    grad_down = jnp.sum(
-        arrive_f[:, :, None, None] * back_grad[:, None, :, :down_cols], axis=0
+    land = jnp.where(owned_any, locally_owned_slots, 0)
+    arrived = jnp.where(owned_any[:, None, None], back_grad, 0.0)
+    grad_down = jnp.zeros((each_owner_rows, rank, down_cols), f32).at[land].add(
+        arrived[:, :, :down_cols]
     )
-    grad_up = jnp.sum(arrive_f[:, :, None, None] * back_grad[:, None, :, down_cols:], axis=0)
+    grad_up = jnp.zeros((each_owner_rows, rank, up_cols), f32).at[land].add(
+        arrived[:, :, down_cols:]
+    )
     return (value, grad_down, grad_up)
 
 

time: 314 us -> 292 us (0.930)
  waiting for transfers between devices: 176 us -> 151 us
  other arithmetic: 34.1 us -> 15.1 us
  local copies, waits for them, and re-layouts: 48.7 us -> 64.7 us
  starting transfers between devices: 12.5 us -> 17.7 us
    ppermute x1 -> x4, waiting for transfers between devices: 0.01 us -> 83.4 us  [the longest x3 83.4 us: body(): lax.ppermute(w_part_full, 'dp', [(i, (i + 2 * step) % dp_count) for i in...]
    unnamed x4, waiting for transfers between devices: 77.7 us -> 0.05 us
    all_gather x1, waiting for transfers between devices: 38 us -> 10.8 us  [body(): w_part_full = lax.all_gather(w_part, 'fsdp', axis=0, tiled=True)]
    reduce_sum x2 -> x0, other arithmetic: 24.8 us -> none  [the longest x1 21.7 us: body(): jnp.sum(arrive_f[:, :, None, None] * back_grad[:, None, :, :down_cols], a...]
    ppermute x1 -> x4, starting transfers between devices: 0.67 us -> 7.42 us  [the longest x3 4.77 us: body(): lax.ppermute(w_part_full, 'dp', [(i, (i + 2 * step) % dp_count) for i in...]
    unnamed x30 -> x38, local copies, waits for them, and re-layouts: 8.41 us -> 14.2 us
    broadcast_in_dim x0 -> x3, local copies, waits for them, and re-layouts: none -> 4.78 us  [the longest x1 4.47 us: body(): jnp.zeros((each_owner_rows, rank, down_cols), f32).at[land]]
    scatter-add x0 -> x2, other arithmetic: none -> 4.09 us  [the longest x1 3.2 us: body(): jnp.zeros((each_owner_rows, rank, down_cols), f32).at[land]]
  transfers between devices with their start and end apart: 6 -> 9, of which waited for: 5 -> 6; matrix products, arithmetic and copies ran while one was open for 24% -> 30% of each run, Pallas kernels for 0% -> 0%
where the time goes in v2:
time: 292 us; the launch traced here: 291 us
  waiting for transfers between devices  151 us (52%)
  local copies, waits for them, and re-layouts  64.7 us (22%)
  matrix products  28.5 us (10%)
  starting transfers between devices  17.7 us (6%)
  other arithmetic  15.1 us (5%)
  between operations  14.2 us (5%)
    ppermute x3, waiting for transfers between devices, body(): lax.ppermute(w_part_full, 'dp', [(i, (i + 2 * step) % dp_count) for i in...  83.4 us
    all_gather x1, waiting for transfers between devices, body(): shares = lax.all_gather(slab, 'fsdp', axis=0, tiled=False)  43 us
    unnamed x38, local copies, waits for them, and re-layouts  14.2 us
    dot_general x1, local copies, waits for them, and re-layouts, body(): lax.dot_general(masked_back, tokens, contract, preferred_element_type=f32)  12 us
    dot_general x1, matrix products, body(): out_own = jnp.dot(tokens, w_own, preferred_element_type=f32)  11.3 us
    all_to_all x1, waiting for transfers between devices, body(): got = lax.all_to_all(send, 'dp', split_axis=0, concat_axis=0, tiled=True)  10.9 us
    concatenate x1, local copies, waits for them, and re-layouts, body(): jnp.concatenate([part_down, part_up], axis=2)  10.9 us
    all_gather x1, waiting for transfers between devices, body(): w_part_full = lax.all_gather(w_part, 'fsdp', axis=0, tiled=True)  10.8 us
  transfers between devices with their start and end apart: 9, of which 6 were waited for; matrix products, arithmetic and copies ran while one was open for 30% of the time, Pallas kernels for 0%

profile of v2, /device:TPU:1, one launch (start us, length us, event | category | flops | bytes accessed | tf_op | source)
XLA Modules:
  0.0 290.9 jit_solution(9394188541867024993)
XLA Ops:
  7.2 0.8 copy.42
  8.0 0.1 reshape.434
  8.1 1.4 gather_fusion.1
  9.5 0.1 reshape.433
  9.6 0.1 fusion.19
  9.7 0.1 fusion.1
  9.9 0.1 select_reduce_fusion
  10.0 1.8 gather_fusion.3
  11.8 2.8 gather_fusion.2
  14.6 0.1 broadcast_select_fusion.2
  14.7 0.1 broadcast_select_fusion.1
  14.8 1.1 maximum_select_fusion
  15.9 5.8 %all-to-all-start = ((bf16[8,64,576]{2,1,0:T(8,128)(2,1)}), bf16[8,64,576]{2,1,0:T(8,128)(2,1)S(1)}, u32[]{:S(2)}, u32[]{:S(2)}) async-start(bf16[8,64,576]{2,1,0:T(8,128)(2,1)} %maximum_select_fusion), calls=%async_computation | async-start | bytes 1310720 | tf_op jit(solution)/shard_map/all_to_all | solution.py:77
  21.7 10.9 %all-to-all-done = bf16[8,64,576]{2,1,0:T(8,128)(2,1)S(1)} async-done(((bf16[8,64,576]{2,1,0:T(8,128)(2,1)}), bf16[8,64,576]{2,1,0:T(8,128)(2,1)S(1)}, u32[]{:S(2)}, u32[]{:S(2)}) %all-to-all-start) | async-done | bytes 589856 | tf_op jit(solution)/shard_map/all_to_all | solution.py:77
  32.6 0.6 gather_fusion.4
  33.2 0.8 bitcast_select_fusion
  34.1 0.7 constant_dynamic-slice_fusion.2
  35.1 1.3 copy.48
  36.5 12.0 %copy.56 = bf16[8192,512]{1,0:T(8,128)(2,1)} copy(bf16[8192,512]{0,1:T(8,128)(2,1)} %bitcast.107) | data formatting | bytes 16777216 | tf_op jit(solution)/shard_map/dot_general | solution.py:111
  48.4 43.0 %all-gather.5.cloned.1.call-done = bf16[16,4,64,576]{3,2,1,0:T(8,128)(2,1)} async-done(((bf16[1,4,64,576]{3,2,1,0:T(8,128)(2,1)}), bf16[16,4,64,576]{3,2,1,0:T(8,128)(2,1)}) %all-gather.5.cloned.1.call-update) | async-done | bytes 4718608 | tf_op jit(solution)/shard_map/all_gather | solution.py:80
  91.4 1.3 slice_bitcast_fusion.1
  92.7 0.7 copy.46
  93.4 0.7 reshape_reshape.7
  94.1 2.9 slice_bitcast_fusion
  97.0 2.4 copy.45
  99.5 4.4 %copy.59 = bf16[32,8,16,512]{3,1,2,0:T(8,128)(2,1)S(1)} copy(bf16[32,8,16,512]{3,2,1,0:T(8,128)(2,1)S(1)} %bitcast.106) | data formatting | bytes 8388608
  103.9 0.5 fusion.21
  104.4 2.4 fusion.20
  106.8 0.1 multiply_reduce_fusion
  107.0 0.9 convolution_bitcast_fusion.1
  108.0 0.2 slice-done.1
  108.1 2.4 convolution_bitcast_fusion
  110.5 5.2 %pad_maximum_fusion = f32[16,256,576]{2,1,0:T(8,128)} fusion(f32[16,256,64]{2,1,0:T(8,128)S(1)} %convolution_bitcast_fusion.1, f32[16,256,512]{2,1,0:T(8,128)S(1)} %convolution_bitcast_fusion), kind=kLoop, calls=%fused_computation.8 | loop fusion | flops 2359296 | bytes 18874368 | tf_op jit(solution)/shard_map/concatenate | solution.py:119
  115.7 10.9 %copy.51 = f32[16,256,576]{1,2,0:T(8,128)} copy(f32[16,256,576]{2,1,0:T(8,128)} %pad_maximum_fusion) | data formatting | bytes 18874368 | tf_op jit(solution)/shard_map/concatenate | solution.py:119
  126.6 10.8 %all-gather.3.cloned.1.call-done = bf16[8192,128]{1,0:T(8,128)(2,1)} async-done(((bf16[512,128]{1,0:T(8,128)(2,1)}), bf16[8192,128]{1,0:T(8,128)(2,1)}) %all-gather.3.cloned.1.call-update) | async-done | bytes 2097168 | tf_op jit(solution)/shard_map/all_gather | solution.py:40
  137.4 1.2 collective-permute-start
  138.6 2.4 collective-permute-start.1
  141.0 1.2 collective-permute-start.2
  142.2 3.1 %constant_dynamic-update-slice_fusion.3 = bf16[8192,512]{1,0:T(8,128)(2,1)} fusion(bf16[8192,128]{1,0:T(8,128)(2,1)} %all-gather.3.cloned.1.call-done), kind=kLoop, calls=%fused_computation.34 | loop fusion | bytes 4194304
  145.3 39.0 %collective-permute-done = bf16[8192,128]{1,0:T(8,128)(2,1)S(1)} collective-permute-done((bf16[8192,128]{1,0:T(8,128)(2,1)}, bf16[8192,128]{1,0:T(8,128)(2,1)S(1)}, u32[]{:S(2)}, u32[]{:S(2)}) %collective-permute-start) | collective-permute-done | bytes 2097184 | tf_op jit(solution)/shard_map/ppermute | solution.py:44
  184.2 1.5 constant_dynamic-update-slice_fusion.2
  185.7 44.4 %collective-permute-done.1 = bf16[8192,128]{1,0:T(8,128)(2,1)S(1)} collective-permute-done((bf16[8192,128]{1,0:T(8,128)(2,1)}, bf16[8192,128]{1,0:T(8,128)(2,1)S(1)}, u32[]{:S(2)}, u32[]{:S(2)}) %collective-permute-start.1) | collective-permute-done | bytes 2097184 | tf_op jit(solution)/shard_map/ppermute | solution.py:44
  230.1 1.5 constant_dynamic-update-slice_fusion.1
  231.5 1.5 constant_dynamic-update-slice_fusion
  233.0 2.6 collective-permute-start.3
  235.7 0.1 fusion.2
  235.9 11.3 %convolution_bitcast_fusion.3 = f32[512,512]{0,1:T(8,128)} fusion(bf16[8192,512]{1,0:T(8,128)(2,1)} %constant_dynamic-update-slice_fusion, bf16[512,8192]{1,0:T(8,128)(2,1)} %param.8), kind=kOutput, calls=%fused_computation.15 | convolution fusion | flops 4294967296 | bytes 17825792 | tf_op jit(solution)/shard_map/dot_general | solution.py:50
  247.2 1.3 copy.52
  248.5 0.6 gather_fusion.5
  249.1 1.2 select_select_fusion
  250.4 4.4 %all-to-all-start.1 = ((f32[8,64,576]{2,1,0:T(8,128)}), f32[8,64,576]{2,1,0:T(8,128)}, u32[]{:S(2)}, u32[]{:S(2)}) async-start(f32[8,64,576]{2,1,0:T(8,128)} %select_select_fusion), calls=%async_computation.1 | async-start | bytes 2621440 | tf_op jit(solution)/shard_map/all_to_all | solution.py:128
  254.8 9.6 %convolution_bitcast_fusion.2 = f32[512,512]{0,1:T(8,128)S(1)} fusion(bf16[8192,512]{1,0:T(8,128)(2,1)} %collective-permute-done.3, bf16[512,8192]{1,0:T(8,128)(2,1)} %param.8), kind=kOutput, calls=%fused_computation.14 | convolution fusion | flops 4294967296 | bytes 17825792 | tf_op jit(solution)/shard_map/dot_general | solution.py:51
  264.5 0.2 pad_maximum_fusion.1
  264.7 2.0 gather_fusion
  266.7 1.9 copy.55
  268.6 1.4 add_convert_fusion
  270.0 2.5 all-to-all-done.1
  272.6 1.5 broadcast_select_fusion
  274.0 0.1 slice.30
  274.2 4.5 %broadcast_in_dim.149 = f32[64,64,512]{2,1,0:T(8,128)} broadcast(f32[]{:T(128)} %constant.200.clone.1), dimensions={} | broadcast | bytes 8388612 | tf_op jit(solution)/shard_map/broadcast_in_dim | solution.py:131
  278.7 3.2 %scatter_fusion = f32[64,64,512]{2,1,0:T(8,128)} fusion(f32[64,64,512]{2,1,0:T(8,128)} %broadcast_in_dim.149, s32[8]{0:T(128)S(1)} %get-tuple-element.13, f32[8,64,512]{2,1,0:T(8,128)S(1)} %slice.30), kind=kCustom, calls=%fused_computation.6 | custom fusion | flops 262144 | bytes 3145760 | tf_op jit(solution)/shard_map/scatter-add | solution.py:131
  281.9 0.2 broadcast_in_dim.155
  282.1 0.9 scatter_fusion.1
  283.0 1.3 copy-done.7
  (60 shorter events, 0.8 us)
Async XLA Ops:
  7.2 26.9 %copy-start = (bf16[512,1024]{1,0:T(8,128)(2,1)S(1)}, bf16[512,1024]{1,0:T(8,128)(2,1)}, u32[]{:S(2)}) copy-start(bf16[512,1024]{1,0:T(8,128)(2,1)} %param.9) | copy-start | bytes 3145732
  9.5 25.4 %copy-start.9 = (s32[1,64]{1,0:T(1,128)S(1)}, s32[1,64]{1,0:T(1,128)}, u32[]{:S(2)}) copy-start(s32[1,64]{1,0:T(1,128)} %param.13) | copy-start | bytes 772
  9.5 25.6 %copy-start.4 = (bf16[512,1024]{1,0:T(8,128)(2,1)S(1)}, bf16[512,1024]{1,0:T(8,128)(2,1)}, u32[]{:S(2)}) copy-start(bf16[512,1024]{1,0:T(8,128)(2,1)} %param.12) | copy-start | bytes 3145732
  15.9 16.7 %all-to-all-start = ((bf16[8,64,576]{2,1,0:T(8,128)(2,1)}), bf16[8,64,576]{2,1,0:T(8,128)(2,1)S(1)}, u32[]{:S(2)}, u32[]{:S(2)}) async-start(bf16[8,64,576]{2,1,0:T(8,128)(2,1)} %maximum_select_fusion), calls=%async_computation | async-start | bytes 1310720 | tf_op jit(solution)/shard_map/all_to_all | solution.py:77
  21.7 69.7 %all-gather.5.cloned.1.call-start = ((), (), s32[]{:S(2)}) async-start(), calls=%async_computation.4 | async-start | bytes 5570560 | tf_op jit(solution)/shard_map/all_gather | solution.py:80
  34.1 103.4 %all-gather.3.cloned.1.call-start = ((), (), s32[]{:S(2)}) async-start(), calls=%async_computation.3 | async-start | bytes 2228224 | tf_op jit(solution)/shard_map/all_gather | solution.py:40
  34.8 212.4 %reduce-scatter.4.cloned.1.call-start = ((), (), s32[]{:S(2)}) async-start(), calls=%async_computation.5 | async-start | bytes 10027008
  94.1 9.7 %copy-start.2 = (bf16[256,1024]{1,0:T(8,128)(2,1)}, bf16[256,1024]{1,0:T(8,128)(2,1)S(1)}, u32[]{:S(2)}) copy-start(bf16[256,1024]{1,0:T(8,128)(2,1)S(1)} %reshape_reshape.7) | copy-start | bytes 1572868
  97.0 7.4 %slice-start.2 = ((s8[8388608]{0:T(1024)(128)(4,1)}), s8[4194304]{0:T(1024)(128)(4,1)S(1)}, s32[]{:S(2)}) async-start(s8[8388608]{0:T(1024)(128)(4,1)} %bitcast.108), calls=%async_computation.8 | async-start | bytes 8388608
  99.5 4.4 %copy-start.5 = (bf16[512,1024]{1,0:T(8,128)(2,1)S(1)}, bf16[512,1024]{1,0:T(8,128)(2,1)}, u32[]{:S(2)}) copy-start(bf16[512,1024]{1,0:T(8,128)(2,1)} %param.12) | copy-start | bytes 3145732
  99.5 4.9 %slice-start.3 = ((s8[8388608]{0:T(1024)(128)(4,1)}), s8[4194304]{0:T(1024)(128)(4,1)S(1)}, s32[]{:S(2)}) async-start(s8[8388608]{0:T(1024)(128)(4,1)} %bitcast.108), calls=%async_computation.9 | async-start | bytes 8388608
  104.4 3.6 %slice-start = ((s8[8388608]{0:T(1024)(128)(4,1)}), s8[4194304]{0:T(1024)(128)(4,1)S(1)}, s32[]{:S(2)}) async-start(s8[8388608]{0:T(1024)(128)(4,1)} %bitcast.103), calls=%async_computation.6 | async-start | bytes 8388608
  104.4 2.6 copy-start.6
  104.4 3.7 %slice-start.1 = ((s8[8388608]{0:T(1024)(128)(4,1)}), s8[4194304]{0:T(1024)(128)(4,1)S(1)}, s32[]{:S(2)}) async-start(s8[8388608]{0:T(1024)(128)(4,1)} %bitcast.103), calls=%async_computation.7 | async-start | bytes 8388608
  137.4 46.8 %collective-permute-start = (bf16[8192,128]{1,0:T(8,128)(2,1)}, bf16[8192,128]{1,0:T(8,128)(2,1)S(1)}, u32[]{:S(2)}, u32[]{:S(2)}) collective-permute-start(bf16[8192,128]{1,0:T(8,128)(2,1)} %all-gather.3.cloned.1.call-done), channel_id=1, source_target_pairs={{0,32},{16,48},{32,64},{48,80},{64,96},{80,112},{96,0},{112,16},{1... | collective-permute-start | bytes 6291464 | tf_op jit(solution)/shard_map/ppermute | solution.py:44
  138.6 91.5 %collective-permute-start.1 = (bf16[8192,128]{1,0:T(8,128)(2,1)}, bf16[8192,128]{1,0:T(8,128)(2,1)S(1)}, u32[]{:S(2)}, u32[]{:S(2)}) collective-permute-start(bf16[8192,128]{1,0:T(8,128)(2,1)} %all-gather.3.cloned.1.call-done), channel_id=1, source_target_pairs={{0,64},{16,80},{32,96},{48,112},{64,0},{80,16},{96,32},{112,48},{1... | collective-permute-start | bytes 6291464 | tf_op jit(solution)/shard_map/ppermute | solution.py:44
  141.0 90.5 %collective-permute-start.2 = (bf16[8192,128]{1,0:T(8,128)(2,1)}, bf16[8192,128]{1,0:T(8,128)(2,1)S(1)}, u32[]{:S(2)}, u32[]{:S(2)}) collective-permute-start(bf16[8192,128]{1,0:T(8,128)(2,1)} %all-gather.3.cloned.1.call-done), channel_id=1, source_target_pairs={{0,96},{16,112},{32,0},{48,16},{64,32},{80,48},{96,64},{112,80},{1... | collective-permute-start | bytes 6291464 | tf_op jit(solution)/shard_map/ppermute | solution.py:44
  233.0 21.8 %collective-permute-start.3 = (bf16[8192,512]{1,0:T(8,128)(2,1)}, bf16[8192,512]{1,0:T(8,128)(2,1)}, u32[]{:S(2)}, u32[]{:S(2)}) collective-permute-start(bf16[8192,512]{1,0:T(8,128)(2,1)} %constant_dynamic-update-slice_fusion), channel_id=1, source_target_pairs={{0,16},{16,0},{32,48},{48,32},{64,80},{80,64},{96,112},{112,96},{1... | collective-permute-start | bytes 25165832 | tf_op jit(solution)/shard_map/ppermute | solution.py:49
  250.4 22.2 %all-to-all-start.1 = ((f32[8,64,576]{2,1,0:T(8,128)}), f32[8,64,576]{2,1,0:T(8,128)}, u32[]{:S(2)}, u32[]{:S(2)}) async-start(f32[8,64,576]{2,1,0:T(8,128)} %select_select_fusion), calls=%async_computation.1 | async-start | bytes 2621440 | tf_op jit(solution)/shard_map/all_to_all | solution.py:128
  254.8 9.6 %copy-start.8 = (f32[512,512]{0,1:T(8,128)S(1)}, f32[512,512]{0,1:T(8,128)}, u32[]{:S(2)}) copy-start(f32[512,512]{0,1:T(8,128)} %convolution_bitcast_fusion.3) | copy-start | bytes 3145732
  264.6 3.9 %copy-start.3 = (bf16[256,1024]{1,0:T(8,128)(2,1)S(1)}, bf16[256,1024]{1,0:T(8,128)(2,1)}, u32[]{:S(2)}) copy-start(bf16[256,1024]{1,0:T(8,128)(2,1)} %copy-done.2) | copy-start | bytes 1572868
  274.2 10.2 %copy-start.1 = (bf16[512,1024]{1,0:T(8,128)(2,1)S(1)}, bf16[512,1024]{1,0:T(8,128)(2,1)}, u32[]{:S(2)}) copy-start(bf16[512,1024]{1,0:T(8,128)(2,1)} %param.9) | copy-start | bytes 3145732
  283.0 1.3 copy-start.7
Sparse Core Ops, SparseCore 0:
  34.2 57.1 all-gather.4
  93.5 43.8 all-gather.2
  140.9 86.8 reduce-scatter.3

commit v3 on v2

--- a/solution.py
+++ b/solution.py
@@ -38,13 +38,15 @@
         frozen_value_matrix, group_index * part_cols, part_cols, axis=1
     )
     w_part_full = lax.all_gather(w_part, "fsdp", axis=0, tiled=True)
-    same_parity = [w_part_full]
-    for step in range(1, dp_count // 2):
-        same_parity.append(
-            lax.ppermute(
-                w_part_full, "dp", [(i, (i + 2 * step) % dp_count) for i in range(dp_count)]
-            )
-        )
+    up_x = [(i, (i + 2) % dp_count) for i in range(dp_count)]
+    down_x = [(i, (i - 2) % dp_count) for i in range(dp_count)]
+    from_left = lax.ppermute(w_part_full, "dp", up_x)
+    from_right = lax.ppermute(w_part_full, "dp", down_x)
+    half_part = part_cols // 2
+    far_a = lax.ppermute(from_left[:, :half_part], "dp", up_x)
+    far_b = lax.ppermute(from_right[:, half_part:], "dp", down_x)
+    far = jnp.concatenate([far_a, far_b], axis=1)
+    same_parity = [w_part_full, from_left, far, from_right]
     w_own = jnp.concatenate(same_parity, axis=1)
     w_partner = lax.ppermute(w_own, "dp", [(i, i ^ 1) for i in range(dp_count)])
     out_own = jnp.dot(tokens, w_own, preferred_element_type=f32)
@@ -115,9 +117,9 @@
     rows = list_len * rank
     part_down = part_down.reshape(rows, fsdp_count, down_cols).transpose(1, 0, 2)
     part_up = part_up.reshape(rows, fsdp_count, up_cols).transpose(1, 0, 2)
-    summed = lax.psum_scatter(
-        jnp.concatenate([part_down, part_up], axis=2), "fsdp", scatter_dimension=0, tiled=True
-    )[0]
+    sum_down = lax.psum_scatter(part_down, "fsdp", scatter_dimension=0, tiled=True)[0]
+    sum_up = lax.psum_scatter(part_up, "fsdp", scatter_dimension=0, tiled=True)[0]
+    summed = jnp.concatenate([sum_down, sum_up], axis=1)
 
     owner_range = jnp.arange(dp_count, dtype=jnp.int32)
     to_owner = my_owner[None, :] == owner_range[:, None]

time: 292 us -> 350 us (1.20)
  waiting for transfers between devices: 151 us -> 211 us
  local copies, waits for them, and re-layouts: 64.7 us -> 55.8 us
  matrix products: 28.5 us -> 35.7 us
  other arithmetic: 15.1 us -> 11 us
  starting transfers between devices: 17.7 us -> 21.2 us
    unnamed x4 -> x6, waiting for transfers between devices: 0.05 us -> 72.1 us
    ppermute x3 -> x4, waiting for transfers between devices: 83.4 us -> 61.5 us  [the longest x1 44.3 us: body(): from_left = lax.ppermute(w_part_full, 'dp', up_x)]
    all_gather x1, waiting for transfers between devices: 43 us -> 55.6 us  [body(): shares = lax.all_gather(slab, 'fsdp', axis=0, tiled=False)]
    concatenate x1, local copies, waits for them, and re-layouts: 10.9 us -> 0.93 us  [body(): summed = jnp.concatenate([sum_down, sum_up], axis=1)]
    dot_general x1, matrix products: 2.38 us -> 9.18 us  [body(): lax.dot_general(masked_back, tokens, contract, preferred_element_type=f32)]
    concatenate x1, other arithmetic: 5.2 us -> 1.09 us  [body(): summed = jnp.concatenate([sum_down, sum_up], axis=1)]
    unnamed x38 -> x32, local copies, waits for them, and re-layouts: 14.2 us -> 14.7 us
  transfers between devices with their start and end apart: 9 -> 11, of which waited for: 6 -> 8; matrix products, arithmetic and copies ran while one was open for 30% -> 23% of each run, Pallas kernels for 0% -> 0%
where the time goes in v3:
time: 350 us; the launch traced here: 349 us
  waiting for transfers between devices  211 us (60%)
  local copies, waits for them, and re-layouts  55.8 us (16%)
  matrix products  35.7 us (10%)
  starting transfers between devices  21.2 us (6%)
  between operations  14.2 us (4%)
  other arithmetic  11 us (3%)
    unnamed x6, waiting for transfers between devices  72.1 us
    all_gather x1, waiting for transfers between devices, body(): shares = lax.all_gather(slab, 'fsdp', axis=0, tiled=False)  55.6 us
    ppermute x1, waiting for transfers between devices, body(): from_left = lax.ppermute(w_part_full, 'dp', up_x)  44.3 us
    ppermute x1, waiting for transfers between devices, body(): far_a = lax.ppermute(from_left[:, :half_part], 'dp', up_x)  16 us
    unnamed x32, local copies, waits for them, and re-layouts  14.7 us
    dot_general x1, local copies, waits for them, and re-layouts, body(): lax.dot_general(masked_back, tokens, contract, preferred_element_type=f32)  12.2 us
    dot_general x1, matrix products, body(): out_own = jnp.dot(tokens, w_own, preferred_element_type=f32)  11.3 us
    all_to_all x1, waiting for transfers between devices, body(): got = lax.all_to_all(send, 'dp', split_axis=0, concat_axis=0, tiled=True)  10.9 us
  transfers between devices with their start and end apart: 11, of which 8 were waited for; matrix products, arithmetic and copies ran while one was open for 23% of the time, Pallas kernels for 0%

profile of v3, /device:TPU:1, one launch (start us, length us, event | category | flops | bytes accessed | tf_op | source)
XLA Modules:
  0.0 349.0 jit_solution(12175471088303171875)
XLA Ops:
  7.2 0.8 copy.32
  8.0 0.1 reshape.439
  8.1 1.4 gather_fusion.1
  9.6 0.1 fusion.19
  9.7 0.1 fusion.1
  9.9 0.1 select_reduce_fusion
  10.0 1.8 gather_fusion.3
  11.8 2.8 gather_fusion.2
  14.7 0.1 broadcast_select_fusion.1
  14.8 1.1 maximum_select_fusion
  15.9 5.8 %all-to-all-start = ((bf16[8,64,576]{2,1,0:T(8,128)(2,1)}), bf16[8,64,576]{2,1,0:T(8,128)(2,1)S(1)}, u32[]{:S(2)}, u32[]{:S(2)}) async-start(bf16[8,64,576]{2,1,0:T(8,128)(2,1)} %maximum_select_fusion), calls=%async_computation | async-start | bytes 1310720 | tf_op jit(solution)/shard_map/all_to_all | solution.py:79
  21.7 10.9 %all-to-all-done = bf16[8,64,576]{2,1,0:T(8,128)(2,1)S(1)} async-done(((bf16[8,64,576]{2,1,0:T(8,128)(2,1)}), bf16[8,64,576]{2,1,0:T(8,128)(2,1)S(1)}, u32[]{:S(2)}, u32[]{:S(2)}) %all-to-all-start) | async-done | bytes 589856 | tf_op jit(solution)/shard_map/all_to_all | solution.py:79
  32.6 0.6 gather_fusion.4
  33.2 0.8 bitcast_select_fusion
  34.2 0.8 copy.46
  35.3 0.5 copy.38
  35.8 55.6 %all-gather.5.cloned.1.call-done = bf16[16,4,64,576]{3,2,1,0:T(8,128)(2,1)} async-done(((bf16[1,4,64,576]{3,2,1,0:T(8,128)(2,1)}), bf16[16,4,64,576]{3,2,1,0:T(8,128)(2,1)}) %all-gather.5.cloned.1.call-update) | async-done | bytes 4718608 | tf_op jit(solution)/shard_map/all_gather | solution.py:82
  91.4 1.3 slice_bitcast_fusion.1
  92.7 1.7 copy.36
  94.4 2.1 reshape_reshape.7
  96.5 2.7 slice_bitcast_fusion
  99.2 2.4 copy.35
  101.6 4.4 %copy.48 = bf16[32,8,16,512]{3,1,2,0:T(8,128)(2,1)S(1)} copy(bf16[32,8,16,512]{3,2,1,0:T(8,128)(2,1)S(1)} %bitcast.105) | data formatting | bytes 8388608
  106.0 0.5 fusion.21
  106.5 2.4 fusion.20
  108.9 0.1 multiply_reduce_fusion
  109.1 1.4 convolution_bitcast_fusion.1
  110.6 12.2 %copy.43 = bf16[8192,512]{1,0:T(8,128)(2,1)} copy(bf16[8192,512]{0,1:T(8,128)(2,1)} %bitcast.107) | data formatting | bytes 16777216 | tf_op jit(solution)/shard_map/dot_general | solution.py:113
  122.8 9.2 %convolution_bitcast_fusion = f32[16,256,512]{2,1,0:T(8,128)} fusion(bf16[512,256,1]{0,1,2:T(8,128)(2,1)S(1)} %bitcast.114, bf16[16,512,512]{2,1,0:T(8,128)(2,1)} %bitcast.104), kind=kOutput, calls=%fused_computation.9 | convolution fusion | flops 2147483648 | bytes 17039360 | tf_op jit(solution)/shard_map/dot_general | solution.py:113
  132.0 8.1 %all-gather.3.cloned.1.call-done = bf16[8192,128]{0,1:T(8,128)(2,1)} async-done(((bf16[512,128]{0,1:T(8,128)(2,1)}), bf16[8192,128]{0,1:T(8,128)(2,1)}) %all-gather.3.cloned.1.call-update) | async-done | bytes 2097168 | tf_op jit(solution)/shard_map/all_gather | solution.py:40
  140.1 1.2 collective-permute-start
  141.3 1.5 collective-permute-start.2
  142.8 44.3 %collective-permute-done = bf16[8192,128]{0,1:T(8,128)(2,1)S(1)} collective-permute-done((bf16[8192,128]{0,1:T(8,128)(2,1)}, bf16[8192,128]{0,1:T(8,128)(2,1)S(1)}, u32[]{:S(2)}, u32[]{:S(2)}) %collective-permute-start) | collective-permute-done | bytes 2097184 | tf_op jit(solution)/shard_map/ppermute | solution.py:43
  187.2 0.2 collective-permute-start.1
  187.3 3.1 constant_dynamic-update-slice_fusion.4
  190.5 2.7 collective-permute-start.3
  193.1 1.5 constant_dynamic-update-slice_fusion.3
  194.6 16.0 %collective-permute-done.1 = bf16[8192,64]{0,1:T(8,128)(2,1)S(1)} collective-permute-done((bf16[8192,64]{0,1:T(8,128)(2,1)S(1)}, bf16[8192,64]{0,1:T(8,128)(2,1)S(1)}, u32[]{:S(2)}, u32[]{:S(2)}) %collective-permute-start.1) | collective-permute-done | bytes 1048608 | tf_op jit(solution)/shard_map/ppermute | solution.py:46
  210.6 1.0 constant_dynamic-update-slice_fusion.2
  211.7 1.2 collective-permute-done.3
  212.8 1.0 constant_dynamic-update-slice_fusion.1
  213.9 1.5 constant_dynamic-update-slice_fusion
  215.3 3.7 %collective-permute-start.4 = (bf16[8192,512]{0,1:T(8,128)(2,1)}, bf16[8192,512]{0,1:T(8,128)(2,1)}, u32[]{:S(2)}, u32[]{:S(2)}) collective-permute-start(bf16[8192,512]{0,1:T(8,128)(2,1)} %constant_dynamic-update-slice_fusion), channel_id=1, source_target_pairs={{0,16},{16,0},{32,48},{48,32},{64,80},{80,64},{96,112},{112,96},{1... | collective-permute-start | bytes 25165832 | tf_op jit(solution)/shard_map/ppermute | solution.py:51
  219.1 0.1 fusion.2
  219.3 11.3 %convolution_bitcast_fusion.3 = f32[512,512]{0,1:T(8,128)} fusion(bf16[8192,512]{0,1:T(8,128)(2,1)} %constant_dynamic-update-slice_fusion, bf16[512,8192]{1,0:T(8,128)(2,1)} %param.8), kind=kOutput, calls=%fused_computation.14 | convolution fusion | flops 4294967296 | bytes 17825792 | tf_op jit(solution)/shard_map/dot_general | solution.py:52
  230.6 0.9 copy.45
  231.5 72.0 %reduce-scatter.7.cloned.1.call-done = f32[1,256,512]{2,1,0:T(8,128)} async-done(((f32[16,256,512]{2,1,0:T(8,128)}), f32[1,256,512]{2,1,0:T(8,128)}) %reduce-scatter.7.cloned.1.call-update) | async-done | bytes 524304
  303.5 1.1 pad_maximum_fusion.1
  304.6 0.6 gather_fusion.5
  305.2 1.3 select_select_fusion
  306.5 6.2 %all-to-all-start.1 = ((f32[8,64,576]{2,1,0:T(8,128)}), f32[8,64,576]{2,1,0:T(8,128)}, u32[]{:S(2)}, u32[]{:S(2)}) async-start(f32[8,64,576]{2,1,0:T(8,128)} %select_select_fusion), calls=%async_computation.1 | async-start | bytes 2621440 | tf_op jit(solution)/shard_map/all_to_all | solution.py:130
  312.6 9.6 %convolution_bitcast_fusion.2 = f32[512,512]{0,1:T(8,128)S(1)} fusion(bf16[8192,512]{0,1:T(8,128)(2,1)} %collective-permute-done.4, bf16[512,8192]{1,0:T(8,128)(2,1)} %param.8), kind=kOutput, calls=%fused_computation.13 | convolution fusion | flops 4294967296 | bytes 17825792 | tf_op jit(solution)/shard_map/dot_general | solution.py:53
  322.3 0.2 pad_maximum_fusion
  322.4 2.0 gather_fusion
  324.4 1.9 copy.42
  326.4 1.4 add_convert_fusion
  327.8 2.8 all-to-all-done.1
  330.7 1.5 broadcast_select_fusion
  332.1 0.1 slice.40
  332.3 4.5 %broadcast_in_dim.149 = f32[64,64,512]{2,1,0:T(8,128)} broadcast(f32[]{:T(128)} %constant.200.clone.1), dimensions={} | broadcast | bytes 8388612 | tf_op jit(solution)/shard_map/broadcast_in_dim | solution.py:133
  336.8 3.2 scatter_fusion
  340.0 0.2 broadcast_in_dim.155
  340.2 0.9 scatter_fusion.1
  341.1 1.3 copy-done.5
  (59 shorter events, 1.1 us)
Async XLA Ops:
  7.2 26.9 %copy-start = (bf16[512,1024]{1,0:T(8,128)(2,1)S(1)}, bf16[512,1024]{1,0:T(8,128)(2,1)}, u32[]{:S(2)}) copy-start(bf16[512,1024]{1,0:T(8,128)(2,1)} %param.9) | copy-start | bytes 3145732
  9.5 25.5 %copy-start.7 = (s32[1,64]{1,0:T(1,128)S(1)}, s32[1,64]{1,0:T(1,128)}, u32[]{:S(2)}) copy-start(s32[1,64]{1,0:T(1,128)} %param.13) | copy-start | bytes 772
  9.5 25.7 %copy-start.4 = (bf16[512,1024]{1,0:T(8,128)(2,1)S(1)}, bf16[512,1024]{1,0:T(8,128)(2,1)}, u32[]{:S(2)}) copy-start(bf16[512,1024]{1,0:T(8,128)(2,1)} %param.12) | copy-start | bytes 3145732
  15.9 16.7 %all-to-all-start = ((bf16[8,64,576]{2,1,0:T(8,128)(2,1)}), bf16[8,64,576]{2,1,0:T(8,128)(2,1)S(1)}, u32[]{:S(2)}, u32[]{:S(2)}) async-start(bf16[8,64,576]{2,1,0:T(8,128)(2,1)} %maximum_select_fusion), calls=%async_computation | async-start | bytes 1310720 | tf_op jit(solution)/shard_map/all_to_all | solution.py:79
  21.7 69.7 %all-gather.5.cloned.1.call-start = ((), (), s32[]{:S(2)}) async-start(), calls=%async_computation.5 | async-start | bytes 5570560 | tf_op jit(solution)/shard_map/all_gather | solution.py:82
  34.0 106.0 %all-gather.3.cloned.1.call-start = ((), (), s32[]{:S(2)}) async-start(), calls=%async_computation.4 | async-start | bytes 2228224 | tf_op jit(solution)/shard_map/all_gather | solution.py:40
  35.0 195.6 %reduce-scatter.9.cloned.1.call-start = ((), (), s32[]{:S(2)}) async-start(), calls=%async_computation.7 | async-start | bytes 1114112
  96.5 9.5 %copy-start.2 = (bf16[256,1024]{1,0:T(8,128)(2,1)}, bf16[256,1024]{1,0:T(8,128)(2,1)S(1)}, u32[]{:S(2)}) copy-start(bf16[256,1024]{1,0:T(8,128)(2,1)S(1)} %reshape_reshape.7) | copy-start | bytes 1572868
  99.2 7.3 %slice-start = ((s8[8388608]{0:T(1024)(128)(4,1)}), s8[4194304]{0:T(1024)(128)(4,1)S(1)}, s32[]{:S(2)}) async-start(s8[8388608]{0:T(1024)(128)(4,1)} %bitcast.108), calls=%async_computation.8 | async-start | bytes 8388608
  101.6 4.9 %slice-start.1 = ((s8[8388608]{0:T(1024)(128)(4,1)}), s8[4194304]{0:T(1024)(128)(4,1)S(1)}, s32[]{:S(2)}) async-start(s8[8388608]{0:T(1024)(128)(4,1)} %bitcast.108), calls=%async_computation.9 | async-start | bytes 8388608
  110.6 192.9 %reduce-scatter.7.cloned.1.call-start = ((), (), s32[]{:S(2)}) async-start(), calls=%async_computation.6 | async-start | bytes 8912896
  140.1 47.0 %collective-permute-start = (bf16[8192,128]{0,1:T(8,128)(2,1)}, bf16[8192,128]{0,1:T(8,128)(2,1)S(1)}, u32[]{:S(2)}, u32[]{:S(2)}) collective-permute-start(bf16[8192,128]{0,1:T(8,128)(2,1)} %all-gather.3.cloned.1.call-done), channel_id=1, source_target_pairs={{0,32},{16,48},{32,64},{48,80},{64,96},{80,112},{96,0},{112,16},{1... | collective-permute-start | bytes 6291464 | tf_op jit(solution)/shard_map/ppermute | solution.py:43
  141.3 49.1 %collective-permute-start.2 = (bf16[8192,128]{0,1:T(8,128)(2,1)}, bf16[8192,128]{0,1:T(8,128)(2,1)S(1)}, u32[]{:S(2)}, u32[]{:S(2)}) collective-permute-start(bf16[8192,128]{0,1:T(8,128)(2,1)} %all-gather.3.cloned.1.call-done), channel_id=1, source_target_pairs={{0,96},{16,112},{32,0},{48,16},{64,32},{80,48},{96,64},{112,80},{1... | collective-permute-start | bytes 6291464 | tf_op jit(solution)/shard_map/ppermute | solution.py:44
  187.2 23.5 %collective-permute-start.1 = (bf16[8192,64]{0,1:T(8,128)(2,1)S(1)}, bf16[8192,64]{0,1:T(8,128)(2,1)S(1)}, u32[]{:S(2)}, u32[]{:S(2)}) collective-permute-start(bf16[8192,64]{0,1:T(8,128)(2,1)S(1)} %slice.36), channel_id=1, source_target_pairs={{0,32},{16,48},{32,64},{48,80},{64,96},{80,112},{96,0},{112,16},{1... | collective-permute-start | bytes 3145736 | tf_op jit(solution)/shard_map/ppermute | solution.py:46
  190.5 22.4 %collective-permute-start.3 = (bf16[8192,64]{0,1:T(8,128)(2,1)S(1)}, bf16[8192,64]{0,1:T(8,128)(2,1)S(1)}, u32[]{:S(2)}, u32[]{:S(2)}) collective-permute-start(bf16[8192,64]{0,1:T(8,128)(2,1)S(1)} %slice.37), channel_id=1, source_target_pairs={{0,96},{16,112},{32,0},{48,16},{64,32},{80,48},{96,64},{112,80},{1... | collective-permute-start | bytes 3145736 | tf_op jit(solution)/shard_map/ppermute | solution.py:47
  215.3 97.3 %collective-permute-start.4 = (bf16[8192,512]{0,1:T(8,128)(2,1)}, bf16[8192,512]{0,1:T(8,128)(2,1)}, u32[]{:S(2)}, u32[]{:S(2)}) collective-permute-start(bf16[8192,512]{0,1:T(8,128)(2,1)} %constant_dynamic-update-slice_fusion), channel_id=1, source_target_pairs={{0,16},{16,0},{32,48},{48,32},{64,80},{80,64},{96,112},{112,96},{1... | collective-permute-start | bytes 25165832 | tf_op jit(solution)/shard_map/ppermute | solution.py:51
  306.5 24.2 %all-to-all-start.1 = ((f32[8,64,576]{2,1,0:T(8,128)}), f32[8,64,576]{2,1,0:T(8,128)}, u32[]{:S(2)}, u32[]{:S(2)}) async-start(f32[8,64,576]{2,1,0:T(8,128)} %select_select_fusion), calls=%async_computation.1 | async-start | bytes 2621440 | tf_op jit(solution)/shard_map/all_to_all | solution.py:130
  312.6 9.6 %copy-start.6 = (f32[512,512]{0,1:T(8,128)S(1)}, f32[512,512]{0,1:T(8,128)}, u32[]{:S(2)}) copy-start(f32[512,512]{0,1:T(8,128)} %convolution_bitcast_fusion.3) | copy-start | bytes 3145732
  322.4 3.9 %copy-start.3 = (bf16[256,1024]{1,0:T(8,128)(2,1)S(1)}, bf16[256,1024]{1,0:T(8,128)(2,1)}, u32[]{:S(2)}) copy-start(bf16[256,1024]{1,0:T(8,128)(2,1)} %copy-done.2) | copy-start | bytes 1572868
  332.3 10.2 %copy-start.1 = (bf16[512,1024]{1,0:T(8,128)(2,1)S(1)}, bf16[512,1024]{1,0:T(8,128)(2,1)}, u32[]{:S(2)}) copy-start(bf16[512,1024]{1,0:T(8,128)(2,1)} %param.9) | copy-start | bytes 3145732
  341.1 1.3 copy-start.5
Sparse Core Ops, SparseCore 0:
  34.2 57.1 all-gather.4
  93.5 46.5 all-gather.2
  143.9 71.5 reduce-scatter.8
  219.1 84.3 reduce-scatter.6

commit v4 on v3

--- a/solution.py
+++ b/solution.py
@@ -37,7 +37,44 @@
     w_part = lax.dynamic_slice_in_dim(
         frozen_value_matrix, group_index * part_cols, part_cols, axis=1
     )
-    w_part_full = lax.all_gather(w_part, "fsdp", axis=0, tiled=True)
+
+    list_slot = jnp.take(composer_storage_index, needed_composers, axis=0)
+    list_owner = list_slot // each_owner_rows
+    list_local = list_slot % each_owner_rows
+    owned_here = list_owner == group_index
+    locally_owned_slots = jnp.sum(jnp.where(owned_here, list_local, 0), axis=1)
+    owned_any = jnp.any(owned_here, axis=1)
+    send = jnp.concatenate(
+        [
+            jnp.take(adapter_down_maps, locally_owned_slots, axis=0),
+            jnp.take(adapter_up_maps, locally_owned_slots, axis=0),
+        ],
+        axis=2,
+    )
+    send = jnp.where(owned_any[:, None, None], send, jnp.zeros((), send.dtype))
+    got = lax.all_to_all(send, "dp", split_axis=0, concat_axis=0, tiled=True)
+    my_owner = lax.dynamic_index_in_dim(list_owner, group_index, 0, keepdims=False)
+    slab = jnp.take(got, my_owner, axis=0)
+    lane = part_cols
+    down_rows = list_len * rank * down_cols // lane
+    buf = jnp.concatenate(
+        [
+            w_part,
+            slab[..., :down_cols].reshape(down_rows, lane),
+            slab[..., down_cols:].reshape(-1, lane),
+        ],
+        axis=0,
+    )
+    gathered = lax.all_gather(buf, "fsdp", axis=0, tiled=False)
+    w_rows = w_part.shape[0]
+    shares_down = gathered[:, w_rows : w_rows + down_rows].reshape(
+        fsdp_count, list_len, rank, down_cols
+    )
+    shares_up = gathered[:, w_rows + down_rows :].reshape(fsdp_count, list_len, rank, up_cols)
+    full_down = shares_down.transpose(1, 2, 0, 3).reshape(list_len, rank, width)
+    full_up = shares_up.transpose(1, 2, 0, 3).reshape(list_len, rank, value_cols)
+
+    w_part_full = gathered[:, : w_part.shape[0]].reshape(width, part_cols)
     up_x = [(i, (i + 2) % dp_count) for i in range(dp_count)]
     down_x = [(i, (i - 2) % dp_count) for i in range(dp_count)]
     from_left = lax.ppermute(w_part_full, "dp", up_x)
@@ -61,27 +98,6 @@
         dp_count // 2 + ((partner_index - part_ids) % dp_count) // 2,
     )
     frozen_rows = jnp.take(held, where_held, axis=1).reshape(tok_rows, value_cols)
-
-    list_slot = jnp.take(composer_storage_index, needed_composers, axis=0)
-    list_owner = list_slot // each_owner_rows
-    list_local = list_slot % each_owner_rows
-    owned_here = list_owner == group_index
-    locally_owned_slots = jnp.sum(jnp.where(owned_here, list_local, 0), axis=1)
-    owned_any = jnp.any(owned_here, axis=1)
-    send = jnp.concatenate(
-        [
-            jnp.take(adapter_down_maps, locally_owned_slots, axis=0),
-            jnp.take(adapter_up_maps, locally_owned_slots, axis=0),
-        ],
-        axis=2,
-    )
-    send = jnp.where(owned_any[:, None, None], send, jnp.zeros((), send.dtype))
-    got = lax.all_to_all(send, "dp", split_axis=0, concat_axis=0, tiled=True)
-    my_owner = lax.dynamic_index_in_dim(list_owner, group_index, 0, keepdims=False)
-    slab = jnp.take(got, my_owner, axis=0)
-    shares = lax.all_gather(slab, "fsdp", axis=0, tiled=False)
-    full_down = shares[..., :down_cols].transpose(1, 2, 0, 3).reshape(list_len, rank, width)
-    full_up = shares[..., down_cols:].transpose(1, 2, 0, 3).reshape(list_len, rank, value_cols)
 
     group_picks = window_composer_position[0]
     my_picks = lax.dynamic_slice_in_dim(group_picks, member_index * windows, windows, 0)
@@ -118,7 +134,7 @@
     part_down = part_down.reshape(rows, fsdp_count, down_cols).transpose(1, 0, 2)
     part_up = part_up.reshape(rows, fsdp_count, up_cols).transpose(1, 0, 2)
     sum_down = lax.psum_scatter(part_down, "fsdp", scatter_dimension=0, tiled=True)[0]
-    sum_up = lax.psum_scatter(part_up, "fsdp", scatter_dimension=0, tiled=True)[0]
+    sum_up = jnp.sum(lax.all_to_all(part_up, "fsdp", 0, 0, tiled=True), axis=0)
     summed = jnp.concatenate([sum_down, sum_up], axis=1)
 
     owner_range = jnp.arange(dp_count, dtype=jnp.int32)

time: 350 us -> 300 us (0.86)
  waiting for transfers between devices: 211 us -> 147 us
  local copies, waits for them, and re-layouts: 55.8 us -> 68.8 us
  starting transfers between devices: 21.2 us -> 25.2 us
    unnamed x6 -> x3, waiting for transfers between devices: 72.1 us -> 0.03 us
    all_to_all x0 -> x1, waiting for transfers between devices: none -> 16.7 us  [body(): sum_up = jnp.sum(lax.all_to_all(part_up, 'fsdp', 0, 0, tiled=True), axis=0)]
    all_gather x2 -> x1, waiting for transfers between devices: 63.7 us -> 52.3 us  [body(): gathered = lax.all_gather(buf, 'fsdp', axis=0, tiled=False)]
    reshape x0 -> x5, local copies, waits for them, and re-layouts: none -> 11.3 us  [the longest x1 7.72 us: body(): gathered[:, w_rows:w_rows + down_rows]]
    slice x0 -> x5, local copies, waits for them, and re-layouts: none -> 9.11 us  [the longest x1 4.67 us: body(): gathered[:, w_rows:w_rows + down_rows]]
    all_to_all x0 -> x1, starting transfers between devices: none -> 4.89 us  [body(): sum_up = jnp.sum(lax.all_to_all(part_up, 'fsdp', 0, 0, tiled=True), axis=0)]
    transpose x4 -> x2, local copies, waits for them, and re-layouts: 8.03 us -> 5.4 us  [the longest x1 4.72 us: body(): full_down = shares_down.transpose(1, 2, 0, 3).reshape(list_len, rank, width)]
    unnamed x32 -> x39, local copies, waits for them, and re-layouts: 14.7 us -> 12.3 us
  transfers between devices with their start and end apart: 11 -> 10, of which waited for: 8 -> 6; matrix products, arithmetic and copies ran while one was open for 23% -> 19% of each run, Pallas kernels for 0% -> 0%
where the time goes in v4:
time: 300 us; the launch traced here: 299 us
  waiting for transfers between devices  147 us (49%)
  local copies, waits for them, and re-layouts  68.8 us (23%)
  matrix products  32.3 us (11%)
  starting transfers between devices  25.2 us (8%)
  between operations  14.6 us (5%)
  other arithmetic  11.8 us (4%)
    all_gather x1, waiting for transfers between devices, body(): gathered = lax.all_gather(buf, 'fsdp', axis=0, tiled=False)  52.3 us
    ppermute x1, waiting for transfers between devices, body(): from_left = lax.ppermute(w_part_full, 'dp', up_x)  45.1 us
    ppermute x1, waiting for transfers between devices, body(): far_a = lax.ppermute(from_left[:, :half_part], 'dp', up_x)  18.7 us
    all_to_all x1, waiting for transfers between devices, body(): sum_up = jnp.sum(lax.all_to_all(part_up, 'fsdp', 0, 0, tiled=True), axis=0)  16.7 us
    unnamed x39, local copies, waits for them, and re-layouts  12.3 us
    dot_general x1, local copies, waits for them, and re-layouts, body(): lax.dot_general(masked_back, tokens, contract, preferred_element_type=f32)  11.9 us
    dot_general x1, matrix products, body(): out_own = jnp.dot(tokens, w_own, preferred_element_type=f32)  11.3 us
    all_to_all x1, waiting for transfers between devices, body(): got = lax.all_to_all(send, 'dp', split_axis=0, concat_axis=0, tiled=True)  10.8 us
  transfers between devices with their start and end apart: 10, of which 6 were waited for; matrix products, arithmetic and copies ran while one was open for 19% of the time, Pallas kernels for 0%

profile of v4, /device:TPU:1, one launch (start us, length us, event | category | flops | bytes accessed | tf_op | source)
XLA Modules:
  0.0 299.2 jit_solution(1529903848178282221)
XLA Ops:
  7.2 0.8 copy.35
  8.1 1.4 gather_fusion
  9.6 0.1 fusion.19
  9.7 0.1 fusion.1
  10.0 1.8 gather_fusion.2
  11.8 2.8 gather_fusion.1
  14.7 0.1 broadcast_select_fusion.1
  14.8 1.1 maximum_select_fusion
  15.9 5.8 %all-to-all-start = ((bf16[8,64,576]{2,1,0:T(8,128)(2,1)}), bf16[8,64,576]{2,1,0:T(8,128)(2,1)S(1)}, u32[]{:S(2)}, u32[]{:S(2)}) async-start(bf16[8,64,576]{2,1,0:T(8,128)(2,1)} %maximum_select_fusion), calls=%async_computation | async-start | bytes 1310720 | tf_op jit(solution)/shard_map/all_to_all | solution.py:55
  21.8 10.8 %all-to-all-done = bf16[8,64,576]{2,1,0:T(8,128)(2,1)S(1)} async-done(((bf16[8,64,576]{2,1,0:T(8,128)(2,1)}), bf16[8,64,576]{2,1,0:T(8,128)(2,1)S(1)}, u32[]{:S(2)}, u32[]{:S(2)}) %all-to-all-start) | async-done | bytes 589856 | tf_op jit(solution)/shard_map/all_to_all | solution.py:55
  32.6 0.6 gather_fusion.3
  33.5 0.2 reshape.433
  33.6 0.8 pad_maximum_fusion.2
  34.8 11.9 %copy.49 = bf16[8192,512]{1,0:T(8,128)(2,1)} copy(bf16[8192,512]{0,1:T(8,128)(2,1)} %bitcast.108) | data formatting | bytes 16777216 | tf_op jit(solution)/shard_map/dot_general | solution.py:129
  46.7 52.3 %all-gather.3.cloned.1.call-done = bf16[26624,128]{1,0:T(8,128)(2,1)} async-done(((bf16[1664,128]{1,0:T(8,128)(2,1)}), bf16[26624,128]{1,0:T(8,128)(2,1)}) %all-gather.3.cloned.1.call-update) | async-done | bytes 6815760 | tf_op jit(solution)/shard_map/all_gather | solution.py:68
  99.0 1.1 slice.54
  100.1 4.7 %slice.53 = bf16[16,1024,128]{2,1,0:T(8,128)(2,1)} slice(bf16[16,1664,128]{2,1,0:T(8,128)(2,1)} %bitcast.115), slice={[0:16], [512:1536], [0:128]} | slice | bytes 8388608 | tf_op jit(solution)/shard_map/slice | solution.py:70
  104.8 0.4 reshape.439
  105.2 0.7 copy.41
  105.9 0.7 reshape_reshape.7
  106.6 7.7 %reshape.437 = bf16[16,4,64,512]{3,2,1,0:T(8,128)(2,1)} reshape(bf16[16,1024,128]{2,1,0:T(8,128)(2,1)} %slice.53) | data formatting | bytes 8388608 | tf_op jit(solution)/shard_map/reshape | solution.py:70
  114.4 4.7 %copy.40 = bf16[4,64,16,512]{3,2,1,0:T(8,128)(2,1)S(1)} copy(bf16[4,64,16,512]{3,1,0,2:T(8,128)(2,1)} %bitcast.105) | data formatting | bytes 8388608 | tf_op jit(solution)/shard_map/transpose | solution.py:74
  119.1 4.4 %copy.53 = bf16[32,8,16,512]{3,1,2,0:T(8,128)(2,1)S(1)} copy(bf16[32,8,16,512]{3,2,1,0:T(8,128)(2,1)S(1)} %bitcast.106) | data formatting | bytes 8388608
  123.5 2.4 fusion.20
  125.9 0.5 fusion.21
  126.4 0.1 multiply_reduce_fusion
  126.6 0.8 broadcast_multiply_fusion
  127.3 5.7 %convolution_bitcast_fusion = f32[16,256,512]{2,1,0:T(8,128)} fusion(bf16[512,256,1]{0,1,2:T(8,128)(2,1)S(1)} %bitcast.120, bf16[16,512,512]{2,1,0:T(8,128)(2,1)S(1)} %bitcast.104), kind=kOutput, calls=%fused_computation.8 | convolution fusion | flops 2147483648 | bytes 17039360 | tf_op jit(solution)/shard_map/dot_general | solution.py:129
  133.1 3.3 %slice.50 = bf16[16,512,128]{2,1,0:T(8,128)(2,1)} slice(bf16[16,1664,128]{2,1,0:T(8,128)(2,1)} %bitcast.116), slice={[0:16], [0:512], [0:128]} | slice | bytes 4194304 | tf_op jit(solution)/shard_map/slice | solution.py:77
  136.4 2.9 copy.47
  139.3 1.3 collective-permute-start
  140.6 1.5 collective-permute-start.2
  142.1 45.1 %collective-permute-done = bf16[8192,128]{0,1:T(8,128)(2,1)S(1)} collective-permute-done((bf16[8192,128]{0,1:T(8,128)(2,1)S(1)}, bf16[8192,128]{0,1:T(8,128)(2,1)S(1)}, u32[]{:S(2)}, u32[]{:S(2)}) %collective-permute-start) | collective-permute-done | bytes 2097184 | tf_op jit(solution)/shard_map/ppermute | solution.py:80
  187.4 1.5 constant_dynamic-update-slice_fusion.4
  188.9 2.7 collective-permute-start.3
  191.6 1.5 constant_dynamic-update-slice_fusion.3
  193.1 18.7 %collective-permute-done.1 = bf16[8192,64]{0,1:T(8,128)(2,1)S(1)} collective-permute-done((bf16[8192,64]{0,1:T(8,128)(2,1)S(1)}, bf16[8192,64]{0,1:T(8,128)(2,1)S(1)}, u32[]{:S(2)}, u32[]{:S(2)}) %collective-permute-start.1) | collective-permute-done | bytes 1048608 | tf_op jit(solution)/shard_map/ppermute | solution.py:83
  211.8 1.0 constant_dynamic-update-slice_fusion.2
  212.8 1.0 constant_dynamic-update-slice_fusion.1
  213.9 1.5 constant_dynamic-update-slice_fusion
  215.3 2.4 collective-permute-start.4
  217.7 0.5 copy.43
  218.3 1.4 convolution_bitcast_fusion.1
  219.7 4.9 %all-to-all-start.1 = ((f32[16,256,64]{1,2,0:T(8,128)}), f32[16,256,64]{1,2,0:T(8,128)S(1)}, u32[]{:S(2)}, u32[]{:S(2)}) async-start(f32[16,256,64]{1,2,0:T(8,128)} %convolution_bitcast_fusion.1), calls=%async_computation.1 | async-start | bytes 2097152 | tf_op jit(solution)/shard_map/all_to_all | solution.py:137
  224.7 0.1 fusion.2
  224.9 16.7 %all-to-all-done.1 = f32[16,256,64]{1,2,0:T(8,128)S(1)} async-done(((f32[16,256,64]{1,2,0:T(8,128)}), f32[16,256,64]{1,2,0:T(8,128)S(1)}, u32[]{:S(2)}, u32[]{:S(2)}) %all-to-all-start.1) | async-done | bytes 1048608 | tf_op jit(solution)/shard_map/all_to_all | solution.py:137
  241.8 11.3 %convolution_bitcast_fusion.3 = f32[512,512]{0,1:T(8,128)} fusion(bf16[8192,512]{0,1:T(8,128)(2,1)} %constant_dynamic-update-slice_fusion, bf16[512,8192]{1,0:T(8,128)(2,1)} %param.8), kind=kOutput, calls=%fused_computation.13 | convolution fusion | flops 4294967296 | bytes 17825792 | tf_op jit(solution)/shard_map/dot_general | solution.py:89
  253.0 1.1 pad_maximum_fusion.1
  254.1 0.6 gather_fusion.5
  254.8 1.2 select_select_fusion
  256.0 6.5 %all-to-all-start.2 = ((f32[8,64,576]{2,1,0:T(8,128)}), f32[8,64,576]{2,1,0:T(8,128)}, u32[]{:S(2)}, u32[]{:S(2)}) async-start(f32[8,64,576]{2,1,0:T(8,128)} %select_select_fusion), calls=%async_computation.2 | async-start | bytes 2621440 | tf_op jit(solution)/shard_map/all_to_all | solution.py:146
  262.6 9.6 %convolution_bitcast_fusion.2 = f32[512,512]{0,1:T(8,128)S(1)} fusion(bf16[8192,512]{0,1:T(8,128)(2,1)} %collective-permute-done.4, bf16[512,8192]{1,0:T(8,128)(2,1)} %param.8), kind=kOutput, calls=%fused_computation.12 | convolution fusion | flops 4294967296 | bytes 17825792 | tf_op jit(solution)/shard_map/dot_general | solution.py:90
  272.2 0.2 pad_maximum_fusion
  272.4 2.0 gather_fusion.4
  274.4 1.9 copy.48
  276.3 1.4 add_convert_fusion
  277.7 2.8 all-to-all-done.2
  280.6 1.5 broadcast_select_fusion
  282.1 0.1 slice.55
  282.2 4.5 %broadcast_in_dim.149 = f32[64,64,512]{2,1,0:T(8,128)} broadcast(f32[]{:T(128)} %constant.200.clone.1), dimensions={} | broadcast | bytes 8388612 | tf_op jit(solution)/shard_map/broadcast_in_dim | solution.py:149
  286.7 3.2 %scatter_fusion = f32[64,64,512]{2,1,0:T(8,128)} fusion(f32[64,64,512]{2,1,0:T(8,128)} %broadcast_in_dim.149, s32[8]{0:T(128)S(1)} %get-tuple-element.13, f32[8,64,512]{2,1,0:T(8,128)S(1)} %slice.55), kind=kCustom, calls=%fused_computation.6 | custom fusion | flops 262144 | bytes 3145760 | tf_op jit(solution)/shard_map/scatter-add | solution.py:149
  289.9 0.2 broadcast_in_dim.155
  290.2 0.9 scatter_fusion.1
  291.1 1.3 copy-done.6
  (73 shorter events, 1.7 us)
Async XLA Ops:
  7.2 14.6 %copy-start = (bf16[512,1024]{1,0:T(8,128)(2,1)S(1)}, bf16[512,1024]{1,0:T(8,128)(2,1)}, u32[]{:S(2)}) copy-start(bf16[512,1024]{1,0:T(8,128)(2,1)} %param.9) | copy-start | bytes 3145732
  14.6 19.9 %copy-start.9 = (s32[1,64]{1,0:T(1,128)S(1)}, s32[1,64]{1,0:T(1,128)}, u32[]{:S(2)}) copy-start(s32[1,64]{1,0:T(1,128)} %param.13) | copy-start | bytes 772
  15.9 16.7 %all-to-all-start = ((bf16[8,64,576]{2,1,0:T(8,128)(2,1)}), bf16[8,64,576]{2,1,0:T(8,128)(2,1)S(1)}, u32[]{:S(2)}, u32[]{:S(2)}) async-start(bf16[8,64,576]{2,1,0:T(8,128)(2,1)} %maximum_select_fusion), calls=%async_computation | async-start | bytes 1310720 | tf_op jit(solution)/shard_map/all_to_all | solution.py:55
  21.7 77.3 %all-gather.3.cloned.1.call-start = ((), (), s32[]{:S(2)}) async-start(), calls=%async_computation.4 | async-start | bytes 7241728 | tf_op jit(solution)/shard_map/all_gather | solution.py:68
  34.4 218.6 %reduce-scatter.4.cloned.1.call-start = ((), (), s32[]{:S(2)}) async-start(), calls=%async_computation.5 | async-start | bytes 8912896
  106.6 19.3 %copy-start.2 = (bf16[256,1024]{1,0:T(8,128)(2,1)}, bf16[256,1024]{1,0:T(8,128)(2,1)S(1)}, u32[]{:S(2)}) copy-start(bf16[256,1024]{1,0:T(8,128)(2,1)S(1)} %reshape_reshape.7) | copy-start | bytes 1572868
  114.4 9.1 %slice-start.2 = ((s8[8388608]{0:T(1024)(128)(4,1)}), s8[4194304]{0:T(1024)(128)(4,1)S(1)}, s32[]{:S(2)}) async-start(s8[8388608]{0:T(1024)(128)(4,1)} %bitcast.109), calls=%async_computation.8 | async-start | bytes 8388608
  119.1 4.4 %slice-start.3 = ((s8[8388608]{0:T(1024)(128)(4,1)}), s8[4194304]{0:T(1024)(128)(4,1)S(1)}, s32[]{:S(2)}) async-start(s8[8388608]{0:T(1024)(128)(4,1)} %bitcast.109), calls=%async_computation.9 | async-start | bytes 8388608
  123.5 3.9 %slice-start = ((s8[8388608]{0:T(1024)(128)(4,1)}), s8[4194304]{0:T(1024)(128)(4,1)S(1)}, s32[]{:S(2)}) async-start(s8[8388608]{0:T(1024)(128)(4,1)} %bitcast.102), calls=%async_computation.6 | async-start | bytes 8388608
  123.5 2.4 copy-start.4
  123.5 3.8 %slice-start.1 = ((s8[8388608]{0:T(1024)(128)(4,1)}), s8[4194304]{0:T(1024)(128)(4,1)S(1)}, s32[]{:S(2)}) async-start(s8[8388608]{0:T(1024)(128)(4,1)} %bitcast.102), calls=%async_computation.7 | async-start | bytes 8388608
  139.3 47.9 %collective-permute-start = (bf16[8192,128]{0,1:T(8,128)(2,1)S(1)}, bf16[8192,128]{0,1:T(8,128)(2,1)S(1)}, u32[]{:S(2)}, u32[]{:S(2)}) collective-permute-start(bf16[8192,128]{0,1:T(8,128)(2,1)S(1)} %copy.47), channel_id=1, source_target_pairs={{0,32},{16,48},{32,64},{48,80},{64,96},{80,112},{96,0},{112,16},{1... | collective-permute-start | bytes 6291464 | tf_op jit(solution)/shard_map/ppermute | solution.py:80
  140.6 48.3 %collective-permute-start.2 = (bf16[8192,128]{0,1:T(8,128)(2,1)S(1)}, bf16[8192,128]{0,1:T(8,128)(2,1)S(1)}, u32[]{:S(2)}, u32[]{:S(2)}) collective-permute-start(bf16[8192,128]{0,1:T(8,128)(2,1)S(1)} %copy.47), channel_id=1, source_target_pairs={{0,96},{16,112},{32,0},{48,16},{64,32},{80,48},{96,64},{112,80},{1... | collective-permute-start | bytes 6291464 | tf_op jit(solution)/shard_map/ppermute | solution.py:81
  187.3 24.5 %collective-permute-start.1 = (bf16[8192,64]{0,1:T(8,128)(2,1)S(1)}, bf16[8192,64]{0,1:T(8,128)(2,1)S(1)}, u32[]{:S(2)}, u32[]{:S(2)}) collective-permute-start(bf16[8192,64]{0,1:T(8,128)(2,1)S(1)} %slice.51), channel_id=1, source_target_pairs={{0,32},{16,48},{32,64},{48,80},{64,96},{80,112},{96,0},{112,16},{1... | collective-permute-start | bytes 3145736 | tf_op jit(solution)/shard_map/ppermute | solution.py:83
  188.9 23.9 %collective-permute-start.3 = (bf16[8192,64]{0,1:T(8,128)(2,1)S(1)}, bf16[8192,64]{0,1:T(8,128)(2,1)S(1)}, u32[]{:S(2)}, u32[]{:S(2)}) collective-permute-start(bf16[8192,64]{0,1:T(8,128)(2,1)S(1)} %slice.52), channel_id=1, source_target_pairs={{0,96},{16,112},{32,0},{48,16},{64,32},{80,48},{96,64},{112,80},{1... | collective-permute-start | bytes 3145736 | tf_op jit(solution)/shard_map/ppermute | solution.py:84
  193.1 24.6 %copy-start.5 = (bf16[512,1024]{1,0:T(8,128)(2,1)S(1)}, bf16[512,1024]{1,0:T(8,128)(2,1)}, u32[]{:S(2)}) copy-start(bf16[512,1024]{1,0:T(8,128)(2,1)} %param.12) | copy-start | bytes 3145732
  212.8 5.4 %copy-start.7 = (bf16[512,4,64]{0,2,1:T(8,128)(2,1)S(1)}, bf16[512,4,64]{0,2,1:T(8,128)(2,1)}, u32[]{:S(2)}) copy-start(bf16[512,4,64]{0,2,1:T(8,128)(2,1)} %get-tuple-element.10) | copy-start | bytes 786436
  215.3 47.2 %collective-permute-start.4 = (bf16[8192,512]{0,1:T(8,128)(2,1)}, bf16[8192,512]{0,1:T(8,128)(2,1)}, u32[]{:S(2)}, u32[]{:S(2)}) collective-permute-start(bf16[8192,512]{0,1:T(8,128)(2,1)} %constant_dynamic-update-slice_fusion), channel_id=1, source_target_pairs={{0,16},{16,0},{32,48},{48,32},{64,80},{80,64},{96,112},{112,96},{1... | collective-permute-start | bytes 25165832 | tf_op jit(solution)/shard_map/ppermute | solution.py:88
  219.7 21.9 %all-to-all-start.1 = ((f32[16,256,64]{1,2,0:T(8,128)}), f32[16,256,64]{1,2,0:T(8,128)S(1)}, u32[]{:S(2)}, u32[]{:S(2)}) async-start(f32[16,256,64]{1,2,0:T(8,128)} %convolution_bitcast_fusion.1), calls=%async_computation.1 | async-start | bytes 2097152 | tf_op jit(solution)/shard_map/all_to_all | solution.py:137
  256.0 24.6 %all-to-all-start.2 = ((f32[8,64,576]{2,1,0:T(8,128)}), f32[8,64,576]{2,1,0:T(8,128)}, u32[]{:S(2)}, u32[]{:S(2)}) async-start(f32[8,64,576]{2,1,0:T(8,128)} %select_select_fusion), calls=%async_computation.2 | async-start | bytes 2621440 | tf_op jit(solution)/shard_map/all_to_all | solution.py:146
  262.6 9.6 %copy-start.8 = (f32[512,512]{0,1:T(8,128)S(1)}, f32[512,512]{0,1:T(8,128)}, u32[]{:S(2)}) copy-start(f32[512,512]{0,1:T(8,128)} %convolution_bitcast_fusion.3) | copy-start | bytes 3145732
  272.3 3.9 %copy-start.3 = (bf16[256,1024]{1,0:T(8,128)(2,1)S(1)}, bf16[256,1024]{1,0:T(8,128)(2,1)}, u32[]{:S(2)}) copy-start(bf16[256,1024]{1,0:T(8,128)(2,1)} %copy-done.2) | copy-start | bytes 1572868
  282.2 10.2 %copy-start.1 = (bf16[512,1024]{1,0:T(8,128)(2,1)S(1)}, bf16[512,1024]{1,0:T(8,128)(2,1)}, u32[]{:S(2)}) copy-start(bf16[512,1024]{1,0:T(8,128)(2,1)} %param.9) | copy-start | bytes 3145732
  291.1 1.3 copy-start.6
Sparse Core Ops, SparseCore 0:
  34.6 64.4 all-gather.2
  133.2 83.1 reduce-scatter.3

commit v5 on v4

--- a/solution.py
+++ b/solution.py
@@ -44,37 +44,29 @@
     owned_here = list_owner == group_index
     locally_owned_slots = jnp.sum(jnp.where(owned_here, list_local, 0), axis=1)
     owned_any = jnp.any(owned_here, axis=1)
+    down_sel = jnp.take(adapter_down_maps, locally_owned_slots, axis=0)
+    up_sel = jnp.take(adapter_up_maps, locally_owned_slots, axis=0)
+    pad_cols = (-(down_cols + up_cols)) % 128
     send = jnp.concatenate(
-        [
-            jnp.take(adapter_down_maps, locally_owned_slots, axis=0),
-            jnp.take(adapter_up_maps, locally_owned_slots, axis=0),
-        ],
-        axis=2,
+        [down_sel, up_sel, jnp.zeros(up_sel.shape[:2] + (pad_cols,), up_sel.dtype)], axis=2
     )
     send = jnp.where(owned_any[:, None, None], send, jnp.zeros((), send.dtype))
     got = lax.all_to_all(send, "dp", split_axis=0, concat_axis=0, tiled=True)
     my_owner = lax.dynamic_index_in_dim(list_owner, group_index, 0, keepdims=False)
     slab = jnp.take(got, my_owner, axis=0)
-    lane = part_cols
-    down_rows = list_len * rank * down_cols // lane
-    buf = jnp.concatenate(
-        [
-            w_part,
-            slab[..., :down_cols].reshape(down_rows, lane),
-            slab[..., down_cols:].reshape(-1, lane),
-        ],
-        axis=0,
+    slab_cols = slab.shape[2]
+    w_as_slab = w_part.reshape(list_len, rank, -1)
+    buf = jnp.concatenate([slab, w_as_slab], axis=2)
+    buf_cols = buf.shape[2]
+    gathered = lax.all_gather(buf, "fsdp", axis=2, tiled=True).reshape(
+        list_len, rank, fsdp_count, buf_cols
     )
-    gathered = lax.all_gather(buf, "fsdp", axis=0, tiled=False)
-    w_rows = w_part.shape[0]
-    shares_down = gathered[:, w_rows : w_rows + down_rows].reshape(
-        fsdp_count, list_len, rank, down_cols
+    full_down = gathered[..., :down_cols].reshape(list_len, rank, width)
+    full_up = gathered[..., down_cols : down_cols + up_cols].reshape(list_len, rank, value_cols)
+    w_part_full = (
+        gathered[..., slab_cols:].transpose(2, 0, 1, 3).reshape(width, part_cols)
     )
-    shares_up = gathered[:, w_rows + down_rows :].reshape(fsdp_count, list_len, rank, up_cols)
-    full_down = shares_down.transpose(1, 2, 0, 3).reshape(list_len, rank, width)
-    full_up = shares_up.transpose(1, 2, 0, 3).reshape(list_len, rank, value_cols)
 
-    w_part_full = gathered[:, : w_part.shape[0]].reshape(width, part_cols)
     up_x = [(i, (i + 2) % dp_count) for i in range(dp_count)]
     down_x = [(i, (i - 2) % dp_count) for i in range(dp_count)]
     from_left = lax.ppermute(w_part_full, "dp", up_x)
@@ -131,9 +123,8 @@
         scaled_masked_low, value_output_gradient, contract, preferred_element_type=f32
     )
     rows = list_len * rank
-    part_down = part_down.reshape(rows, fsdp_count, down_cols).transpose(1, 0, 2)
     part_up = part_up.reshape(rows, fsdp_count, up_cols).transpose(1, 0, 2)
-    sum_down = lax.psum_scatter(part_down, "fsdp", scatter_dimension=0, tiled=True)[0]
+    sum_down = lax.psum_scatter(part_down, "fsdp", scatter_dimension=1, tiled=True)
     sum_up = jnp.sum(lax.all_to_all(part_up, "fsdp", 0, 0, tiled=True), axis=0)
     summed = jnp.concatenate([sum_down, sum_up], axis=1)
 

time: 300 us -> 324 us (1.080)
  waiting for transfers between devices: 147 us -> 161 us
  local copies, waits for them, and re-layouts: 68.8 us -> 73.8 us
  matrix products: 32.3 us -> 35.7 us
    all_gather x1, waiting for transfers between devices: 52.3 us -> 66.9 us  [body(): lax.all_gather(buf, 'fsdp', axis=2, tiled=True)]
    concatenate x1, local copies, waits for them, and re-layouts: 1.46 us -> 14.4 us  [body(): w_own = jnp.concatenate(same_parity, axis=1)]
    dot_general x1 -> x0, local copies, waits for them, and re-layouts: 11.9 us -> none  [body(): lax.dot_general(masked_back, tokens, contract, preferred_element_type=f32)]
    unnamed x39, local copies, waits for them, and re-layouts: 12.3 us -> 21.4 us
    reshape x5 -> x2, local copies, waits for them, and re-layouts: 11.3 us -> 2.72 us  [the longest x1 2.67 us: body(): gathered[..., slab_cols:].transpose(2, 0, 1, 3).reshape(width, part_cols)]
    slice x1 -> x2, local copies, waits for them, and re-layouts: 0.07 us -> 6.24 us  [body(): far_b = lax.ppermute(from_right[:, half_part:], 'dp', down_x)]
    transpose x2 -> x0, local copies, waits for them, and re-layouts: 5.4 us -> none  [the longest x1 4.72 us: body(): full_down = shares_down.transpose(1, 2, 0, 3).reshape(list_len, rank, width)]
    ppermute x0 -> x2, local copies, waits for them, and re-layouts: none -> 4.52 us  [the longest x1 2.73 us: body(): far_b = lax.ppermute(from_right[:, half_part:], 'dp', down_x)]
  transfers between devices with their start and end apart: 10 -> 10, of which waited for: 6 -> 7; matrix products, arithmetic and copies ran while one was open for 19% -> 21% of each run, Pallas kernels for 0% -> 0%
where the time goes in v5:
time: 324 us; the launch traced here: 323 us
  waiting for transfers between devices  161 us (50%)
  local copies, waits for them, and re-layouts  73.8 us (23%)
  matrix products  35.7 us (11%)
  starting transfers between devices  26 us (8%)
  between operations  14.5 us (4%)
  other arithmetic  11.8 us (4%)
    all_gather x1, waiting for transfers between devices, body(): lax.all_gather(buf, 'fsdp', axis=2, tiled=True)  66.9 us
    ppermute x1, waiting for transfers between devices, body(): from_left = lax.ppermute(w_part_full, 'dp', up_x)  45.1 us
    unnamed x39, local copies, waits for them, and re-layouts  21.4 us
    all_to_all x1, waiting for transfers between devices, body(): sum_up = jnp.sum(lax.all_to_all(part_up, 'fsdp', 0, 0, tiled=True), axis=0)  16.4 us
    ppermute x1, waiting for transfers between devices, body(): far_a = lax.ppermute(from_left[:, :half_part], 'dp', up_x)  15.8 us
    concatenate x1, local copies, waits for them, and re-layouts, body(): w_own = jnp.concatenate(same_parity, axis=1)  14.4 us
    dot_general x1, matrix products, body(): out_own = jnp.dot(tokens, w_own, preferred_element_type=f32)  11.3 us
    all_to_all x1, waiting for transfers between devices, body(): got = lax.all_to_all(send, 'dp', split_axis=0, concat_axis=0, tiled=True)  10.7 us
  transfers between devices with their start and end apart: 10, of which 7 were waited for; matrix products, arithmetic and copies ran while one was open for 21% of the time, Pallas kernels for 0%

profile of v5, /device:TPU:1, one launch (start us, length us, event | category | flops | bytes accessed | tf_op | source)
XLA Modules:
  0.0 323.0 jit_solution(3192790582854841569)
XLA Ops:
  7.2 0.8 copy.24
  8.1 0.7 gather_fusion
  8.9 0.1 fusion.19
  9.1 0.1 fusion.1
  9.4 1.8 gather_fusion.2
  11.2 2.8 gather_fusion.1
  14.2 1.0 maximum_select_fusion
  15.3 5.9 %all-to-all-start = ((bf16[8,64,640]{2,1,0:T(8,128)(2,1)}), bf16[8,64,640]{2,1,0:T(8,128)(2,1)S(1)}, u32[]{:S(2)}, u32[]{:S(2)}) async-start(bf16[8,64,640]{2,1,0:T(8,128)(2,1)} %maximum_select_fusion), calls=%async_computation | async-start | bytes 1310720 | tf_op jit(solution)/shard_map/all_to_all | solution.py:54
  21.4 10.7 %all-to-all-done = bf16[8,64,640]{2,1,0:T(8,128)(2,1)S(1)} async-done(((bf16[8,64,640]{2,1,0:T(8,128)(2,1)}), bf16[8,64,640]{2,1,0:T(8,128)(2,1)S(1)}, u32[]{:S(2)}, u32[]{:S(2)}) %all-to-all-start) | async-done | bytes 655392 | tf_op jit(solution)/shard_map/all_to_all | solution.py:54
  32.1 0.6 gather_fusion.3
  32.8 0.8 pad_maximum_fusion.2
  34.0 66.9 %all-gather.2.cloned.1.call-done = bf16[4,64,14336]{2,1,0:T(8,128)(2,1)} async-done(((bf16[4,64,896]{2,1,0:T(8,128)(2,1)}), bf16[4,64,14336]{2,1,0:T(8,128)(2,1)}) %all-gather.2.cloned.1.call-update) | async-done | bytes 7340048 | tf_op jit(solution)/shard_map/all_gather | solution.py:61
  100.8 4.7 %copy.40 = bf16[32,8,16,896]{3,2,1,0:T(8,128)(2,1)S(1)} copy(bf16[32,8,16,896]{3,1,2,0:T(8,128)(2,1)} %bitcast.111) | data formatting | bytes 14680064
  105.5 0.2 slice.44
  105.7 2.8 copy-done.3
  108.6 2.5 slice.43
  111.1 0.7 reshape_reshape.7
  111.8 6.7 %copy.42 = bf16[32,8,16,512]{3,1,2,0:T(8,128)(2,1)S(1)} copy(bf16[32,8,16,512]{3,2,1,0:T(8,128)(2,1)} %bitcast.103) | data formatting | bytes 8388608
  118.5 0.5 fusion.21
  119.1 5.9 %fusion.20 = f32[256,512]{1,0:T(8,128)S(1)} fusion(bf16[256,8192]{1,0:T(8,128)(2,1)S(1)} %bitcast.113, bf16[512,8192]{1,0:T(8,128)(2,1)} %param.8), kind=kOutput, calls=%fused_computation.118 | convolution fusion | flops 2147483648 | bytes 13107200 | tf_op jit(solution)/shard_map/dot_general | solution.py:104
  125.0 0.1 multiply_reduce_fusion
  125.1 0.8 broadcast_multiply_fusion
  125.9 5.6 %fusion.22 = f32[256,8192]{1,0:T(8,128)} fusion(bf16[512,256]{0,1:T(8,128)(2,1)S(1)} %bitcast.115, bf16[512,8192]{1,0:T(8,128)(2,1)S(1)} %bitcast.107), kind=kOutput, calls=%fused_computation.120 | convolution fusion | flops 2147483648 | bytes 17039360 | tf_op jit(solution)/shard_map/dot_general | solution.py:121
  131.5 1.9 slice.40
  133.4 2.0 copy.47
  135.4 2.7 reshape.417
  138.1 1.3 collective-permute-start
  139.4 1.5 collective-permute-start.2
  140.9 45.1 %collective-permute-done = bf16[8192,128]{1,0:T(8,128)(2,1)S(1)} collective-permute-done((bf16[8192,128]{1,0:T(8,128)(2,1)S(1)}, bf16[8192,128]{1,0:T(8,128)(2,1)S(1)}, u32[]{:S(2)}, u32[]{:S(2)}) %collective-permute-start) | collective-permute-done | bytes 2097184 | tf_op jit(solution)/shard_map/ppermute | solution.py:72
  186.0 1.3 copy-done.4
  187.3 2.7 copy.28
  190.0 3.5 %slice.42 = bf16[8192,64]{1,0:T(8,128)(2,1)} slice(bf16[8192,128]{1,0:T(8,128)(2,1)} %collective-permute-done.2), slice={[0:8192], [64:128]} | slice | bytes 2097152 | tf_op jit(solution)/shard_map/slice | solution.py:76
  193.5 2.7 copy.29
  196.2 2.7 collective-permute-start.3
  198.9 15.8 %collective-permute-done.1 = bf16[8192,64]{0,1:T(8,128)(2,1)S(1)} collective-permute-done((bf16[8192,64]{0,1:T(8,128)(2,1)}, bf16[8192,64]{0,1:T(8,128)(2,1)S(1)}, u32[]{:S(2)}, u32[]{:S(2)}) %collective-permute-start.1) | collective-permute-done | bytes 1048608 | tf_op jit(solution)/shard_map/ppermute | solution.py:75
  214.7 1.8 copy.30
  216.5 3.4 %collective-permute-done.3 = bf16[8192,64]{0,1:T(8,128)(2,1)} collective-permute-done((bf16[8192,64]{0,1:T(8,128)(2,1)}, bf16[8192,64]{0,1:T(8,128)(2,1)}, u32[]{:S(2)}, u32[]{:S(2)}) %collective-permute-start.3) | collective-permute-done | bytes 1048608 | tf_op jit(solution)/shard_map/ppermute | solution.py:76
  219.9 2.7 copy.31
  222.7 14.4 %concatenate.17 = bf16[8192,512]{1,0:T(8,128)(2,1)} concatenate(bf16[8192,128]{1,0:T(8,128)(2,1)S(1)} %reshape.417, bf16[8192,128]{1,0:T(8,128)(2,1)} %copy-done.4, bf16[8192,64]{1,0:T(8,128)(2,1)} %copy.30, bf16[8192,64]{1,0:T(8,128)(2,1)} %copy.31, bf16[8192,128]{1,0:T(8,128)(2,1)} %collective-permute-done.2), dimensions={1} | concatenate | bytes 16777216 | tf_op jit(solution)/shard_map/concatenate | solution.py:79
  237.0 2.7 collective-permute-start.4
  239.7 1.5 copy.33
  241.2 1.4 convolution_bitcast_fusion
  242.6 4.9 %all-to-all-start.1 = ((f32[16,256,64]{1,2,0:T(8,128)}), f32[16,256,64]{1,2,0:T(8,128)S(1)}, u32[]{:S(2)}, u32[]{:S(2)}) async-start(f32[16,256,64]{1,2,0:T(8,128)} %convolution_bitcast_fusion), calls=%async_computation.2 | async-start | bytes 2097152 | tf_op jit(solution)/shard_map/all_to_all | solution.py:128
  247.6 0.1 fusion.2
  247.8 16.4 %all-to-all-done.1 = f32[16,256,64]{1,2,0:T(8,128)S(1)} async-done(((f32[16,256,64]{1,2,0:T(8,128)}), f32[16,256,64]{1,2,0:T(8,128)S(1)}, u32[]{:S(2)}, u32[]{:S(2)}) %all-to-all-start.1) | async-done | bytes 1048608 | tf_op jit(solution)/shard_map/all_to_all | solution.py:128
  264.4 11.3 %convolution_bitcast_fusion.2 = f32[512,512]{0,1:T(8,128)} fusion(bf16[8192,512]{1,0:T(8,128)(2,1)} %concatenate.17, bf16[512,8192]{1,0:T(8,128)(2,1)} %param.8), kind=kOutput, calls=%fused_computation.13 | convolution fusion | flops 4294967296 | bytes 17825792 | tf_op jit(solution)/shard_map/dot_general | solution.py:81
  275.7 1.1 pad_maximum_fusion.1
  276.8 0.6 gather_fusion.5
  277.4 1.2 select_select_fusion
  278.7 7.0 %all-to-all-start.2 = ((f32[8,64,576]{2,1,0:T(8,128)}), f32[8,64,576]{2,1,0:T(8,128)}, u32[]{:S(2)}, u32[]{:S(2)}) async-start(f32[8,64,576]{2,1,0:T(8,128)} %select_select_fusion), calls=%async_computation.3 | async-start | bytes 2621440 | tf_op jit(solution)/shard_map/all_to_all | solution.py:137
  285.7 9.6 %convolution_bitcast_fusion.1 = f32[512,512]{0,1:T(8,128)S(1)} fusion(bf16[8192,512]{1,0:T(8,128)(2,1)} %collective-permute-done.4, bf16[512,8192]{1,0:T(8,128)(2,1)} %param.8), kind=kOutput, calls=%fused_computation.12 | convolution fusion | flops 4294967296 | bytes 17825792 | tf_op jit(solution)/shard_map/dot_general | solution.py:82
  295.3 0.2 pad_maximum_fusion
  295.5 2.0 gather_fusion.4
  297.5 2.0 copy.37
  299.5 1.4 add_convert_fusion
  300.9 2.8 all-to-all-done.2
  303.7 1.5 broadcast_select_fusion
  305.2 0.1 slice.45
  305.3 4.5 %broadcast_in_dim.155 = f32[64,64,512]{2,1,0:T(8,128)} broadcast(f32[]{:T(128)} %constant.201.clone.1), dimensions={} | broadcast | bytes 8388612 | tf_op jit(solution)/shard_map/broadcast_in_dim | solution.py:140
  309.8 3.2 scatter_fusion
  313.0 0.2 broadcast_in_dim.162
  313.2 0.7 slice-done.2
  313.9 0.9 scatter_fusion.1
  314.8 1.3 copy-done.9
  (70 shorter events, 1.5 us)
Async XLA Ops:
  7.2 14.1 %copy-start = (bf16[512,1024]{1,0:T(8,128)(2,1)S(1)}, bf16[512,1024]{1,0:T(8,128)(2,1)}, u32[]{:S(2)}) copy-start(bf16[512,1024]{1,0:T(8,128)(2,1)} %param.9) | copy-start | bytes 3145732
  7.2 1.0 copy-start.2
  15.3 18.4 %copy-start.12 = (s32[1,64]{1,0:T(1,128)S(1)}, s32[1,64]{1,0:T(1,128)}, u32[]{:S(2)}) copy-start(s32[1,64]{1,0:T(1,128)} %param.13) | copy-start | bytes 772
  15.3 16.8 %all-to-all-start = ((bf16[8,64,640]{2,1,0:T(8,128)(2,1)}), bf16[8,64,640]{2,1,0:T(8,128)(2,1)S(1)}, u32[]{:S(2)}, u32[]{:S(2)}) async-start(bf16[8,64,640]{2,1,0:T(8,128)(2,1)} %maximum_select_fusion), calls=%async_computation | async-start | bytes 1310720 | tf_op jit(solution)/shard_map/all_to_all | solution.py:54
  21.2 79.6 %all-gather.2.cloned.1.call-start = ((), (), s32[]{:S(2)}) async-start(), calls=%async_computation.4 | async-start | bytes 7798784 | tf_op jit(solution)/shard_map/all_gather | solution.py:61
  33.7 242.0 %reduce-scatter.2.cloned.1.call-start = ((), (), s32[]{:S(2)}) async-start(), calls=%async_computation.5 | async-start | bytes 8912896 | tf_op jit(solution)/shard_map/reduce_scatter | solution.py:127
  105.5 3.1 copy-start.3
  111.8 6.7 %copy-start.6 = (bf16[256,1024]{1,0:T(8,128)(2,1)}, bf16[256,1024]{1,0:T(8,128)(2,1)S(1)}, u32[]{:S(2)}) copy-start(bf16[256,1024]{1,0:T(8,128)(2,1)S(1)} %reshape_reshape.7) | copy-start | bytes 1572868
  111.8 6.7 %copy-start.8 = (bf16[512,1024]{1,0:T(8,128)(2,1)S(1)}, bf16[512,1024]{1,0:T(8,128)(2,1)}, u32[]{:S(2)}) copy-start(bf16[512,1024]{1,0:T(8,128)(2,1)} %param.12) | copy-start | bytes 3145732
  119.0 6.8 %slice-start = ((s8[8388608]{0:T(1024)(128)(4,1)}), s8[4194304]{0:T(1024)(128)(4,1)S(1)}, s32[]{:S(2)}) async-start(s8[8388608]{0:T(1024)(128)(4,1)} %bitcast.106), calls=%async_computation.6 | async-start | bytes 8388608
  119.0 6.8 %slice-start.1 = ((s8[8388608]{0:T(1024)(128)(4,1)}), s8[4194304]{0:T(1024)(128)(4,1)S(1)}, s32[]{:S(2)}) async-start(s8[8388608]{0:T(1024)(128)(4,1)} %bitcast.106), calls=%async_computation.7 | async-start | bytes 8388608
  138.1 47.9 %collective-permute-start = (bf16[8192,128]{1,0:T(8,128)(2,1)S(1)}, bf16[8192,128]{1,0:T(8,128)(2,1)S(1)}, u32[]{:S(2)}, u32[]{:S(2)}) collective-permute-start(bf16[8192,128]{1,0:T(8,128)(2,1)S(1)} %reshape.417), channel_id=1, source_target_pairs={{0,32},{16,48},{32,64},{48,80},{64,96},{80,112},{96,0},{112,16},{1... | collective-permute-start | bytes 6291464 | tf_op jit(solution)/shard_map/ppermute | solution.py:72
  139.4 50.6 %collective-permute-start.2 = (bf16[8192,128]{1,0:T(8,128)(2,1)S(1)}, bf16[8192,128]{1,0:T(8,128)(2,1)}, u32[]{:S(2)}, u32[]{:S(2)}) collective-permute-start(bf16[8192,128]{1,0:T(8,128)(2,1)S(1)} %reshape.417), channel_id=1, source_target_pairs={{0,96},{16,112},{32,0},{48,16},{64,32},{80,48},{96,64},{112,80},{1... | collective-permute-start | bytes 6291464 | tf_op jit(solution)/shard_map/ppermute | solution.py:73
  186.0 1.3 copy-start.4
  190.0 24.7 %collective-permute-start.1 = (bf16[8192,64]{0,1:T(8,128)(2,1)}, bf16[8192,64]{0,1:T(8,128)(2,1)S(1)}, u32[]{:S(2)}, u32[]{:S(2)}) collective-permute-start(bf16[8192,64]{0,1:T(8,128)(2,1)} %copy.28), channel_id=1, source_target_pairs={{0,32},{16,48},{32,64},{48,80},{64,96},{80,112},{96,0},{112,16},{1... | collective-permute-start | bytes 3145736 | tf_op jit(solution)/shard_map/ppermute | solution.py:75
  196.2 23.7 %collective-permute-start.3 = (bf16[8192,64]{0,1:T(8,128)(2,1)}, bf16[8192,64]{0,1:T(8,128)(2,1)}, u32[]{:S(2)}, u32[]{:S(2)}) collective-permute-start(bf16[8192,64]{0,1:T(8,128)(2,1)} %copy.29), channel_id=1, source_target_pairs={{0,96},{16,112},{32,0},{48,16},{64,32},{80,48},{96,64},{112,80},{1... | collective-permute-start | bytes 3145736 | tf_op jit(solution)/shard_map/ppermute | solution.py:76
  237.0 4.2 %copy-start.10 = (bf16[512,4,64]{0,2,1:T(8,128)(2,1)S(1)}, bf16[512,4,64]{0,2,1:T(8,128)(2,1)}, u32[]{:S(2)}) copy-start(bf16[512,4,64]{0,2,1:T(8,128)(2,1)} %get-tuple-element.10) | copy-start | bytes 786436
  237.0 48.7 %collective-permute-start.4 = (bf16[8192,512]{1,0:T(8,128)(2,1)}, bf16[8192,512]{1,0:T(8,128)(2,1)}, u32[]{:S(2)}, u32[]{:S(2)}) collective-permute-start(bf16[8192,512]{1,0:T(8,128)(2,1)} %concatenate.17), channel_id=1, source_target_pairs={{0,16},{16,0},{32,48},{48,32},{64,80},{80,64},{96,112},{112,96},{1... | collective-permute-start | bytes 25165832 | tf_op jit(solution)/shard_map/ppermute | solution.py:80
  242.6 21.6 %all-to-all-start.1 = ((f32[16,256,64]{1,2,0:T(8,128)}), f32[16,256,64]{1,2,0:T(8,128)S(1)}, u32[]{:S(2)}, u32[]{:S(2)}) async-start(f32[16,256,64]{1,2,0:T(8,128)} %convolution_bitcast_fusion), calls=%async_computation.2 | async-start | bytes 2097152 | tf_op jit(solution)/shard_map/all_to_all | solution.py:128
  278.7 25.0 %all-to-all-start.2 = ((f32[8,64,576]{2,1,0:T(8,128)}), f32[8,64,576]{2,1,0:T(8,128)}, u32[]{:S(2)}, u32[]{:S(2)}) async-start(f32[8,64,576]{2,1,0:T(8,128)} %select_select_fusion), calls=%async_computation.3 | async-start | bytes 2621440 | tf_op jit(solution)/shard_map/all_to_all | solution.py:137
  285.7 9.6 %copy-start.11 = (f32[512,512]{0,1:T(8,128)S(1)}, f32[512,512]{0,1:T(8,128)}, u32[]{:S(2)}) copy-start(f32[512,512]{0,1:T(8,128)} %convolution_bitcast_fusion.2) | copy-start | bytes 3145732
  297.5 2.0 copy-start.7
  305.2 4.6 %copy-start.5 = (f32[8,64,576]{2,1,0:T(8,128)}, f32[8,64,576]{2,1,0:T(8,128)S(1)}, u32[]{:S(2)}) copy-start(f32[8,64,576]{2,1,0:T(8,128)S(1)} %broadcast_select_fusion) | copy-start | bytes 3538948
  309.8 6.3 %copy-start.1 = (bf16[512,1024]{1,0:T(8,128)(2,1)S(1)}, bf16[512,1024]{1,0:T(8,128)(2,1)}, u32[]{:S(2)}) copy-start(bf16[512,1024]{1,0:T(8,128)(2,1)} %param.9) | copy-start | bytes 3145732
  313.0 0.9 slice-start.2
  314.8 1.3 copy-start.9
Sparse Core Ops, SparseCore 0:
  33.8 66.9 all-gather.1
  131.6 83.1 reduce-scatter.1

commit v6 on v3

--- a/solution.py
+++ b/solution.py
@@ -117,9 +117,9 @@
     rows = list_len * rank
     part_down = part_down.reshape(rows, fsdp_count, down_cols).transpose(1, 0, 2)
     part_up = part_up.reshape(rows, fsdp_count, up_cols).transpose(1, 0, 2)
-    sum_down = lax.psum_scatter(part_down, "fsdp", scatter_dimension=0, tiled=True)[0]
-    sum_up = lax.psum_scatter(part_up, "fsdp", scatter_dimension=0, tiled=True)[0]
-    summed = jnp.concatenate([sum_down, sum_up], axis=1)
+    summed = lax.psum_scatter(
+        jnp.concatenate([part_down, part_up], axis=2), "fsdp", scatter_dimension=0, tiled=True
+    )[0]
 
     owner_range = jnp.arange(dp_count, dtype=jnp.int32)
     to_owner = my_owner[None, :] == owner_range[:, None]

time: 350 us -> 277 us (0.79)
  waiting for transfers between devices: 211 us -> 132 us
  local copies, waits for them, and re-layouts: 55.8 us -> 65.8 us
  matrix products: 35.7 us -> 28.7 us
  other arithmetic: 11 us -> 15.1 us
    unnamed x6 -> x4, waiting for transfers between devices: 72.1 us -> 0.05 us
    all_gather x1, waiting for transfers between devices: 55.6 us -> 42.9 us  [body(): shares = lax.all_gather(slab, 'fsdp', axis=0, tiled=False)]
    concatenate x1, local copies, waits for them, and re-layouts: 0.93 us -> 10.9 us  [body(): jnp.concatenate([part_down, part_up], axis=2)]
    dot_general x1, matrix products: 9.18 us -> 2.37 us  [body(): lax.dot_general(masked_back, tokens, contract, preferred_element_type=f32)]
    all_gather x1, waiting for transfers between devices: 8.11 us -> 13.4 us  [body(): w_part_full = lax.all_gather(w_part, 'fsdp', axis=0, tiled=True)]
    concatenate x1, other arithmetic: 1.09 us -> 5.19 us  [body(): jnp.concatenate([part_down, part_up], axis=2)]
    unnamed x32 -> x40, local copies, waits for them, and re-layouts: 14.7 us -> 15.8 us
  transfers between devices with their start and end apart: 11 -> 10, of which waited for: 8 -> 7; matrix products, arithmetic and copies ran while one was open for 23% -> 32% of each run, Pallas kernels for 0% -> 0%
where the time goes in v6:
time: 277 us; the launch traced here: 276 us
  waiting for transfers between devices  132 us (48%)
  local copies, waits for them, and re-layouts  65.8 us (24%)
  matrix products  28.7 us (10%)
  starting transfers between devices  20.3 us (7%)
  other arithmetic  15.1 us (5%)
  between operations  14.3 us (5%)
    ppermute x1, waiting for transfers between devices, body(): from_left = lax.ppermute(w_part_full, 'dp', up_x)  44.4 us
    all_gather x1, waiting for transfers between devices, body(): shares = lax.all_gather(slab, 'fsdp', axis=0, tiled=False)  42.9 us
    ppermute x1, waiting for transfers between devices, body(): far_a = lax.ppermute(from_left[:, :half_part], 'dp', up_x)  16 us
    unnamed x40, local copies, waits for them, and re-layouts  15.8 us
    all_gather x1, waiting for transfers between devices, body(): w_part_full = lax.all_gather(w_part, 'fsdp', axis=0, tiled=True)  13.4 us
    dot_general x1, local copies, waits for them, and re-layouts, body(): lax.dot_general(masked_back, tokens, contract, preferred_element_type=f32)  11.9 us
    dot_general x1, matrix products, body(): out_own = jnp.dot(tokens, w_own, preferred_element_type=f32)  11.5 us
    concatenate x1, local copies, waits for them, and re-layouts, body(): jnp.concatenate([part_down, part_up], axis=2)  10.9 us
  transfers between devices with their start and end apart: 10, of which 7 were waited for; matrix products, arithmetic and copies ran while one was open for 32% of the time, Pallas kernels for 0%

profile of v6, /device:TPU:1, one launch (start us, length us, event | category | flops | bytes accessed | tf_op | source)
XLA Modules:
  0.0 276.1 jit_solution(5865001813368719480)
XLA Ops:
  7.2 0.8 copy.44
  8.0 0.1 reshape.434
  8.1 1.4 gather_fusion.1
  9.6 0.1 fusion.19
  9.7 0.1 fusion.1
  9.9 0.1 select_reduce_fusion
  10.0 1.8 gather_fusion.3
  11.8 2.8 %gather_fusion.2 = bf16[8,64,512]{2,1,0:T(8,128)(2,1)S(1)} fusion(bf16[64,64,512]{2,1,0:T(8,128)(2,1)} %param.10, s32[1024]{0:T(1024)S(1)} %pad_clamp_fusion.2), kind=kCustom, calls=%fused_computation.2 | custom fusion | bytes 1048608 | tf_op jit(solution)/shard_map/jit(_take)/gather | solution.py:73
  14.7 0.1 broadcast_select_fusion.1
  14.8 1.1 maximum_select_fusion
  15.9 5.8 %all-to-all-start = ((bf16[8,64,576]{2,1,0:T(8,128)(2,1)}), bf16[8,64,576]{2,1,0:T(8,128)(2,1)S(1)}, u32[]{:S(2)}, u32[]{:S(2)}) async-start(bf16[8,64,576]{2,1,0:T(8,128)(2,1)} %maximum_select_fusion), calls=%async_computation | async-start | bytes 1310720 | tf_op jit(solution)/shard_map/all_to_all | solution.py:79
  21.7 10.9 %all-to-all-done = bf16[8,64,576]{2,1,0:T(8,128)(2,1)S(1)} async-done(((bf16[8,64,576]{2,1,0:T(8,128)(2,1)}), bf16[8,64,576]{2,1,0:T(8,128)(2,1)S(1)}, u32[]{:S(2)}, u32[]{:S(2)}) %all-to-all-start) | async-done | bytes 589856 | tf_op jit(solution)/shard_map/all_to_all | solution.py:79
  32.6 0.6 gather_fusion.4
  33.2 0.8 bitcast_select_fusion
  34.2 0.8 copy.60
  35.3 1.3 copy.50
  36.6 11.9 %copy.58 = bf16[8192,512]{1,0:T(8,128)(2,1)} copy(bf16[8192,512]{0,1:T(8,128)(2,1)} %bitcast.107) | data formatting | bytes 16777216 | tf_op jit(solution)/shard_map/dot_general | solution.py:113
  48.5 42.9 %all-gather.5.cloned.1.call-done = bf16[16,4,64,576]{3,2,1,0:T(8,128)(2,1)} async-done(((bf16[1,4,64,576]{3,2,1,0:T(8,128)(2,1)}), bf16[16,4,64,576]{3,2,1,0:T(8,128)(2,1)}) %all-gather.5.cloned.1.call-update) | async-done | bytes 4718608 | tf_op jit(solution)/shard_map/all_gather | solution.py:82
  91.4 1.3 slice_bitcast_fusion.1
  92.7 0.7 copy.48
  93.4 0.7 reshape_reshape.7
  94.1 2.9 %slice_bitcast_fusion = bf16[4,64,16,512]{3,1,0,2:T(8,128)(2,1)S(1)} fusion(bf16[16,4,64,576]{3,2,1,0:T(8,128)(2,1)} %all-gather.5.cloned.1.call-done), kind=kLoop, calls=%fused_computation.9 | loop fusion | bytes 8388608 | tf_op jit(solution)/shard_map/transpose | solution.py:83
  97.0 2.4 copy.47
  99.5 4.4 %copy.62 = bf16[32,8,16,512]{3,1,2,0:T(8,128)(2,1)S(1)} copy(bf16[32,8,16,512]{3,2,1,0:T(8,128)(2,1)S(1)} %bitcast.106) | data formatting | bytes 8388608
  103.9 0.5 fusion.21
  104.4 2.4 fusion.20
  106.8 0.1 multiply_reduce_fusion
  107.0 0.9 convolution_bitcast_fusion.1
  108.0 0.2 slice-done.1
  108.1 2.4 convolution_bitcast_fusion
  110.5 5.2 %pad_maximum_fusion = f32[16,256,576]{2,1,0:T(8,128)} fusion(f32[16,256,64]{2,1,0:T(8,128)S(1)} %convolution_bitcast_fusion.1, f32[16,256,512]{2,1,0:T(8,128)S(1)} %convolution_bitcast_fusion), kind=kLoop, calls=%fused_computation.8 | loop fusion | flops 2359296 | bytes 18874368 | tf_op jit(solution)/shard_map/concatenate | solution.py:121
  115.7 10.9 %copy.53 = f32[16,256,576]{1,2,0:T(8,128)} copy(f32[16,256,576]{2,1,0:T(8,128)} %pad_maximum_fusion) | data formatting | bytes 18874368 | tf_op jit(solution)/shard_map/concatenate | solution.py:121
  126.6 13.4 %all-gather.3.cloned.1.call-done = bf16[8192,128]{0,1:T(8,128)(2,1)} async-done(((bf16[512,128]{0,1:T(8,128)(2,1)}), bf16[8192,128]{0,1:T(8,128)(2,1)}) %all-gather.3.cloned.1.call-update) | async-done | bytes 2097168 | tf_op jit(solution)/shard_map/all_gather | solution.py:40
  140.1 1.2 collective-permute-start
  141.3 1.5 collective-permute-start.2
  142.8 44.4 %collective-permute-done = bf16[8192,128]{0,1:T(8,128)(2,1)S(1)} collective-permute-done((bf16[8192,128]{0,1:T(8,128)(2,1)}, bf16[8192,128]{0,1:T(8,128)(2,1)S(1)}, u32[]{:S(2)}, u32[]{:S(2)}) %collective-permute-start) | collective-permute-done | bytes 2097184 | tf_op jit(solution)/shard_map/ppermute | solution.py:43
  187.3 3.2 %constant_dynamic-update-slice_fusion.4 = bf16[8192,512]{0,1:T(8,128)(2,1)} fusion(bf16[8192,128]{0,1:T(8,128)(2,1)} %all-gather.3.cloned.1.call-done), kind=kLoop, calls=%fused_computation.34 | loop fusion | bytes 4194304
  190.6 2.7 collective-permute-start.3
  193.4 1.5 constant_dynamic-update-slice_fusion.3
  194.8 16.0 %collective-permute-done.1 = bf16[8192,64]{0,1:T(8,128)(2,1)S(1)} collective-permute-done((bf16[8192,64]{0,1:T(8,128)(2,1)S(1)}, bf16[8192,64]{0,1:T(8,128)(2,1)S(1)}, u32[]{:S(2)}, u32[]{:S(2)}) %collective-permute-start.1) | collective-permute-done | bytes 1048608 | tf_op jit(solution)/shard_map/ppermute | solution.py:46
  210.8 1.0 constant_dynamic-update-slice_fusion.2
  211.9 1.4 collective-permute-done.3
  213.3 1.0 constant_dynamic-update-slice_fusion.1
  214.3 1.5 constant_dynamic-update-slice_fusion
  215.8 3.5 %collective-permute-start.4 = (bf16[8192,512]{0,1:T(8,128)(2,1)}, bf16[8192,512]{0,1:T(8,128)(2,1)}, u32[]{:S(2)}, u32[]{:S(2)}) collective-permute-start(bf16[8192,512]{0,1:T(8,128)(2,1)} %constant_dynamic-update-slice_fusion), channel_id=1, source_target_pairs={{0,16},{16,0},{32,48},{48,32},{64,80},{80,64},{96,112},{112,96},{1... | collective-permute-start | bytes 25165832 | tf_op jit(solution)/shard_map/ppermute | solution.py:51
  219.3 0.1 fusion.2
  219.5 11.5 %convolution_bitcast_fusion.3 = f32[512,512]{0,1:T(8,128)} fusion(bf16[8192,512]{0,1:T(8,128)(2,1)} %constant_dynamic-update-slice_fusion, bf16[512,8192]{1,0:T(8,128)(2,1)} %param.8), kind=kOutput, calls=%fused_computation.15 | convolution fusion | flops 4294967296 | bytes 17825792 | tf_op jit(solution)/shard_map/dot_general | solution.py:52
  231.1 1.3 copy.54
  232.4 0.6 gather_fusion.5
  233.0 1.2 select_select_fusion
  234.2 5.5 %all-to-all-start.1 = ((f32[8,64,576]{2,1,0:T(8,128)}), f32[8,64,576]{2,1,0:T(8,128)}, u32[]{:S(2)}, u32[]{:S(2)}) async-start(f32[8,64,576]{2,1,0:T(8,128)} %select_select_fusion), calls=%async_computation.1 | async-start | bytes 2621440 | tf_op jit(solution)/shard_map/all_to_all | solution.py:130
  239.7 9.6 %convolution_bitcast_fusion.2 = f32[512,512]{0,1:T(8,128)S(1)} fusion(bf16[8192,512]{0,1:T(8,128)(2,1)} %collective-permute-done.4, bf16[512,8192]{1,0:T(8,128)(2,1)} %param.8), kind=kOutput, calls=%fused_computation.14 | convolution fusion | flops 4294967296 | bytes 17825792 | tf_op jit(solution)/shard_map/dot_general | solution.py:53
  249.3 0.2 pad_maximum_fusion.1
  249.5 2.0 gather_fusion
  251.5 1.9 copy.57
  253.5 1.4 add_convert_fusion
  254.9 2.8 %all-to-all-done.1 = f32[8,64,576]{2,1,0:T(8,128)} async-done(((f32[8,64,576]{2,1,0:T(8,128)}), f32[8,64,576]{2,1,0:T(8,128)}, u32[]{:S(2)}, u32[]{:S(2)}) %all-to-all-start.1) | async-done | bytes 1179680 | tf_op jit(solution)/shard_map/all_to_all | solution.py:130
  257.7 1.5 broadcast_select_fusion
  259.2 0.1 slice.40
  259.4 4.5 %broadcast_in_dim.149 = f32[64,64,512]{2,1,0:T(8,128)} broadcast(f32[]{:T(128)} %constant.200.clone.1), dimensions={} | broadcast | bytes 8388612 | tf_op jit(solution)/shard_map/broadcast_in_dim | solution.py:133
  263.9 3.2 %scatter_fusion = f32[64,64,512]{2,1,0:T(8,128)} fusion(f32[64,64,512]{2,1,0:T(8,128)} %broadcast_in_dim.149, s32[8]{0:T(128)S(1)} %get-tuple-element.13, f32[8,64,512]{2,1,0:T(8,128)S(1)} %slice.40), kind=kCustom, calls=%fused_computation.6 | custom fusion | flops 262144 | bytes 3145760 | tf_op jit(solution)/shard_map/scatter-add | solution.py:133
  267.1 0.2 broadcast_in_dim.155
  267.3 0.9 scatter_fusion.1
  268.2 1.3 copy-done.7
  (66 shorter events, 1.2 us)
Async XLA Ops:
  7.2 26.9 %copy-start = (bf16[512,1024]{1,0:T(8,128)(2,1)S(1)}, bf16[512,1024]{1,0:T(8,128)(2,1)}, u32[]{:S(2)}) copy-start(bf16[512,1024]{1,0:T(8,128)(2,1)} %param.9) | copy-start | bytes 3145732
  9.5 25.5 %copy-start.9 = (s32[1,64]{1,0:T(1,128)S(1)}, s32[1,64]{1,0:T(1,128)}, u32[]{:S(2)}) copy-start(s32[1,64]{1,0:T(1,128)} %param.13) | copy-start | bytes 772
  9.5 25.7 %copy-start.4 = (bf16[512,1024]{1,0:T(8,128)(2,1)S(1)}, bf16[512,1024]{1,0:T(8,128)(2,1)}, u32[]{:S(2)}) copy-start(bf16[512,1024]{1,0:T(8,128)(2,1)} %param.12) | copy-start | bytes 3145732
  15.9 16.7 %all-to-all-start = ((bf16[8,64,576]{2,1,0:T(8,128)(2,1)}), bf16[8,64,576]{2,1,0:T(8,128)(2,1)S(1)}, u32[]{:S(2)}, u32[]{:S(2)}) async-start(bf16[8,64,576]{2,1,0:T(8,128)(2,1)} %maximum_select_fusion), calls=%async_computation | async-start | bytes 1310720 | tf_op jit(solution)/shard_map/all_to_all | solution.py:79
  21.7 69.7 %all-gather.5.cloned.1.call-start = ((), (), s32[]{:S(2)}) async-start(), calls=%async_computation.4 | async-start | bytes 5570560 | tf_op jit(solution)/shard_map/all_gather | solution.py:82
  34.1 106.0 %all-gather.3.cloned.1.call-start = ((), (), s32[]{:S(2)}) async-start(), calls=%async_computation.3 | async-start | bytes 2228224 | tf_op jit(solution)/shard_map/all_gather | solution.py:40
  35.0 196.1 %reduce-scatter.4.cloned.1.call-start = ((), (), s32[]{:S(2)}) async-start(), calls=%async_computation.5 | async-start | bytes 10027008
  94.1 9.7 %copy-start.2 = (bf16[256,1024]{1,0:T(8,128)(2,1)}, bf16[256,1024]{1,0:T(8,128)(2,1)S(1)}, u32[]{:S(2)}) copy-start(bf16[256,1024]{1,0:T(8,128)(2,1)S(1)} %reshape_reshape.7) | copy-start | bytes 1572868
  97.0 7.4 %slice-start.2 = ((s8[8388608]{0:T(1024)(128)(4,1)}), s8[4194304]{0:T(1024)(128)(4,1)S(1)}, s32[]{:S(2)}) async-start(s8[8388608]{0:T(1024)(128)(4,1)} %bitcast.108), calls=%async_computation.8 | async-start | bytes 8388608
  99.5 4.4 %copy-start.5 = (bf16[512,1024]{1,0:T(8,128)(2,1)S(1)}, bf16[512,1024]{1,0:T(8,128)(2,1)}, u32[]{:S(2)}) copy-start(bf16[512,1024]{1,0:T(8,128)(2,1)} %param.12) | copy-start | bytes 3145732
  99.5 4.9 %slice-start.3 = ((s8[8388608]{0:T(1024)(128)(4,1)}), s8[4194304]{0:T(1024)(128)(4,1)S(1)}, s32[]{:S(2)}) async-start(s8[8388608]{0:T(1024)(128)(4,1)} %bitcast.108), calls=%async_computation.9 | async-start | bytes 8388608
  104.4 3.6 %slice-start = ((s8[8388608]{0:T(1024)(128)(4,1)}), s8[4194304]{0:T(1024)(128)(4,1)S(1)}, s32[]{:S(2)}) async-start(s8[8388608]{0:T(1024)(128)(4,1)} %bitcast.103), calls=%async_computation.6 | async-start | bytes 8388608
  104.4 2.6 copy-start.6
  104.4 3.7 %slice-start.1 = ((s8[8388608]{0:T(1024)(128)(4,1)}), s8[4194304]{0:T(1024)(128)(4,1)S(1)}, s32[]{:S(2)}) async-start(s8[8388608]{0:T(1024)(128)(4,1)} %bitcast.103), calls=%async_computation.7 | async-start | bytes 8388608
  140.1 47.1 %collective-permute-start = (bf16[8192,128]{0,1:T(8,128)(2,1)}, bf16[8192,128]{0,1:T(8,128)(2,1)S(1)}, u32[]{:S(2)}, u32[]{:S(2)}) collective-permute-start(bf16[8192,128]{0,1:T(8,128)(2,1)} %all-gather.3.cloned.1.call-done), channel_id=1, source_target_pairs={{0,32},{16,48},{32,64},{48,80},{64,96},{80,112},{96,0},{112,16},{1... | collective-permute-start | bytes 6291464 | tf_op jit(solution)/shard_map/ppermute | solution.py:43
  141.3 49.3 %collective-permute-start.2 = (bf16[8192,128]{0,1:T(8,128)(2,1)}, bf16[8192,128]{0,1:T(8,128)(2,1)S(1)}, u32[]{:S(2)}, u32[]{:S(2)}) collective-permute-start(bf16[8192,128]{0,1:T(8,128)(2,1)} %all-gather.3.cloned.1.call-done), channel_id=1, source_target_pairs={{0,96},{16,112},{32,0},{48,16},{64,32},{80,48},{96,64},{112,80},{1... | collective-permute-start | bytes 6291464 | tf_op jit(solution)/shard_map/ppermute | solution.py:44
  187.3 23.6 %collective-permute-start.1 = (bf16[8192,64]{0,1:T(8,128)(2,1)S(1)}, bf16[8192,64]{0,1:T(8,128)(2,1)S(1)}, u32[]{:S(2)}, u32[]{:S(2)}) collective-permute-start(bf16[8192,64]{0,1:T(8,128)(2,1)S(1)} %slice.36), channel_id=1, source_target_pairs={{0,32},{16,48},{32,64},{48,80},{64,96},{80,112},{96,0},{112,16},{1... | collective-permute-start | bytes 3145736 | tf_op jit(solution)/shard_map/ppermute | solution.py:46
  190.6 22.6 %collective-permute-start.3 = (bf16[8192,64]{0,1:T(8,128)(2,1)S(1)}, bf16[8192,64]{0,1:T(8,128)(2,1)S(1)}, u32[]{:S(2)}, u32[]{:S(2)}) collective-permute-start(bf16[8192,64]{0,1:T(8,128)(2,1)S(1)} %slice.37), channel_id=1, source_target_pairs={{0,96},{16,112},{32,0},{48,16},{64,32},{80,48},{96,64},{112,80},{1... | collective-permute-start | bytes 3145736 | tf_op jit(solution)/shard_map/ppermute | solution.py:47
  215.8 23.9 %collective-permute-start.4 = (bf16[8192,512]{0,1:T(8,128)(2,1)}, bf16[8192,512]{0,1:T(8,128)(2,1)}, u32[]{:S(2)}, u32[]{:S(2)}) collective-permute-start(bf16[8192,512]{0,1:T(8,128)(2,1)} %constant_dynamic-update-slice_fusion), channel_id=1, source_target_pairs={{0,16},{16,0},{32,48},{48,32},{64,80},{80,64},{96,112},{112,96},{1... | collective-permute-start | bytes 25165832 | tf_op jit(solution)/shard_map/ppermute | solution.py:51
  234.2 23.5 %all-to-all-start.1 = ((f32[8,64,576]{2,1,0:T(8,128)}), f32[8,64,576]{2,1,0:T(8,128)}, u32[]{:S(2)}, u32[]{:S(2)}) async-start(f32[8,64,576]{2,1,0:T(8,128)} %select_select_fusion), calls=%async_computation.1 | async-start | bytes 2621440 | tf_op jit(solution)/shard_map/all_to_all | solution.py:130
  239.7 9.6 %copy-start.8 = (f32[512,512]{0,1:T(8,128)S(1)}, f32[512,512]{0,1:T(8,128)}, u32[]{:S(2)}) copy-start(f32[512,512]{0,1:T(8,128)} %convolution_bitcast_fusion.3) | copy-start | bytes 3145732
  249.5 3.9 %copy-start.3 = (bf16[256,1024]{1,0:T(8,128)(2,1)S(1)}, bf16[256,1024]{1,0:T(8,128)(2,1)}, u32[]{:S(2)}) copy-start(bf16[256,1024]{1,0:T(8,128)(2,1)} %copy-done.2) | copy-start | bytes 1572868
  259.4 10.2 %copy-start.1 = (bf16[512,1024]{1,0:T(8,128)(2,1)S(1)}, bf16[512,1024]{1,0:T(8,128)(2,1)}, u32[]{:S(2)}) copy-start(bf16[512,1024]{1,0:T(8,128)(2,1)} %param.9) | copy-start | bytes 3145732
  268.2 1.3 copy-start.7
Sparse Core Ops, SparseCore 0:
  34.2 57.1 all-gather.4
  93.5 46.5 all-gather.2
  143.6 86.9 reduce-scatter.3

commit v7 on v6

--- a/solution.py
+++ b/solution.py
@@ -47,8 +47,9 @@
     far_b = lax.ppermute(from_right[:, half_part:], "dp", down_x)
     far = jnp.concatenate([far_a, far_b], axis=1)
     same_parity = [w_part_full, from_left, far, from_right]
+    pair = [(i, i ^ 1) for i in range(dp_count)]
     w_own = jnp.concatenate(same_parity, axis=1)
-    w_partner = lax.ppermute(w_own, "dp", [(i, i ^ 1) for i in range(dp_count)])
+    w_partner = jnp.concatenate([lax.ppermute(p, "dp", pair) for p in same_parity], axis=1)
     out_own = jnp.dot(tokens, w_own, preferred_element_type=f32)
     out_partner = jnp.dot(tokens, w_partner, preferred_element_type=f32)
     held = jnp.concatenate([out_own, out_partner], axis=1).reshape(tok_rows, dp_count, part_cols)

time: 277 us -> 281 us (1.014)
  waiting for transfers between devices: 132 us -> 121 us
  local copies, waits for them, and re-layouts: 65.8 us -> 73.3 us
  starting transfers between devices: 20.3 us -> 24.3 us
  other arithmetic: 15.1 us -> 18 us
    ppermute x1, waiting for transfers between devices: 44.4 us -> 0.01 us  [body(): from_left = lax.ppermute(w_part_full, 'dp', up_x)]
    ppermute x1, waiting for transfers between devices: 0.01 us -> 41.6 us  [body(): from_right = lax.ppermute(w_part_full, 'dp', down_x)]
    ppermute x1, waiting for transfers between devices: 16 us -> 4.45 us  [body(): far_a = lax.ppermute(from_left[:, :half_part], 'dp', up_x)]
    ppermute x1, waiting for transfers between devices: 1.41 us -> 11.2 us  [body(): far_b = lax.ppermute(from_right[:, half_part:], 'dp', down_x)]
    all_gather x1, waiting for transfers between devices: 13.4 us -> 5.35 us  [body(): w_part_full = lax.all_gather(w_part, 'fsdp', axis=0, tiled=True)]
    dot_general x1, matrix products: 2.36 us -> 7.2 us  [body(): lax.dot_general(tokens, down_flat, (((1,), (1,)), ((), ())), preferred_el...]
    ppermute x1 -> x4, starting transfers between devices: 3.47 us -> 8.18 us  [body(): lax.ppermute(p, 'dp', pair)]
    dot_general x1, matrix products: 11.5 us -> 8.23 us  [body(): out_own = jnp.dot(tokens, w_own, preferred_element_type=f32)]
  transfers between devices with their start and end apart: 10 -> 13, of which waited for: 7 -> 7; matrix products, arithmetic and copies ran while one was open for 32% -> 35% of each run, Pallas kernels for 0% -> 0%
where the time goes in v7:
time: 281 us; the launch traced here: 280 us
  waiting for transfers between devices  121 us (43%)
  local copies, waits for them, and re-layouts  73.3 us (26%)
  matrix products  28.9 us (10%)
  starting transfers between devices  24.3 us (9%)
  other arithmetic  18 us (6%)
  between operations  14.2 us (5%)
    all_gather x1, waiting for transfers between devices, body(): shares = lax.all_gather(slab, 'fsdp', axis=0, tiled=False)  43.6 us
    ppermute x1, waiting for transfers between devices, body(): from_right = lax.ppermute(w_part_full, 'dp', down_x)  41.6 us
    unnamed x36, local copies, waits for them, and re-layouts  15.5 us
    dot_general x1, local copies, waits for them, and re-layouts, body(): lax.dot_general(masked_back, tokens, contract, preferred_element_type=f32)  12 us
    ppermute x1, waiting for transfers between devices, body(): far_b = lax.ppermute(from_right[:, half_part:], 'dp', down_x)  11.2 us
    concatenate x1, local copies, waits for them, and re-layouts, body(): jnp.concatenate([part_down, part_up], axis=2)  10.9 us
    all_to_all x1, waiting for transfers between devices, body(): got = lax.all_to_all(send, 'dp', split_axis=0, concat_axis=0, tiled=True)  10.9 us
    dot_general x1, matrix products, body(): out_partner = jnp.dot(tokens, w_partner, preferred_element_type=f32)  8.31 us
  transfers between devices with their start and end apart: 13, of which 7 were waited for; matrix products, arithmetic and copies ran while one was open for 35% of the time, Pallas kernels for 0%

profile of v7, /device:TPU:1, one launch (start us, length us, event | category | flops | bytes accessed | tf_op | source)
XLA Modules:
  0.0 279.9 jit_solution(8043532204003902921)
XLA Ops:
  7.2 0.8 copy.44
  8.1 1.4 gather_fusion.1
  9.6 0.1 fusion.31
  9.7 0.1 fusion.12
  10.0 1.8 gather_fusion.3
  11.8 2.8 gather_fusion.2
  14.7 0.1 broadcast_select_fusion.1
  14.8 1.1 maximum_select_fusion
  15.9 5.8 %all-to-all-start = ((bf16[8,64,576]{2,1,0:T(8,128)(2,1)}), bf16[8,64,576]{2,1,0:T(8,128)(2,1)S(1)}, u32[]{:S(2)}, u32[]{:S(2)}) async-start(bf16[8,64,576]{2,1,0:T(8,128)(2,1)} %maximum_select_fusion), calls=%async_computation | async-start | bytes 1310720 | tf_op jit(solution)/shard_map/all_to_all | solution.py:80
  21.7 10.9 %all-to-all-done = bf16[8,64,576]{2,1,0:T(8,128)(2,1)S(1)} async-done(((bf16[8,64,576]{2,1,0:T(8,128)(2,1)}), bf16[8,64,576]{2,1,0:T(8,128)(2,1)S(1)}, u32[]{:S(2)}, u32[]{:S(2)}) %all-to-all-start) | async-done | bytes 589856 | tf_op jit(solution)/shard_map/all_to_all | solution.py:80
  32.6 0.6 gather_fusion.4
  33.2 0.8 bitcast_select_fusion
  34.2 0.8 copy.60
  35.3 0.5 copy.50
  35.8 12.0 %copy.58 = bf16[8192,512]{1,0:T(8,128)(2,1)} copy(bf16[8192,512]{0,1:T(8,128)(2,1)} %bitcast.106) | data formatting | bytes 16777216 | tf_op jit(solution)/shard_map/dot_general | solution.py:114
  47.8 43.6 %all-gather.5.cloned.1.call-done = bf16[16,4,64,576]{3,2,1,0:T(8,128)(2,1)} async-done(((bf16[1,4,64,576]{3,2,1,0:T(8,128)(2,1)}), bf16[16,4,64,576]{3,2,1,0:T(8,128)(2,1)}) %all-gather.5.cloned.1.call-update) | async-done | bytes 4718608 | tf_op jit(solution)/shard_map/all_gather | solution.py:83
  91.4 2.7 slice_bitcast_fusion
  94.1 2.4 copy.47
  96.5 6.3 %copy.62 = bf16[32,8,16,512]{3,1,2,0:T(8,128)(2,1)} copy(bf16[32,8,16,512]{3,2,1,0:T(8,128)(2,1)S(1)} %bitcast.105) | data formatting | bytes 8388608
  102.8 1.3 slice_bitcast_fusion.1
  104.2 1.7 copy.48
  105.8 2.1 reshape_reshape.7
  108.0 0.5 fusion.33
  108.5 7.2 %fusion.32 = f32[256,512]{1,0:T(8,128)S(1)} fusion(bf16[256,8192]{1,0:T(8,128)(2,1)} %bitcast.112, bf16[512,8192]{1,0:T(8,128)(2,1)} %param.8), kind=kOutput, calls=%fused_computation.134 | convolution fusion | flops 2147483648 | bytes 13107200 | tf_op jit(solution)/shard_map/dot_general | solution.py:97
  115.7 0.1 multiply_reduce_fusion
  115.9 0.7 convolution_bitcast_fusion.1
  116.7 2.5 convolution_bitcast_fusion
  119.2 5.2 %pad_maximum_fusion = f32[16,256,576]{2,1,0:T(8,128)} fusion(f32[16,256,64]{2,1,0:T(8,128)S(1)} %convolution_bitcast_fusion.1, f32[16,256,512]{2,1,0:T(8,128)S(1)} %convolution_bitcast_fusion), kind=kLoop, calls=%fused_computation.8 | loop fusion | flops 2359296 | bytes 18874368 | tf_op jit(solution)/shard_map/concatenate | solution.py:122
  124.4 10.9 %copy.53 = f32[16,256,576]{1,2,0:T(8,128)} copy(f32[16,256,576]{2,1,0:T(8,128)} %pad_maximum_fusion) | data formatting | bytes 18874368 | tf_op jit(solution)/shard_map/concatenate | solution.py:122
  135.3 5.4 %all-gather.3.cloned.1.call-done = bf16[8192,128]{0,1:T(8,128)(2,1)} async-done(((bf16[512,128]{0,1:T(8,128)(2,1)}), bf16[8192,128]{0,1:T(8,128)(2,1)}) %all-gather.3.cloned.1.call-update) | async-done | bytes 2097168 | tf_op jit(solution)/shard_map/all_gather | solution.py:40
  140.7 2.4 collective-permute-start.2
  143.1 0.1 fusion.13
  143.4 1.8 collective-permute-start.4
  145.2 41.6 %collective-permute-done.2 = bf16[8192,128]{0,1:T(8,128)(2,1)} collective-permute-done((bf16[8192,128]{0,1:T(8,128)(2,1)}, bf16[8192,128]{0,1:T(8,128)(2,1)}, u32[]{:S(2)}, u32[]{:S(2)}) %collective-permute-start.2) | collective-permute-done | bytes 2097184 | tf_op jit(solution)/shard_map/ppermute | solution.py:44
  186.8 1.3 slice.37
  188.1 3.6 %collective-permute-start.3 = (bf16[8192,64]{0,1:T(8,128)(2,1)S(1)}, bf16[8192,64]{0,1:T(8,128)(2,1)S(1)}, u32[]{:S(2)}, u32[]{:S(2)}) collective-permute-start(bf16[8192,64]{0,1:T(8,128)(2,1)S(1)} %slice.37), channel_id=1, source_target_pairs={{0,96},{16,112},{32,0},{48,16},{64,32},{80,48},{96,64},{112,80},{1... | collective-permute-start | bytes 3145736 | tf_op jit(solution)/shard_map/ppermute | solution.py:47
  191.7 1.3 slice.36
  193.1 1.5 constant_dynamic-update-slice_fusion.4
  194.5 2.7 collective-permute-start.7
  197.2 3.3 %constant_dynamic-update-slice_fusion.3 = bf16[8192,512]{0,1:T(8,128)(2,1)} fusion(bf16[8192,512]{0,1:T(8,128)(2,1)} %constant_dynamic-update-slice_fusion.4, bf16[8192,128]{0,1:T(8,128)(2,1)} %collective-permute-done), kind=kLoop, calls=%fused_computation.42 | loop fusion | bytes 4194304
  200.5 11.2 %collective-permute-done.3 = bf16[8192,64]{0,1:T(8,128)(2,1)S(1)} collective-permute-done((bf16[8192,64]{0,1:T(8,128)(2,1)S(1)}, bf16[8192,64]{0,1:T(8,128)(2,1)S(1)}, u32[]{:S(2)}, u32[]{:S(2)}) %collective-permute-start.3) | collective-permute-done | bytes 1048608 | tf_op jit(solution)/shard_map/ppermute | solution.py:47
  211.7 4.4 %collective-permute-done.1 = bf16[8192,64]{0,1:T(8,128)(2,1)S(1)} collective-permute-done((bf16[8192,64]{0,1:T(8,128)(2,1)S(1)}, bf16[8192,64]{0,1:T(8,128)(2,1)S(1)}, u32[]{:S(2)}, u32[]{:S(2)}) %collective-permute-start.1) | collective-permute-done | bytes 1048608 | tf_op jit(solution)/shard_map/ppermute | solution.py:46
  216.2 1.5 pad_maximum_fusion.1
  217.7 3.6 %collective-permute-start.6 = (bf16[8192,128]{0,1:T(8,128)(2,1)}, bf16[8192,128]{0,1:T(8,128)(2,1)}, u32[]{:S(2)}, u32[]{:S(2)}) collective-permute-start(bf16[8192,128]{0,1:T(8,128)(2,1)} %pad_maximum_fusion.1), channel_id=1, source_target_pairs={{0,16},{16,0},{32,48},{48,32},{64,80},{80,64},{96,112},{112,96},{1... | collective-permute-start | bytes 6291464 | tf_op jit(solution)/shard_map/ppermute | solution.py:52
  221.3 1.0 constant_dynamic-update-slice_fusion.2
  222.4 1.0 constant_dynamic-update-slice_fusion.1
  223.4 3.1 %constant_dynamic-update-slice_fusion = bf16[8192,512]{0,1:T(8,128)(2,1)} fusion(bf16[8192,512]{0,1:T(8,128)(2,1)} %constant_dynamic-update-slice_fusion.1, bf16[8192,128]{0,1:T(8,128)(2,1)} %collective-permute-done.2), kind=kLoop, calls=%fused_computation.39 | loop fusion | bytes 4194304 | tf_op jit(solution)/shard_map/concatenate | solution.py:51
  226.5 8.2 %convolution_bitcast_fusion.2 = f32[512,512]{0,1:T(8,128)} fusion(bf16[8192,512]{0,1:T(8,128)(2,1)} %constant_dynamic-update-slice_fusion, bf16[512,8192]{1,0:T(8,128)(2,1)S(1)} %bitcast.108), kind=kOutput, calls=%fused_computation.24 | convolution fusion | flops 4294967296 | bytes 17825792 | tf_op jit(solution)/shard_map/dot_general | solution.py:53
  234.8 1.3 copy.54
  236.1 0.6 gather_fusion.5
  236.7 1.2 select_select_fusion
  237.9 4.2 %all-to-all-start.1 = ((f32[8,64,576]{2,1,0:T(8,128)}), f32[8,64,576]{2,1,0:T(8,128)}, u32[]{:S(2)}, u32[]{:S(2)}) async-start(f32[8,64,576]{2,1,0:T(8,128)} %select_select_fusion), calls=%async_computation.1 | async-start | bytes 2621440 | tf_op jit(solution)/shard_map/all_to_all | solution.py:131
  242.2 8.3 %fusion.8 = f32[512,512]{0,1:T(8,128)S(1)} fusion(bf16[512,8192]{1,0:T(8,128)(2,1)} %param.8, bf16[8192,128]{0,1:T(8,128)(2,1)} %collective-permute-done.7, bf16[8192,128]{0,1:T(8,128)(2,1)} %collective-permute-done.6, bf16[8192,128]{0,1:T(8,128)(2,1)} %collective-permute-done.5, bf16[8192,128]{0,1:T(8,128)(2,1)} %collective-permute-done.4), kind=kOutput, calls=%fused_computation.23 | convolution fusion | flops 4328521728 | bytes 17825792 | tf_op jit(solution)/shard_map/dot_general | solution.py:54
  250.5 0.2 pad_maximum_fusion.2
  250.7 2.0 gather_fusion
  252.7 1.9 copy.57
  254.7 1.4 add_convert_fusion
  256.1 4.1 %all-to-all-done.1 = f32[8,64,576]{2,1,0:T(8,128)} async-done(((f32[8,64,576]{2,1,0:T(8,128)}), f32[8,64,576]{2,1,0:T(8,128)}, u32[]{:S(2)}, u32[]{:S(2)}) %all-to-all-start.1) | async-done | bytes 1179680 | tf_op jit(solution)/shard_map/all_to_all | solution.py:131
  260.2 1.5 broadcast_select_fusion
  261.7 0.1 slice.40
  261.8 1.6 broadcast_in_dim.155
  263.4 2.3 scatter_fusion.1
  265.7 4.5 %broadcast_in_dim.149 = f32[64,64,512]{2,1,0:T(8,128)} broadcast(f32[]{:T(128)} %constant.200.clone.1), dimensions={} | broadcast | bytes 8388612 | tf_op jit(solution)/shard_map/broadcast_in_dim | solution.py:134
  270.2 3.2 %scatter_fusion = f32[64,64,512]{2,1,0:T(8,128)} fusion(f32[64,64,512]{2,1,0:T(8,128)} %broadcast_in_dim.149, s32[8]{0:T(128)S(1)} %get-tuple-element.13, f32[8,64,512]{2,1,0:T(8,128)S(1)} %slice.40), kind=kCustom, calls=%fused_computation.6 | custom fusion | flops 262144 | bytes 3145760 | tf_op jit(solution)/shard_map/scatter-add | solution.py:134
  (69 shorter events, 1.2 us)
Async XLA Ops:
  7.2 26.9 %copy-start = (bf16[512,1024]{1,0:T(8,128)(2,1)S(1)}, bf16[512,1024]{1,0:T(8,128)(2,1)}, u32[]{:S(2)}) copy-start(bf16[512,1024]{1,0:T(8,128)(2,1)} %param.9) | copy-start | bytes 3145732
  9.5 25.5 %copy-start.7 = (s32[1,64]{1,0:T(1,128)S(1)}, s32[1,64]{1,0:T(1,128)}, u32[]{:S(2)}) copy-start(s32[1,64]{1,0:T(1,128)} %param.13) | copy-start | bytes 772
  9.5 25.7 %copy-start.4 = (bf16[512,1024]{1,0:T(8,128)(2,1)S(1)}, bf16[512,1024]{1,0:T(8,128)(2,1)}, u32[]{:S(2)}) copy-start(bf16[512,1024]{1,0:T(8,128)(2,1)} %param.12) | copy-start | bytes 3145732
  15.9 16.7 %all-to-all-start = ((bf16[8,64,576]{2,1,0:T(8,128)(2,1)}), bf16[8,64,576]{2,1,0:T(8,128)(2,1)S(1)}, u32[]{:S(2)}, u32[]{:S(2)}) async-start(bf16[8,64,576]{2,1,0:T(8,128)(2,1)} %maximum_select_fusion), calls=%async_computation | async-start | bytes 1310720 | tf_op jit(solution)/shard_map/all_to_all | solution.py:80
  21.7 69.7 %all-gather.5.cloned.1.call-start = ((), (), s32[]{:S(2)}) async-start(), calls=%async_computation.4 | async-start | bytes 5570560 | tf_op jit(solution)/shard_map/all_gather | solution.py:83
  34.0 106.6 %all-gather.3.cloned.1.call-start = ((), (), s32[]{:S(2)}) async-start(), calls=%async_computation.3 | async-start | bytes 2228224 | tf_op jit(solution)/shard_map/all_gather | solution.py:40
  35.0 199.8 %reduce-scatter.4.cloned.1.call-start = ((), (), s32[]{:S(2)}) async-start(), calls=%async_computation.5 | async-start | bytes 10027008
  108.0 7.7 %copy-start.2 = (bf16[256,1024]{1,0:T(8,128)(2,1)}, bf16[256,1024]{1,0:T(8,128)(2,1)S(1)}, u32[]{:S(2)}) copy-start(bf16[256,1024]{1,0:T(8,128)(2,1)S(1)} %reshape_reshape.7) | copy-start | bytes 1572868
  108.4 8.2 %slice-start = ((s8[8388608]{0:T(1024)(128)(4,1)}), s8[4194304]{0:T(1024)(128)(4,1)S(1)}, s32[]{:S(2)}) async-start(s8[8388608]{0:T(1024)(128)(4,1)} %bitcast.102), calls=%async_computation.6 | async-start | bytes 8388608
  108.5 8.2 %slice-start.1 = ((s8[8388608]{0:T(1024)(128)(4,1)}), s8[4194304]{0:T(1024)(128)(4,1)S(1)}, s32[]{:S(2)}) async-start(s8[8388608]{0:T(1024)(128)(4,1)} %bitcast.102), calls=%async_computation.7 | async-start | bytes 8388608
  140.7 52.4 %copy-start.5 = (bf16[8192,128]{0,1:T(8,128)(2,1)S(1)}, bf16[8192,128]{0,1:T(8,128)(2,1)}, u32[]{:S(2)}) copy-start(bf16[8192,128]{0,1:T(8,128)(2,1)} %all-gather.3.cloned.1.call-done) | copy-start | bytes 6291460
  140.7 46.1 %collective-permute-start.2 = (bf16[8192,128]{0,1:T(8,128)(2,1)}, bf16[8192,128]{0,1:T(8,128)(2,1)}, u32[]{:S(2)}, u32[]{:S(2)}) collective-permute-start(bf16[8192,128]{0,1:T(8,128)(2,1)} %all-gather.3.cloned.1.call-done), channel_id=1, source_target_pairs={{0,96},{16,112},{32,0},{48,16},{64,32},{80,48},{96,64},{112,80},{1... | collective-permute-start | bytes 6291464 | tf_op jit(solution)/shard_map/ppermute | solution.py:44
  143.1 48.6 %collective-permute-start = (bf16[8192,128]{0,1:T(8,128)(2,1)}, bf16[8192,128]{0,1:T(8,128)(2,1)}, u32[]{:S(2)}, u32[]{:S(2)}) collective-permute-start(bf16[8192,128]{0,1:T(8,128)(2,1)} %all-gather.3.cloned.1.call-done), channel_id=1, source_target_pairs={{0,32},{16,48},{32,64},{48,80},{64,96},{80,112},{96,0},{112,16},{1... | collective-permute-start | bytes 6291464 | tf_op jit(solution)/shard_map/ppermute | solution.py:43
  143.4 98.8 %collective-permute-start.4 = (bf16[8192,128]{0,1:T(8,128)(2,1)}, bf16[8192,128]{0,1:T(8,128)(2,1)}, u32[]{:S(2)}, u32[]{:S(2)}) collective-permute-start(bf16[8192,128]{0,1:T(8,128)(2,1)} %all-gather.3.cloned.1.call-done), channel_id=1, source_target_pairs={{0,16},{16,0},{32,48},{48,32},{64,80},{80,64},{96,112},{112,96},{1... | collective-permute-start | bytes 6291464 | tf_op jit(solution)/shard_map/ppermute | solution.py:52
  188.1 23.6 %collective-permute-start.3 = (bf16[8192,64]{0,1:T(8,128)(2,1)S(1)}, bf16[8192,64]{0,1:T(8,128)(2,1)S(1)}, u32[]{:S(2)}, u32[]{:S(2)}) collective-permute-start(bf16[8192,64]{0,1:T(8,128)(2,1)S(1)} %slice.37), channel_id=1, source_target_pairs={{0,96},{16,112},{32,0},{48,16},{64,32},{80,48},{96,64},{112,80},{1... | collective-permute-start | bytes 3145736 | tf_op jit(solution)/shard_map/ppermute | solution.py:47
  193.0 23.2 %collective-permute-start.1 = (bf16[8192,64]{0,1:T(8,128)(2,1)S(1)}, bf16[8192,64]{0,1:T(8,128)(2,1)S(1)}, u32[]{:S(2)}, u32[]{:S(2)}) collective-permute-start(bf16[8192,64]{0,1:T(8,128)(2,1)S(1)} %slice.36), channel_id=1, source_target_pairs={{0,32},{16,48},{32,64},{48,80},{64,96},{80,112},{96,0},{112,16},{1... | collective-permute-start | bytes 3145736 | tf_op jit(solution)/shard_map/ppermute | solution.py:46
  194.5 47.7 %collective-permute-start.7 = (bf16[8192,128]{0,1:T(8,128)(2,1)}, bf16[8192,128]{0,1:T(8,128)(2,1)}, u32[]{:S(2)}, u32[]{:S(2)}) collective-permute-start(bf16[8192,128]{0,1:T(8,128)(2,1)} %collective-permute-done.2), channel_id=1, source_target_pairs={{0,16},{16,0},{32,48},{48,32},{64,80},{80,64},{96,112},{112,96},{1... | collective-permute-start | bytes 6291464 | tf_op jit(solution)/shard_map/ppermute | solution.py:52
  197.2 45.0 %collective-permute-start.5 = (bf16[8192,128]{0,1:T(8,128)(2,1)}, bf16[8192,128]{0,1:T(8,128)(2,1)}, u32[]{:S(2)}, u32[]{:S(2)}) collective-permute-start(bf16[8192,128]{0,1:T(8,128)(2,1)} %collective-permute-done), channel_id=1, source_target_pairs={{0,16},{16,0},{32,48},{48,32},{64,80},{80,64},{96,112},{112,96},{1... | collective-permute-start | bytes 6291464 | tf_op jit(solution)/shard_map/ppermute | solution.py:52
  197.2 29.3 %slice-start.2 = ((s8[8388608]{0:T(1024)(128)(4,1)}), s8[4194304]{0:T(1024)(128)(4,1)S(1)}, s32[]{:S(2)}) async-start(s8[8388608]{0:T(1024)(128)(4,1)} %bitcast.107), calls=%async_computation.8 | async-start | bytes 8388608
  217.7 8.8 %slice-start.3 = ((s8[8388608]{0:T(1024)(128)(4,1)}), s8[4194304]{0:T(1024)(128)(4,1)S(1)}, s32[]{:S(2)}) async-start(s8[8388608]{0:T(1024)(128)(4,1)} %bitcast.107), calls=%async_computation.9 | async-start | bytes 8388608
  217.7 24.5 %collective-permute-start.6 = (bf16[8192,128]{0,1:T(8,128)(2,1)}, bf16[8192,128]{0,1:T(8,128)(2,1)}, u32[]{:S(2)}, u32[]{:S(2)}) collective-permute-start(bf16[8192,128]{0,1:T(8,128)(2,1)} %pad_maximum_fusion.1), channel_id=1, source_target_pairs={{0,16},{16,0},{32,48},{48,32},{64,80},{80,64},{96,112},{112,96},{1... | collective-permute-start | bytes 6291464 | tf_op jit(solution)/shard_map/ppermute | solution.py:52
  237.9 22.2 %all-to-all-start.1 = ((f32[8,64,576]{2,1,0:T(8,128)}), f32[8,64,576]{2,1,0:T(8,128)}, u32[]{:S(2)}, u32[]{:S(2)}) async-start(f32[8,64,576]{2,1,0:T(8,128)} %select_select_fusion), calls=%async_computation.1 | async-start | bytes 2621440 | tf_op jit(solution)/shard_map/all_to_all | solution.py:131
  242.2 8.4 %copy-start.6 = (f32[512,512]{0,1:T(8,128)S(1)}, f32[512,512]{0,1:T(8,128)}, u32[]{:S(2)}) copy-start(f32[512,512]{0,1:T(8,128)} %convolution_bitcast_fusion.2) | copy-start | bytes 3145732
  250.7 3.9 %copy-start.3 = (bf16[256,1024]{1,0:T(8,128)(2,1)S(1)}, bf16[256,1024]{1,0:T(8,128)(2,1)}, u32[]{:S(2)}) copy-start(bf16[256,1024]{1,0:T(8,128)(2,1)} %copy-done.2) | copy-start | bytes 1572868
  263.4 10.0 %copy-start.1 = (bf16[512,1024]{1,0:T(8,128)(2,1)S(1)}, bf16[512,1024]{1,0:T(8,128)(2,1)}, u32[]{:S(2)}) copy-start(bf16[512,1024]{1,0:T(8,128)(2,1)} %param.9) | copy-start | bytes 3145732
Sparse Core Ops, SparseCore 0:
  34.2 57.1 all-gather.4
  94.1 46.5 all-gather.2
  144.1 86.3 reduce-scatter.3

commit v8 on v6

--- a/solution.py
+++ b/solution.py
@@ -115,26 +115,38 @@
         scaled_masked_low, value_output_gradient, contract, preferred_element_type=f32
     )
     rows = list_len * rank
-    part_down = part_down.reshape(rows, fsdp_count, down_cols).transpose(1, 0, 2)
-    part_up = part_up.reshape(rows, fsdp_count, up_cols).transpose(1, 0, 2)
-    summed = lax.psum_scatter(
-        jnp.concatenate([part_down, part_up], axis=2), "fsdp", scatter_dimension=0, tiled=True
-    )[0]
+    up_rows = rows * up_cols // down_cols
+    up_as_rows = (
+        part_up.reshape(rows, fsdp_count, up_cols)
+        .transpose(1, 0, 2)
+        .reshape(fsdp_count, up_rows, down_cols)
+        .transpose(1, 0, 2)
+        .reshape(up_rows, fsdp_count * down_cols)
+    )
+    both = jnp.concatenate([part_down, up_as_rows], axis=0)
+    summed = lax.psum_scatter(both, "fsdp", scatter_dimension=1, tiled=True)
+    per_slot = jnp.concatenate(
+        [
+            summed[:rows].reshape(list_len, rank, down_cols),
+            summed[rows:].reshape(list_len, up_rows // list_len, down_cols),
+        ],
+        axis=1,
+    )
 
     owner_range = jnp.arange(dp_count, dtype=jnp.int32)
     to_owner = my_owner[None, :] == owner_range[:, None]
     pick_index = jnp.sum(jnp.where(to_owner, slot_range[None, :], 0), axis=1)
     owner_has = jnp.any(to_owner, axis=1)
-    send_grad = jnp.take(summed.reshape(list_len, rank, down_cols + up_cols), pick_index, axis=0)
+    send_grad = jnp.take(per_slot, pick_index, axis=0)
     send_grad = jnp.where(owner_has[:, None, None], send_grad, 0.0)
     back_grad = lax.all_to_all(send_grad, "dp", split_axis=0, concat_axis=0, tiled=True)
     land = jnp.where(owned_any, locally_owned_slots, 0)
     arrived = jnp.where(owned_any[:, None, None], back_grad, 0.0)
     grad_down = jnp.zeros((each_owner_rows, rank, down_cols), f32).at[land].add(
-        arrived[:, :, :down_cols]
+        arrived[:, :rank]
     )
     grad_up = jnp.zeros((each_owner_rows, rank, up_cols), f32).at[land].add(
-        arrived[:, :, down_cols:]
+        arrived[:, rank:].reshape(dp_count, rank, up_cols)
     )
     return (value, grad_down, grad_up)
 

time: 277 us -> 277 us (level)
  local copies, waits for them, and re-layouts: 65.8 us -> 48.5 us
  waiting for transfers between devices: 132 us -> 139 us
  matrix products: 28.7 us -> 35.2 us
  other arithmetic: 15.1 us -> 19 us
    all_gather x1, waiting for transfers between devices: 42.9 us -> 55.6 us  [body(): shares = lax.all_gather(slab, 'fsdp', axis=0, tiled=False)]
    dot_general x1 -> x0, local copies, waits for them, and re-layouts: 11.9 us -> none  [body(): lax.dot_general(masked_back, tokens, contract, preferred_element_type=f32)]
    concatenate x1 -> x0, local copies, waits for them, and re-layouts: 10.9 us -> none  [body(): jnp.concatenate([part_down, part_up], axis=2)]
    dot_general x1, matrix products: 2.37 us -> 9.36 us  [body(): lax.dot_general(masked_back, tokens, contract, preferred_element_type=f32)]
    all_gather x1, waiting for transfers between devices: 13.4 us -> 9.21 us  [body(): w_part_full = lax.all_gather(w_part, 'fsdp', axis=0, tiled=True)]
    reshape x0 -> x4, local copies, waits for them, and re-layouts: none -> 3.74 us  [the longest x2 2.79 us: body(): up_as_rows = part_up.reshape(rows, fsdp_count, up_cols).transpose(1, 0, 2...]
    concatenate x1 -> x2, other arithmetic: 5.19 us -> 8.25 us  [the longest x1 8.21 us: body(): both = jnp.concatenate([part_down, up_as_rows], axis=0)]
    unnamed x40 -> x34, local copies, waits for them, and re-layouts: 15.8 us -> 14.8 us
  transfers between devices with their start and end apart: 10 -> 10, of which waited for: 7 -> 7; matrix products, arithmetic and copies ran while one was open for 32% -> 29% of each run, Pallas kernels for 0% -> 0%
where the time goes in v8:
time: 277 us; the launch traced here: 276 us
  waiting for transfers between devices  139 us (50%)
  local copies, waits for them, and re-layouts  48.5 us (18%)
  matrix products  35.2 us (13%)
  starting transfers between devices  20 us (7%)
  other arithmetic  19 us (7%)
  between operations  14.2 us (5%)
    all_gather x1, waiting for transfers between devices, body(): shares = lax.all_gather(slab, 'fsdp', axis=0, tiled=False)  55.6 us
    ppermute x1, waiting for transfers between devices, body(): from_left = lax.ppermute(w_part_full, 'dp', up_x)  44.4 us
    ppermute x1, waiting for transfers between devices, body(): far_a = lax.ppermute(from_left[:, :half_part], 'dp', up_x)  16 us
    unnamed x34, local copies, waits for them, and re-layouts  14.8 us
    dot_general x1, matrix products, body(): out_own = jnp.dot(tokens, w_own, preferred_element_type=f32)  11.5 us
    all_to_all x1, waiting for transfers between devices, body(): got = lax.all_to_all(send, 'dp', split_axis=0, concat_axis=0, tiled=True)  10.9 us
    dot_general x1, matrix products, body(): out_partner = jnp.dot(tokens, w_partner, preferred_element_type=f32)  9.59 us
    dot_general x1, matrix products, body(): lax.dot_general(masked_back, tokens, contract, preferred_element_type=f32)  9.36 us
  transfers between devices with their start and end apart: 10, of which 7 were waited for; matrix products, arithmetic and copies ran while one was open for 29% of the time, Pallas kernels for 0%

profile of v8, /device:TPU:1, one launch (start us, length us, event | category | flops | bytes accessed | tf_op | source)
XLA Modules:
  0.0 275.8 jit_solution(16079173203989045500)
XLA Ops:
  7.2 0.8 copy.29
  8.1 1.4 gather_fusion.1
  9.6 0.1 fusion.19
  9.7 0.1 fusion.1
  9.9 0.1 select_reduce_fusion
  10.0 1.8 gather_fusion.3
  11.8 2.8 %gather_fusion.2 = bf16[8,64,512]{2,1,0:T(8,128)(2,1)S(1)} fusion(bf16[64,64,512]{2,1,0:T(8,128)(2,1)} %param.10, s32[1024]{0:T(1024)S(1)} %pad_clamp_fusion.2), kind=kCustom, calls=%fused_computation.2 | custom fusion | bytes 1048608 | tf_op jit(solution)/shard_map/jit(_take)/gather | solution.py:73
  14.7 0.1 broadcast_select_fusion.1
  14.8 1.1 maximum_select_fusion
  15.9 5.8 %all-to-all-start = ((bf16[8,64,576]{2,1,0:T(8,128)(2,1)}), bf16[8,64,576]{2,1,0:T(8,128)(2,1)S(1)}, u32[]{:S(2)}, u32[]{:S(2)}) async-start(bf16[8,64,576]{2,1,0:T(8,128)(2,1)} %maximum_select_fusion), calls=%async_computation | async-start | bytes 1310720 | tf_op jit(solution)/shard_map/all_to_all | solution.py:79
  21.7 10.9 %all-to-all-done = bf16[8,64,576]{2,1,0:T(8,128)(2,1)S(1)} async-done(((bf16[8,64,576]{2,1,0:T(8,128)(2,1)}), bf16[8,64,576]{2,1,0:T(8,128)(2,1)S(1)}, u32[]{:S(2)}, u32[]{:S(2)}) %all-to-all-start) | async-done | bytes 589856 | tf_op jit(solution)/shard_map/all_to_all | solution.py:79
  32.6 0.6 gather_fusion.4
  33.2 0.8 bitcast_select_fusion
  34.2 0.8 copy.41
  35.3 0.5 copy.34
  35.8 55.6 %all-gather.5.cloned.1.call-done = bf16[16,4,64,576]{3,2,1,0:T(8,128)(2,1)} async-done(((bf16[1,4,64,576]{3,2,1,0:T(8,128)(2,1)}), bf16[16,4,64,576]{3,2,1,0:T(8,128)(2,1)}) %all-gather.5.cloned.1.call-update) | async-done | bytes 4718608 | tf_op jit(solution)/shard_map/all_gather | solution.py:82
  91.4 1.3 slice_bitcast_fusion.1
  92.7 1.7 copy.33
  94.4 2.1 reshape_reshape.7
  96.5 2.9 %slice_bitcast_fusion = bf16[4,64,16,512]{3,1,0,2:T(8,128)(2,1)S(1)} fusion(bf16[16,4,64,576]{3,2,1,0:T(8,128)(2,1)} %all-gather.5.cloned.1.call-done), kind=kLoop, calls=%fused_computation.9 | loop fusion | bytes 8388608 | tf_op jit(solution)/shard_map/transpose | solution.py:83
  99.4 0.5 fusion.21
  99.9 2.4 copy.32
  102.3 4.4 %copy.44 = bf16[32,8,16,512]{3,1,2,0:T(8,128)(2,1)S(1)} copy(bf16[32,8,16,512]{3,2,1,0:T(8,128)(2,1)S(1)} %bitcast.101) | data formatting | bytes 8388608
  106.7 2.4 fusion.20
  109.1 0.1 multiply_reduce_fusion
  109.3 0.8 broadcast_multiply_fusion
  110.0 0.5 convolution_bitcast_fusion
  110.5 0.6 copy.36
  111.1 1.5 reshape.428
  112.6 1.3 copy.42
  113.9 9.4 %fusion.22 = f32[256,8192]{1,0:T(8,128)} fusion(bf16[512,256]{0,1:T(8,128)(2,1)S(1)} %bitcast.112, bf16[512,8192]{1,0:T(8,128)(2,1)} %param.8), kind=kOutput, calls=%fused_computation.127 | convolution fusion | flops 2147483648 | bytes 17039360 | tf_op jit(solution)/shard_map/dot_general | solution.py:113
  123.3 8.2 %pad_maximum_fusion = f32[288,8192]{1,0:T(8,128)} fusion(f32[32,8192]{1,0:T(8,128)S(1)} %bitcast.107, f32[256,8192]{1,0:T(8,128)} %fusion.22), kind=kLoop, calls=%fused_computation.8 | loop fusion | flops 2359296 | bytes 18874368 | tf_op jit(solution)/shard_map/concatenate | solution.py:126
  131.5 9.2 %all-gather.3.cloned.1.call-done = bf16[8192,128]{0,1:T(8,128)(2,1)} async-done(((bf16[512,128]{0,1:T(8,128)(2,1)}), bf16[8192,128]{0,1:T(8,128)(2,1)}) %all-gather.3.cloned.1.call-update) | async-done | bytes 2097168 | tf_op jit(solution)/shard_map/all_gather | solution.py:40
  140.7 1.2 collective-permute-start
  141.9 1.5 collective-permute-start.2
  143.4 44.4 %collective-permute-done = bf16[8192,128]{0,1:T(8,128)(2,1)S(1)} collective-permute-done((bf16[8192,128]{0,1:T(8,128)(2,1)}, bf16[8192,128]{0,1:T(8,128)(2,1)S(1)}, u32[]{:S(2)}, u32[]{:S(2)}) %collective-permute-start) | collective-permute-done | bytes 2097184 | tf_op jit(solution)/shard_map/ppermute | solution.py:43
  188.0 3.2 %constant_dynamic-update-slice_fusion.4 = bf16[8192,512]{0,1:T(8,128)(2,1)} fusion(bf16[8192,128]{0,1:T(8,128)(2,1)} %all-gather.3.cloned.1.call-done), kind=kLoop, calls=%fused_computation.35 | loop fusion | bytes 4194304
  191.3 2.7 collective-permute-start.3
  194.0 1.5 constant_dynamic-update-slice_fusion.3
  195.5 16.0 %collective-permute-done.1 = bf16[8192,64]{0,1:T(8,128)(2,1)S(1)} collective-permute-done((bf16[8192,64]{0,1:T(8,128)(2,1)S(1)}, bf16[8192,64]{0,1:T(8,128)(2,1)S(1)}, u32[]{:S(2)}, u32[]{:S(2)}) %collective-permute-start.1) | collective-permute-done | bytes 1048608 | tf_op jit(solution)/shard_map/ppermute | solution.py:46
  211.5 1.0 constant_dynamic-update-slice_fusion.2
  212.5 1.5 collective-permute-done.3
  214.0 1.0 constant_dynamic-update-slice_fusion.1
  215.0 1.5 constant_dynamic-update-slice_fusion
  216.5 3.4 %collective-permute-start.4 = (bf16[8192,512]{0,1:T(8,128)(2,1)}, bf16[8192,512]{0,1:T(8,128)(2,1)}, u32[]{:S(2)}, u32[]{:S(2)}) collective-permute-start(bf16[8192,512]{0,1:T(8,128)(2,1)} %constant_dynamic-update-slice_fusion), channel_id=1, source_target_pairs={{0,16},{16,0},{32,48},{48,32},{64,80},{80,64},{96,112},{112,96},{1... | collective-permute-start | bytes 25165832 | tf_op jit(solution)/shard_map/ppermute | solution.py:51
  220.0 0.1 fusion.2
  220.2 11.5 %convolution_bitcast_fusion.2 = f32[512,512]{0,1:T(8,128)} fusion(bf16[8192,512]{0,1:T(8,128)(2,1)} %constant_dynamic-update-slice_fusion, bf16[512,8192]{1,0:T(8,128)(2,1)} %param.8), kind=kOutput, calls=%fused_computation.14 | convolution fusion | flops 4294967296 | bytes 17825792 | tf_op jit(solution)/shard_map/dot_general | solution.py:52
  231.7 1.1 slice.48
  232.8 0.8 slice_bitcast_fusion.2
  233.7 0.6 gather_fusion.5
  234.3 1.3 select_select_fusion
  235.6 5.1 %all-to-all-start.1 = ((f32[8,72,512]{2,1,0:T(8,128)}), f32[8,72,512]{2,1,0:T(8,128)}, u32[]{:S(2)}, u32[]{:S(2)}) async-start(f32[8,72,512]{2,1,0:T(8,128)} %select_select_fusion), calls=%async_computation.2 | async-start | bytes 2359296 | tf_op jit(solution)/shard_map/all_to_all | solution.py:142
  240.7 9.6 %convolution_bitcast_fusion.1 = f32[512,512]{0,1:T(8,128)S(1)} fusion(bf16[8192,512]{0,1:T(8,128)(2,1)} %collective-permute-done.4, bf16[512,8192]{1,0:T(8,128)(2,1)} %param.8), kind=kOutput, calls=%fused_computation.13 | convolution fusion | flops 4294967296 | bytes 17825792 | tf_op jit(solution)/shard_map/dot_general | solution.py:53
  250.3 0.2 pad_maximum_fusion.1
  250.5 2.0 gather_fusion
  252.5 1.9 copy.39
  254.5 1.4 add_convert_fusion
  255.9 1.4 all-to-all-done.1
  257.3 1.5 broadcast_select_fusion
  259.0 4.5 %broadcast_in_dim.151 = f32[64,64,512]{2,1,0:T(8,128)} broadcast(f32[]{:T(128)} %constant.200.clone.1), dimensions={} | broadcast | bytes 8388612 | tf_op jit(solution)/shard_map/broadcast_in_dim | solution.py:145
  263.5 3.3 %scatter_fusion = f32[64,64,512]{2,1,0:T(8,128)} fusion(f32[64,64,512]{2,1,0:T(8,128)} %broadcast_in_dim.151, s32[8]{0:T(128)S(1)} %get-tuple-element.13, f32[8,64,512]{2,1,0:T(8,128)S(1)} %slice.50), kind=kCustom, calls=%fused_computation.6 | custom fusion | flops 262144 | bytes 3145760 | tf_op jit(solution)/shard_map/scatter-add | solution.py:145
  266.8 0.2 broadcast_in_dim.158
  267.0 0.9 scatter_fusion.1
  268.0 1.3 copy-done.5
  (63 shorter events, 1.4 us)
Async XLA Ops:
  7.2 26.9 %copy-start = (bf16[512,1024]{1,0:T(8,128)(2,1)S(1)}, bf16[512,1024]{1,0:T(8,128)(2,1)}, u32[]{:S(2)}) copy-start(bf16[512,1024]{1,0:T(8,128)(2,1)} %param.9) | copy-start | bytes 3145732
  9.5 25.5 %copy-start.8 = (s32[1,64]{1,0:T(1,128)S(1)}, s32[1,64]{1,0:T(1,128)}, u32[]{:S(2)}) copy-start(s32[1,64]{1,0:T(1,128)} %param.13) | copy-start | bytes 772
  9.5 25.7 %copy-start.4 = (bf16[512,1024]{1,0:T(8,128)(2,1)S(1)}, bf16[512,1024]{1,0:T(8,128)(2,1)}, u32[]{:S(2)}) copy-start(bf16[512,1024]{1,0:T(8,128)(2,1)} %param.12) | copy-start | bytes 3145732
  15.9 16.7 %all-to-all-start = ((bf16[8,64,576]{2,1,0:T(8,128)(2,1)}), bf16[8,64,576]{2,1,0:T(8,128)(2,1)S(1)}, u32[]{:S(2)}, u32[]{:S(2)}) async-start(bf16[8,64,576]{2,1,0:T(8,128)(2,1)} %maximum_select_fusion), calls=%async_computation | async-start | bytes 1310720 | tf_op jit(solution)/shard_map/all_to_all | solution.py:79
  21.7 69.7 %all-gather.5.cloned.1.call-start = ((), (), s32[]{:S(2)}) async-start(), calls=%async_computation.4 | async-start | bytes 5570560 | tf_op jit(solution)/shard_map/all_gather | solution.py:82
  34.0 106.7 %all-gather.3.cloned.1.call-start = ((), (), s32[]{:S(2)}) async-start(), calls=%async_computation.3 | async-start | bytes 2228224 | tf_op jit(solution)/shard_map/all_gather | solution.py:40
  35.0 196.7 %reduce-scatter.2.cloned.1.call-start = ((), (), s32[]{:S(2)}) async-start(), calls=%async_computation.5 | async-start | bytes 10027008 | tf_op jit(solution)/shard_map/reduce_scatter | solution.py:127
  96.5 3.4 %copy-start.2 = (bf16[256,1024]{1,0:T(8,128)(2,1)}, bf16[256,1024]{1,0:T(8,128)(2,1)S(1)}, u32[]{:S(2)}) copy-start(bf16[256,1024]{1,0:T(8,128)(2,1)S(1)} %reshape_reshape.7) | copy-start | bytes 1572868
  99.9 6.8 %slice-start = ((s8[8388608]{0:T(1024)(128)(4,1)}), s8[4194304]{0:T(1024)(128)(4,1)S(1)}, s32[]{:S(2)}) async-start(s8[8388608]{0:T(1024)(128)(4,1)} %bitcast.103), calls=%async_computation.6 | async-start | bytes 8388608
  102.3 4.4 %slice-start.1 = ((s8[8388608]{0:T(1024)(128)(4,1)}), s8[4194304]{0:T(1024)(128)(4,1)S(1)}, s32[]{:S(2)}) async-start(s8[8388608]{0:T(1024)(128)(4,1)} %bitcast.103), calls=%async_computation.7 | async-start | bytes 8388608
  140.7 47.1 %collective-permute-start = (bf16[8192,128]{0,1:T(8,128)(2,1)}, bf16[8192,128]{0,1:T(8,128)(2,1)S(1)}, u32[]{:S(2)}, u32[]{:S(2)}) collective-permute-start(bf16[8192,128]{0,1:T(8,128)(2,1)} %all-gather.3.cloned.1.call-done), channel_id=1, source_target_pairs={{0,32},{16,48},{32,64},{48,80},{64,96},{80,112},{96,0},{112,16},{1... | collective-permute-start | bytes 6291464 | tf_op jit(solution)/shard_map/ppermute | solution.py:43
  141.9 49.3 %collective-permute-start.2 = (bf16[8192,128]{0,1:T(8,128)(2,1)}, bf16[8192,128]{0,1:T(8,128)(2,1)S(1)}, u32[]{:S(2)}, u32[]{:S(2)}) collective-permute-start(bf16[8192,128]{0,1:T(8,128)(2,1)} %all-gather.3.cloned.1.call-done), channel_id=1, source_target_pairs={{0,96},{16,112},{32,0},{48,16},{64,32},{80,48},{96,64},{112,80},{1... | collective-permute-start | bytes 6291464 | tf_op jit(solution)/shard_map/ppermute | solution.py:44
  187.9 23.6 %collective-permute-start.1 = (bf16[8192,64]{0,1:T(8,128)(2,1)S(1)}, bf16[8192,64]{0,1:T(8,128)(2,1)S(1)}, u32[]{:S(2)}, u32[]{:S(2)}) collective-permute-start(bf16[8192,64]{0,1:T(8,128)(2,1)S(1)} %slice.44), channel_id=1, source_target_pairs={{0,32},{16,48},{32,64},{48,80},{64,96},{80,112},{96,0},{112,16},{1... | collective-permute-start | bytes 3145736 | tf_op jit(solution)/shard_map/ppermute | solution.py:46
  191.3 22.7 %collective-permute-start.3 = (bf16[8192,64]{0,1:T(8,128)(2,1)S(1)}, bf16[8192,64]{0,1:T(8,128)(2,1)S(1)}, u32[]{:S(2)}, u32[]{:S(2)}) collective-permute-start(bf16[8192,64]{0,1:T(8,128)(2,1)S(1)} %slice.45), channel_id=1, source_target_pairs={{0,96},{16,112},{32,0},{48,16},{64,32},{80,48},{96,64},{112,80},{1... | collective-permute-start | bytes 3145736 | tf_op jit(solution)/shard_map/ppermute | solution.py:47
  216.5 24.3 %collective-permute-start.4 = (bf16[8192,512]{0,1:T(8,128)(2,1)}, bf16[8192,512]{0,1:T(8,128)(2,1)}, u32[]{:S(2)}, u32[]{:S(2)}) collective-permute-start(bf16[8192,512]{0,1:T(8,128)(2,1)} %constant_dynamic-update-slice_fusion), channel_id=1, source_target_pairs={{0,16},{16,0},{32,48},{48,32},{64,80},{80,64},{96,112},{112,96},{1... | collective-permute-start | bytes 25165832 | tf_op jit(solution)/shard_map/ppermute | solution.py:51
  235.6 21.8 %all-to-all-start.1 = ((f32[8,72,512]{2,1,0:T(8,128)}), f32[8,72,512]{2,1,0:T(8,128)}, u32[]{:S(2)}, u32[]{:S(2)}) async-start(f32[8,72,512]{2,1,0:T(8,128)} %select_select_fusion), calls=%async_computation.2 | async-start | bytes 2359296 | tf_op jit(solution)/shard_map/all_to_all | solution.py:142
  240.7 9.6 %copy-start.7 = (f32[512,512]{0,1:T(8,128)S(1)}, f32[512,512]{0,1:T(8,128)}, u32[]{:S(2)}) copy-start(f32[512,512]{0,1:T(8,128)} %convolution_bitcast_fusion.2) | copy-start | bytes 3145732
  250.5 4.0 %copy-start.3 = (bf16[256,1024]{1,0:T(8,128)(2,1)S(1)}, bf16[256,1024]{1,0:T(8,128)(2,1)}, u32[]{:S(2)}) copy-start(bf16[256,1024]{1,0:T(8,128)(2,1)} %copy-done.2) | copy-start | bytes 1572868
  250.5 4.0 %copy-start.6 = (bf16[512,4,64]{0,2,1:T(8,128)(2,1)S(1)}, bf16[512,4,64]{0,2,1:T(8,128)(2,1)}, u32[]{:S(2)}) copy-start(bf16[512,4,64]{0,2,1:T(8,128)(2,1)} %get-tuple-element.11) | copy-start | bytes 786436
  259.0 10.2 %copy-start.1 = (bf16[512,1024]{1,0:T(8,128)(2,1)S(1)}, bf16[512,1024]{1,0:T(8,128)(2,1)}, u32[]{:S(2)}) copy-start(bf16[512,1024]{1,0:T(8,128)(2,1)} %param.9) | copy-start | bytes 3145732
  267.9 1.3 copy-start.5
Sparse Core Ops, SparseCore 0:
  34.2 57.1 all-gather.4
  94.1 46.5 all-gather.2
  144.2 86.6 reduce-scatter.1

commit v9 on v4

--- a/solution.py
+++ b/solution.py
@@ -55,26 +55,20 @@
     got = lax.all_to_all(send, "dp", split_axis=0, concat_axis=0, tiled=True)
     my_owner = lax.dynamic_index_in_dim(list_owner, group_index, 0, keepdims=False)
     slab = jnp.take(got, my_owner, axis=0)
-    lane = part_cols
-    down_rows = list_len * rank * down_cols // lane
-    buf = jnp.concatenate(
-        [
-            w_part,
-            slab[..., :down_cols].reshape(down_rows, lane),
-            slab[..., down_cols:].reshape(-1, lane),
-        ],
-        axis=0,
+    slab_size = rank * slab.shape[2]
+    w_slabs = -(-w_part.size // slab_size)
+    w_flat = jnp.pad(w_part.reshape(-1), (0, w_slabs * slab_size - w_part.size))
+    buf = jnp.concatenate([slab, w_flat.reshape(w_slabs, rank, slab.shape[2])], axis=0)
+    gathered = lax.all_gather(buf, "fsdp", axis=0, tiled=False)
+    shares = gathered[:, :list_len]
+    w_part_full = (
+        gathered[:, list_len:]
+        .reshape(fsdp_count, w_slabs * slab_size)[:, : w_part.size]
+        .reshape(width, part_cols)
     )
-    gathered = lax.all_gather(buf, "fsdp", axis=0, tiled=False)
-    w_rows = w_part.shape[0]
-    shares_down = gathered[:, w_rows : w_rows + down_rows].reshape(
-        fsdp_count, list_len, rank, down_cols
-    )
-    shares_up = gathered[:, w_rows + down_rows :].reshape(fsdp_count, list_len, rank, up_cols)
-    full_down = shares_down.transpose(1, 2, 0, 3).reshape(list_len, rank, width)
-    full_up = shares_up.transpose(1, 2, 0, 3).reshape(list_len, rank, value_cols)
+    full_down = shares[..., :down_cols].transpose(1, 2, 0, 3).reshape(list_len, rank, width)
+    full_up = shares[..., down_cols:].transpose(1, 2, 0, 3).reshape(list_len, rank, value_cols)
 
-    w_part_full = gathered[:, : w_part.shape[0]].reshape(width, part_cols)
     up_x = [(i, (i + 2) % dp_count) for i in range(dp_count)]
     down_x = [(i, (i - 2) % dp_count) for i in range(dp_count)]
     from_left = lax.ppermute(w_part_full, "dp", up_x)
@@ -133,9 +127,9 @@
     rows = list_len * rank
     part_down = part_down.reshape(rows, fsdp_count, down_cols).transpose(1, 0, 2)
     part_up = part_up.reshape(rows, fsdp_count, up_cols).transpose(1, 0, 2)
-    sum_down = lax.psum_scatter(part_down, "fsdp", scatter_dimension=0, tiled=True)[0]
-    sum_up = jnp.sum(lax.all_to_all(part_up, "fsdp", 0, 0, tiled=True), axis=0)
-    summed = jnp.concatenate([sum_down, sum_up], axis=1)
+    summed = lax.psum_scatter(
+        jnp.concatenate([part_down, part_up], axis=2), "fsdp", scatter_dimension=0, tiled=True
+    )[0]
 
     owner_range = jnp.arange(dp_count, dtype=jnp.int32)
     to_owner = my_owner[None, :] == owner_range[:, None]

time: 300 us -> 318 us (1.060)
  local copies, waits for them, and re-layouts: 68.8 us -> 97.6 us
  waiting for transfers between devices: 147 us -> 136 us
  starting transfers between devices: 25.2 us -> 18.8 us
  other arithmetic: 11.8 us -> 16.9 us
    ppermute x1, waiting for transfers between devices: 45.1 us -> 0.01 us  [body(): from_left = lax.ppermute(w_part_full, 'dp', up_x)]
    ppermute x1, waiting for transfers between devices: 0.01 us -> 44.3 us  [body(): from_right = lax.ppermute(w_part_full, 'dp', down_x)]
    ppermute x1, waiting for transfers between devices: 0.01 us -> 18.2 us  [body(): far_b = lax.ppermute(from_right[:, half_part:], 'dp', down_x)]
    all_to_all x1 -> x0, waiting for transfers between devices: 16.7 us -> none  [body(): sum_up = jnp.sum(lax.all_to_all(part_up, 'fsdp', 0, 0, tiled=True), axis=0)]
    ppermute x1, waiting for transfers between devices: 18.7 us -> 3.38 us  [body(): far_a = lax.ppermute(from_left[:, :half_part], 'dp', up_x)]
    concatenate x1, local copies, waits for them, and re-layouts: 1.46 us -> 14.4 us  [body(): w_own = jnp.concatenate(same_parity, axis=1)]
    concatenate x1, local copies, waits for them, and re-layouts: 0.09 us -> 10.9 us  [body(): jnp.concatenate([part_down, part_up], axis=2)]
    ppermute x0 -> x2, local copies, waits for them, and re-layouts: none -> 5.46 us  [the longest x1 2.75 us: body(): far_b = lax.ppermute(from_right[:, half_part:], 'dp', down_x)]
  transfers between devices with their start and end apart: 10 -> 9, of which waited for: 6 -> 6; matrix products, arithmetic and copies ran while one was open for 19% -> 26% of each run, Pallas kernels for 0% -> 0%
where the time goes in v9:
time: 318 us; the launch traced here: 316 us
  waiting for transfers between devices  136 us (43%)
  local copies, waits for them, and re-layouts  97.6 us (31%)
  matrix products  32.4 us (10%)
  starting transfers between devices  18.8 us (6%)
  other arithmetic  16.9 us (5%)
  between operations  14.5 us (5%)
    all_gather x1, waiting for transfers between devices, body(): gathered = lax.all_gather(buf, 'fsdp', axis=0, tiled=False)  56.6 us
    ppermute x1, waiting for transfers between devices, body(): from_right = lax.ppermute(w_part_full, 'dp', down_x)  44.3 us
    ppermute x1, waiting for transfers between devices, body(): far_b = lax.ppermute(from_right[:, half_part:], 'dp', down_x)  18.2 us
    concatenate x1, local copies, waits for them, and re-layouts, body(): w_own = jnp.concatenate(same_parity, axis=1)  14.4 us
    unnamed x37, local copies, waits for them, and re-layouts  12.7 us
    dot_general x1, local copies, waits for them, and re-layouts, body(): lax.dot_general(masked_back, tokens, contract, preferred_element_type=f32)  12.1 us
    dot_general x1, matrix products, body(): out_own = jnp.dot(tokens, w_own, preferred_element_type=f32)  11.3 us
    concatenate x1, local copies, waits for them, and re-layouts, body(): jnp.concatenate([part_down, part_up], axis=2)  10.9 us
  transfers between devices with their start and end apart: 9, of which 6 were waited for; matrix products, arithmetic and copies ran while one was open for 26% of the time, Pallas kernels for 0%

profile of v9, /device:TPU:1, one launch (start us, length us, event | category | flops | bytes accessed | tf_op | source)
XLA Modules:
  0.0 316.0 jit_solution(7789983782196074454)
XLA Ops:
  7.2 0.8 copy.41
  8.1 0.7 gather_fusion
  8.9 0.1 fusion.19
  9.2 0.1 fusion.1
  9.4 2.8 gather_fusion.1
  12.1 1.8 gather_fusion.2
  14.2 1.1 maximum_select_fusion
  15.2 5.8 %all-to-all-start = ((bf16[8,64,576]{2,1,0:T(8,128)(2,1)}), bf16[8,64,576]{2,1,0:T(8,128)(2,1)S(1)}, u32[]{:S(2)}, u32[]{:S(2)}) async-start(bf16[8,64,576]{2,1,0:T(8,128)(2,1)} %maximum_select_fusion), calls=%async_computation | async-start | bytes 1310720 | tf_op jit(solution)/shard_map/all_to_all | solution.py:55
  21.1 0.2 reshape.427
  21.3 10.6 %all-to-all-done = bf16[8,64,576]{2,1,0:T(8,128)(2,1)S(1)} async-done(((bf16[8,64,576]{2,1,0:T(8,128)(2,1)}), bf16[8,64,576]{2,1,0:T(8,128)(2,1)S(1)}, u32[]{:S(2)}, u32[]{:S(2)}) %all-to-all-start) | async-done | bytes 589856 | tf_op jit(solution)/shard_map/all_to_all | solution.py:55
  31.9 0.6 gather_fusion.3
  32.6 0.8 pad_maximum_fusion.2
  33.8 12.1 %copy.60 = bf16[8192,512]{1,0:T(8,128)(2,1)} copy(bf16[8192,512]{0,1:T(8,128)(2,1)} %bitcast.109) | data formatting | bytes 16777216 | tf_op jit(solution)/shard_map/dot_general | solution.py:123
  45.9 0.5 copy.52
  46.5 56.6 %all-gather.3.cloned.1.call-done = bf16[96,64,576]{2,1,0:T(8,128)(2,1)} async-done(((bf16[6,64,576]{2,1,0:T(8,128)(2,1)}), bf16[96,64,576]{2,1,0:T(8,128)(2,1)}) %all-gather.3.cloned.1.call-update) | async-done | bytes 7077904 | tf_op jit(solution)/shard_map/all_gather | solution.py:62
  103.0 2.7 slice.51
  105.7 1.3 slice.52
  107.1 2.4 copy.62
  109.5 4.4 %copy.65 = bf16[32,8,16,512]{3,1,2,0:T(8,128)(2,1)S(1)} copy(bf16[32,8,16,512]{3,2,1,0:T(8,128)(2,1)S(1)} %bitcast.108) | data formatting | bytes 8388608
  113.9 3.2 fusion.20
  117.1 1.6 copy.70
  118.7 2.1 reshape_reshape.7
  120.9 0.5 fusion.21
  121.4 1.1 multiply_reduce_fusion
  122.5 0.7 broadcast_multiply_fusion
  123.3 5.8 %convolution_bitcast_fusion = f32[16,256,512]{2,1,0:T(8,128)S(1)} fusion(bf16[512,256,1]{0,1,2:T(8,128)(2,1)S(1)} %bitcast.122, bf16[16,512,512]{2,1,0:T(8,128)(2,1)} %bitcast.107), kind=kOutput, calls=%fused_computation.9 | convolution fusion | flops 2147483648 | bytes 17039360 | tf_op jit(solution)/shard_map/dot_general | solution.py:123
  129.0 0.7 convolution_bitcast_fusion.1
  129.8 5.2 %pad_maximum_fusion = f32[16,256,576]{2,1,0:T(8,128)} fusion(f32[16,256,64]{2,1,0:T(8,128)S(1)} %convolution_bitcast_fusion.1, f32[16,256,512]{2,1,0:T(8,128)S(1)} %convolution_bitcast_fusion), kind=kLoop, calls=%fused_computation.8 | loop fusion | flops 2359296 | bytes 18874368 | tf_op jit(solution)/shard_map/concatenate | solution.py:131
  134.9 10.9 %copy.55 = f32[16,256,576]{1,2,0:T(8,128)} copy(f32[16,256,576]{2,1,0:T(8,128)} %pad_maximum_fusion) | data formatting | bytes 18874368 | tf_op jit(solution)/shard_map/concatenate | solution.py:131
  145.8 3.5 %slice.47 = bf16[16,2,64,576]{3,2,1,0:T(8,128)(2,1)} slice(bf16[16,6,64,576]{3,2,1,0:T(8,128)(2,1)} %bitcast.116), slice={[0:16], [4:6], [0:64], [0:576]} | slice | bytes 4718592 | tf_op jit(solution)/shard_map/slice | solution.py:65
  149.4 4.4 %reshape.428 = bf16[16,73728]{1,0:T(8,128)(2,1)S(1)} reshape(bf16[16,2,64,576]{3,2,1,0:T(8,128)(2,1)} %slice.47) | data formatting | bytes 4718592 | tf_op jit(solution)/shard_map/reshape | solution.py:66
  153.7 1.5 slice.48
  155.2 2.2 reshape.429
  157.4 2.5 collective-permute-start.2
  159.9 44.3 %collective-permute-done.2 = bf16[8192,128]{1,0:T(8,128)(2,1)S(1)} collective-permute-done((bf16[8192,128]{1,0:T(8,128)(2,1)S(1)}, bf16[8192,128]{1,0:T(8,128)(2,1)S(1)}, u32[]{:S(2)}, u32[]{:S(2)}) %collective-permute-start.2) | collective-permute-done | bytes 2097184 | tf_op jit(solution)/shard_map/ppermute | solution.py:75
  204.3 1.3 copy-done.3
  205.6 1.9 slice.50
  207.5 1.9 copy.45
  209.4 3.5 %collective-permute-start.3 = (bf16[8192,64]{0,1:T(8,128)(2,1)S(1)}, bf16[8192,64]{0,1:T(8,128)(2,1)}, u32[]{:S(2)}, u32[]{:S(2)}) collective-permute-start(bf16[8192,64]{0,1:T(8,128)(2,1)S(1)} %copy.45), channel_id=1, source_target_pairs={{0,96},{16,112},{32,0},{48,16},{64,32},{80,48},{96,64},{112,80},{1... | collective-permute-start | bytes 3145736 | tf_op jit(solution)/shard_map/ppermute | solution.py:78
  212.9 2.7 copy.44
  215.6 18.2 %collective-permute-done.3 = bf16[8192,64]{0,1:T(8,128)(2,1)} collective-permute-done((bf16[8192,64]{0,1:T(8,128)(2,1)S(1)}, bf16[8192,64]{0,1:T(8,128)(2,1)}, u32[]{:S(2)}, u32[]{:S(2)}) %collective-permute-start.3) | collective-permute-done | bytes 1048608 | tf_op jit(solution)/shard_map/ppermute | solution.py:78
  233.8 2.7 copy.47
  236.6 3.4 %collective-permute-done.1 = bf16[8192,64]{0,1:T(8,128)(2,1)} collective-permute-done((bf16[8192,64]{0,1:T(8,128)(2,1)}, bf16[8192,64]{0,1:T(8,128)(2,1)}, u32[]{:S(2)}, u32[]{:S(2)}) %collective-permute-start.1) | collective-permute-done | bytes 1048608 | tf_op jit(solution)/shard_map/ppermute | solution.py:77
  240.0 2.7 copy.46
  242.7 14.4 %concatenate.17 = bf16[8192,512]{1,0:T(8,128)(2,1)} concatenate(bf16[8192,128]{1,0:T(8,128)(2,1)S(1)} %reshape.429, bf16[8192,128]{1,0:T(8,128)(2,1)} %collective-permute-done, bf16[8192,64]{1,0:T(8,128)(2,1)} %copy.46, bf16[8192,64]{1,0:T(8,128)(2,1)} %copy.47, bf16[8192,128]{1,0:T(8,128)(2,1)} %copy-done.3), dimensions={1} | concatenate | bytes 16777216 | tf_op jit(solution)/shard_map/concatenate | solution.py:81
  257.0 2.7 collective-permute-start.4
  260.0 11.3 %convolution_bitcast_fusion.3 = f32[512,512]{0,1:T(8,128)} fusion(bf16[8192,512]{1,0:T(8,128)(2,1)} %concatenate.17, bf16[512,8192]{1,0:T(8,128)(2,1)} %param.8), kind=kOutput, calls=%fused_computation.14 | convolution fusion | flops 4294967296 | bytes 17825792 | tf_op jit(solution)/shard_map/dot_general | solution.py:83
  271.3 1.3 copy.56
  272.6 0.6 gather_fusion.5
  273.3 1.2 select_select_fusion
  274.5 4.2 %all-to-all-start.1 = ((f32[8,64,576]{2,1,0:T(8,128)}), f32[8,64,576]{2,1,0:T(8,128)}, u32[]{:S(2)}, u32[]{:S(2)}) async-start(f32[8,64,576]{2,1,0:T(8,128)} %select_select_fusion), calls=%async_computation.1 | async-start | bytes 2621440 | tf_op jit(solution)/shard_map/all_to_all | solution.py:140
  278.8 9.6 %convolution_bitcast_fusion.2 = f32[512,512]{0,1:T(8,128)S(1)} fusion(bf16[8192,512]{1,0:T(8,128)(2,1)} %collective-permute-done.4, bf16[512,8192]{1,0:T(8,128)(2,1)} %param.8), kind=kOutput, calls=%fused_computation.13 | convolution fusion | flops 4294967296 | bytes 17825792 | tf_op jit(solution)/shard_map/dot_general | solution.py:84
  288.4 0.2 pad_maximum_fusion.1
  288.6 2.0 gather_fusion.4
  290.6 2.0 copy.59
  292.6 1.4 add_convert_fusion
  294.0 2.7 all-to-all-done.1
  296.7 1.5 broadcast_select_fusion
  298.3 4.5 %broadcast_in_dim.149 = f32[64,64,512]{2,1,0:T(8,128)} broadcast(f32[]{:T(128)} %constant.201.clone.1), dimensions={} | broadcast | bytes 8388612 | tf_op jit(solution)/shard_map/broadcast_in_dim | solution.py:143
  302.8 3.2 %scatter_fusion = f32[64,64,512]{2,1,0:T(8,128)} fusion(f32[64,64,512]{2,1,0:T(8,128)} %broadcast_in_dim.149, s32[8]{0:T(128)S(1)} %get-tuple-element.13, f32[8,64,512]{2,1,0:T(8,128)S(1)} %slice.53), kind=kCustom, calls=%fused_computation.6 | custom fusion | flops 262144 | bytes 3145760 | tf_op jit(solution)/shard_map/scatter-add | solution.py:143
  306.0 0.2 broadcast_in_dim.155
  306.3 0.7 slice-done.2
  307.0 0.9 scatter_fusion.1
  307.9 1.3 copy-done.8
  (68 shorter events, 1.5 us)
Async XLA Ops:
  7.2 13.9 %copy-start = (bf16[512,1024]{1,0:T(8,128)(2,1)S(1)}, bf16[512,1024]{1,0:T(8,128)(2,1)}, u32[]{:S(2)}) copy-start(bf16[512,1024]{1,0:T(8,128)(2,1)} %param.9) | copy-start | bytes 3145732
  7.2 1.0 copy-start.2
  15.2 16.7 %all-to-all-start = ((bf16[8,64,576]{2,1,0:T(8,128)(2,1)}), bf16[8,64,576]{2,1,0:T(8,128)(2,1)S(1)}, u32[]{:S(2)}, u32[]{:S(2)}) async-start(bf16[8,64,576]{2,1,0:T(8,128)(2,1)} %maximum_select_fusion), calls=%async_computation | async-start | bytes 1310720 | tf_op jit(solution)/shard_map/all_to_all | solution.py:55
  21.0 12.5 %copy-start.11 = (s32[1,64]{1,0:T(1,128)S(1)}, s32[1,64]{1,0:T(1,128)}, u32[]{:S(2)}) copy-start(s32[1,64]{1,0:T(1,128)} %param.13) | copy-start | bytes 772
  21.0 82.0 %all-gather.3.cloned.1.call-start = ((), (), s32[]{:S(2)}) async-start(), calls=%async_computation.3 | async-start | bytes 8355840 | tf_op jit(solution)/shard_map/all_gather | solution.py:62
  33.5 237.8 %reduce-scatter.4.cloned.1.call-start = ((), (), s32[]{:S(2)}) async-start(), calls=%async_computation.4 | async-start | bytes 10027008
  33.8 12.1 %copy-start.7 = (bf16[512,1024]{1,0:T(8,128)(2,1)S(1)}, bf16[512,1024]{1,0:T(8,128)(2,1)}, u32[]{:S(2)}) copy-start(bf16[512,1024]{1,0:T(8,128)(2,1)} %param.12) | copy-start | bytes 3145732
  107.1 6.8 %slice-start = ((s8[8388608]{0:T(1024)(128)(4,1)}), s8[4194304]{0:T(1024)(128)(4,1)S(1)}, s32[]{:S(2)}) async-start(s8[8388608]{0:T(1024)(128)(4,1)} %bitcast.110), calls=%async_computation.5 | async-start | bytes 8388608
  109.5 4.4 %slice-start.1 = ((s8[8388608]{0:T(1024)(128)(4,1)}), s8[4194304]{0:T(1024)(128)(4,1)S(1)}, s32[]{:S(2)}) async-start(s8[8388608]{0:T(1024)(128)(4,1)} %bitcast.110), calls=%async_computation.6 | async-start | bytes 8388608
  120.9 2.4 copy-start.5
  157.4 46.8 %collective-permute-start.2 = (bf16[8192,128]{1,0:T(8,128)(2,1)S(1)}, bf16[8192,128]{1,0:T(8,128)(2,1)S(1)}, u32[]{:S(2)}, u32[]{:S(2)}) collective-permute-start(bf16[8192,128]{1,0:T(8,128)(2,1)S(1)} %reshape.429), channel_id=1, source_target_pairs={{0,96},{16,112},{32,0},{48,16},{64,32},{80,48},{96,64},{112,80},{1... | collective-permute-start | bytes 6291464 | tf_op jit(solution)/shard_map/ppermute | solution.py:75
  159.9 53.0 %collective-permute-start = (bf16[8192,128]{1,0:T(8,128)(2,1)S(1)}, bf16[8192,128]{1,0:T(8,128)(2,1)}, u32[]{:S(2)}, u32[]{:S(2)}) collective-permute-start(bf16[8192,128]{1,0:T(8,128)(2,1)S(1)} %reshape.429), channel_id=1, source_target_pairs={{0,32},{16,48},{32,64},{48,80},{64,96},{80,112},{96,0},{112,16},{1... | collective-permute-start | bytes 6291464 | tf_op jit(solution)/shard_map/ppermute | solution.py:74
  204.3 1.3 copy-start.3
  209.4 24.4 %collective-permute-start.3 = (bf16[8192,64]{0,1:T(8,128)(2,1)S(1)}, bf16[8192,64]{0,1:T(8,128)(2,1)}, u32[]{:S(2)}, u32[]{:S(2)}) collective-permute-start(bf16[8192,64]{0,1:T(8,128)(2,1)S(1)} %copy.45), channel_id=1, source_target_pairs={{0,96},{16,112},{32,0},{48,16},{64,32},{80,48},{96,64},{112,80},{1... | collective-permute-start | bytes 3145736 | tf_op jit(solution)/shard_map/ppermute | solution.py:78
  215.6 24.4 %collective-permute-start.1 = (bf16[8192,64]{0,1:T(8,128)(2,1)}, bf16[8192,64]{0,1:T(8,128)(2,1)}, u32[]{:S(2)}, u32[]{:S(2)}) collective-permute-start(bf16[8192,64]{0,1:T(8,128)(2,1)} %copy.44), channel_id=1, source_target_pairs={{0,32},{16,48},{32,64},{48,80},{64,96},{80,112},{96,0},{112,16},{1... | collective-permute-start | bytes 3145736 | tf_op jit(solution)/shard_map/ppermute | solution.py:77
  257.0 21.7 %collective-permute-start.4 = (bf16[8192,512]{1,0:T(8,128)(2,1)}, bf16[8192,512]{1,0:T(8,128)(2,1)}, u32[]{:S(2)}, u32[]{:S(2)}) collective-permute-start(bf16[8192,512]{1,0:T(8,128)(2,1)} %concatenate.17), channel_id=1, source_target_pairs={{0,16},{16,0},{32,48},{48,32},{64,80},{80,64},{96,112},{112,96},{1... | collective-permute-start | bytes 25165832 | tf_op jit(solution)/shard_map/ppermute | solution.py:82
  274.5 22.2 %all-to-all-start.1 = ((f32[8,64,576]{2,1,0:T(8,128)}), f32[8,64,576]{2,1,0:T(8,128)}, u32[]{:S(2)}, u32[]{:S(2)}) async-start(f32[8,64,576]{2,1,0:T(8,128)} %select_select_fusion), calls=%async_computation.1 | async-start | bytes 2621440 | tf_op jit(solution)/shard_map/all_to_all | solution.py:140
  278.7 9.6 %copy-start.10 = (f32[512,512]{0,1:T(8,128)S(1)}, f32[512,512]{0,1:T(8,128)}, u32[]{:S(2)}) copy-start(f32[512,512]{0,1:T(8,128)} %convolution_bitcast_fusion.3) | copy-start | bytes 3145732
  290.6 2.0 copy-start.6
  290.6 2.0 copy-start.9
  298.2 4.6 %copy-start.4 = (f32[8,64,576]{2,1,0:T(8,128)}, f32[8,64,576]{2,1,0:T(8,128)S(1)}, u32[]{:S(2)}) copy-start(f32[8,64,576]{2,1,0:T(8,128)S(1)} %broadcast_select_fusion) | copy-start | bytes 3538948
  302.8 6.4 %copy-start.1 = (bf16[512,1024]{1,0:T(8,128)(2,1)S(1)}, bf16[512,1024]{1,0:T(8,128)(2,1)}, u32[]{:S(2)}) copy-start(bf16[512,1024]{1,0:T(8,128)(2,1)} %param.9) | copy-start | bytes 3145732
  306.0 0.9 slice-start.2
  307.9 1.3 copy-start.8
Sparse Core Ops, SparseCore 0:
  33.6 69.3 all-gather.2
  145.9 86.1 reduce-scatter.3

commit v10 on v6

--- a/solution.py
+++ b/solution.py
@@ -37,7 +37,9 @@
     w_part = lax.dynamic_slice_in_dim(
         frozen_value_matrix, group_index * part_cols, part_cols, axis=1
     )
-    w_part_full = lax.all_gather(w_part, "fsdp", axis=0, tiled=True)
+    w_part_full = lax.all_to_all(
+        jnp.broadcast_to(w_part[None], (fsdp_count,) + w_part.shape), "fsdp", 0, 0, tiled=True
+    ).reshape(width, part_cols)
     up_x = [(i, (i + 2) % dp_count) for i in range(dp_count)]
     down_x = [(i, (i - 2) % dp_count) for i in range(dp_count)]
     from_left = lax.ppermute(w_part_full, "dp", up_x)

time: 277 us -> 332 us (1.20)
  blocking collectives: 0 us -> 41.2 us
  local copies, waits for them, and re-layouts: 65.8 us -> 90 us
  waiting for transfers between devices: 132 us -> 114 us
    ppermute x1, waiting for transfers between devices: 44.4 us -> 0.01 us  [body(): from_left = lax.ppermute(w_part_full, 'dp', up_x)]
    all_to_all x0 -> x1, blocking collectives: none -> 41.2 us  [body(): lax.all_to_all(jnp.broadcast_to(w_part[None], (fsdp_count,) + w_part.shap...]
    ppermute x1, waiting for transfers between devices: 0.01 us -> 39.7 us  [body(): from_right = lax.ppermute(w_part_full, 'dp', down_x)]
    all_gather x1 -> x0, waiting for transfers between devices: 13.4 us -> none  [body(): w_part_full = lax.all_gather(w_part, 'fsdp', axis=0, tiled=True)]
    concatenate x1, local copies, waits for them, and re-layouts: 1.46 us -> 14.4 us  [body(): w_own = jnp.concatenate(same_parity, axis=1)]
    ppermute x1, waiting for transfers between devices: 16 us -> 3.38 us  [body(): far_a = lax.ppermute(from_left[:, :half_part], 'dp', up_x)]
    ppermute x1, waiting for transfers between devices: 1.41 us -> 13.6 us  [body(): far_b = lax.ppermute(from_right[:, half_part:], 'dp', down_x)]
    unnamed x40 -> x35, local copies, waits for them, and re-layouts: 15.8 us -> 9.47 us
  transfers between devices with their start and end apart: 10 -> 9, of which waited for: 7 -> 6; matrix products, arithmetic and copies ran while one was open for 32% -> 22% of each run, Pallas kernels for 0% -> 0%
where the time goes in v10:
time: 332 us; the launch traced here: 330 us
  waiting for transfers between devices  114 us (34%)
  local copies, waits for them, and re-layouts  90 us (27%)
  blocking collectives  41.2 us (12%)
  matrix products  31.7 us (10%)
  starting transfers between devices  23.4 us (7%)
  other arithmetic  15.1 us (5%)
  between operations  14.5 us (4%)
    all_gather x1, waiting for transfers between devices, body(): shares = lax.all_gather(slab, 'fsdp', axis=0, tiled=False)  43.7 us
    all_to_all x1, blocking collectives, body(): lax.all_to_all(jnp.broadcast_to(w_part[None], (fsdp_count,) + w_part.shap...  41.2 us
    ppermute x1, waiting for transfers between devices, body(): from_right = lax.ppermute(w_part_full, 'dp', down_x)  39.7 us
    concatenate x1, local copies, waits for them, and re-layouts, body(): w_own = jnp.concatenate(same_parity, axis=1)  14.4 us
    ppermute x1, waiting for transfers between devices, body(): far_b = lax.ppermute(from_right[:, half_part:], 'dp', down_x)  13.6 us
    dot_general x1, local copies, waits for them, and re-layouts, body(): lax.dot_general(masked_back, tokens, contract, preferred_element_type=f32)  12.1 us
    dot_general x1, matrix products, body(): out_own = jnp.dot(tokens, w_own, preferred_element_type=f32)  11.3 us
    all_to_all x1, waiting for transfers between devices, body(): got = lax.all_to_all(send, 'dp', split_axis=0, concat_axis=0, tiled=True)  10.9 us
  transfers between devices with their start and end apart: 9, of which 6 were waited for; matrix products, arithmetic and copies ran while one was open for 22% of the time, Pallas kernels for 0%

profile of v10, /device:TPU:1, one launch (start us, length us, event | category | flops | bytes accessed | tf_op | source)
XLA Modules:
  0.0 329.8 jit_solution(11445415908031516488)
XLA Ops:
  7.2 0.8 copy.75
  8.1 0.7 gather_fusion.1
  8.9 0.1 fusion.19
  9.2 0.1 fusion.1
  9.4 2.8 gather_fusion.2
  12.1 1.8 gather_fusion.3
  13.9 0.1 broadcast_select_fusion.1
  14.2 1.1 maximum_select_fusion
  15.2 5.8 %all-to-all-start.1 = ((bf16[8,64,576]{2,1,0:T(8,128)(2,1)}), bf16[8,64,576]{2,1,0:T(8,128)(2,1)S(1)}, u32[]{:S(2)}, u32[]{:S(2)}) async-start(bf16[8,64,576]{2,1,0:T(8,128)(2,1)} %maximum_select_fusion), calls=%async_computation.1 | async-start | bytes 1310720 | tf_op jit(solution)/shard_map/all_to_all | solution.py:81
  21.1 10.9 %all-to-all-done.1 = bf16[8,64,576]{2,1,0:T(8,128)(2,1)S(1)} async-done(((bf16[8,64,576]{2,1,0:T(8,128)(2,1)}), bf16[8,64,576]{2,1,0:T(8,128)(2,1)S(1)}, u32[]{:S(2)}, u32[]{:S(2)}) %all-to-all-start.1) | async-done | bytes 589856 | tf_op jit(solution)/shard_map/all_to_all | solution.py:81
  31.9 0.6 gather_fusion.4
  32.5 0.8 bitcast_select_fusion
  33.7 12.1 %copy.89 = bf16[8192,512]{1,0:T(8,128)(2,1)} copy(bf16[8192,512]{0,1:T(8,128)(2,1)} %bitcast.110) | data formatting | bytes 16777216 | tf_op jit(solution)/shard_map/dot_general | solution.py:115
  45.8 1.3 copy.81
  47.1 43.7 %all-gather.2.cloned.1.call-done = bf16[16,4,64,576]{3,2,1,0:T(8,128)(2,1)} async-done(((bf16[1,4,64,576]{3,2,1,0:T(8,128)(2,1)}), bf16[16,4,64,576]{3,2,1,0:T(8,128)(2,1)}) %all-gather.2.cloned.1.call-update) | async-done | bytes 4718608 | tf_op jit(solution)/shard_map/all_gather | solution.py:84
  90.7 2.7 slice_bitcast_fusion
  93.4 2.4 copy.78
  95.9 4.4 %copy.92 = bf16[32,8,16,512]{3,1,2,0:T(8,128)(2,1)S(1)} copy(bf16[32,8,16,512]{3,2,1,0:T(8,128)(2,1)S(1)} %bitcast.106) | data formatting | bytes 8388608
  100.3 2.4 fusion.20
  102.7 1.3 slice_bitcast_fusion.1
  104.0 1.7 copy.79
  105.6 2.1 reshape_reshape.7
  107.8 0.5 fusion.21
  108.3 0.1 multiply_reduce_fusion
  108.6 5.8 %convolution_bitcast_fusion = f32[16,256,512]{2,1,0:T(8,128)S(1)} fusion(bf16[512,256,1]{0,1,2:T(8,128)(2,1)S(1)} %bitcast.119, bf16[16,512,512]{2,1,0:T(8,128)(2,1)} %bitcast.105), kind=kOutput, calls=%fused_computation.10 | convolution fusion | flops 2147483648 | bytes 17039360 | tf_op jit(solution)/shard_map/dot_general | solution.py:115
  114.4 0.7 convolution_bitcast_fusion.1
  115.2 5.2 %pad_maximum_fusion = f32[16,256,576]{2,1,0:T(8,128)} fusion(f32[16,256,64]{2,1,0:T(8,128)S(1)} %convolution_bitcast_fusion.1, f32[16,256,512]{2,1,0:T(8,128)S(1)} %convolution_bitcast_fusion), kind=kLoop, calls=%fused_computation.8 | loop fusion | flops 2359296 | bytes 18874368 | tf_op jit(solution)/shard_map/concatenate | solution.py:123
  120.3 10.9 %copy.84 = f32[16,256,576]{1,2,0:T(8,128)} copy(f32[16,256,576]{2,1,0:T(8,128)} %pad_maximum_fusion) | data formatting | bytes 18874368 | tf_op jit(solution)/shard_map/concatenate | solution.py:123
  131.4 0.2 broadcast_in_dim.142
  131.6 41.2 %all_to_all.15 = bf16[16,512,128]{1,2,0:T(8,128)(2,1)} all-to-all(bf16[16,512,128]{1,2,0:T(8,128)(2,1)S(1)} %broadcast_in_dim.142), channel_id=1, replica_groups=mesh['dp'=8,'fsdp'=16] {'fsdp'}, dimensions={0} | all-to-all | bytes 4194304 | tf_op jit(solution)/shard_map/all_to_all | solution.py:40
  172.8 3.1 copy.69
  175.9 2.4 collective-permute-start.2
  178.3 39.7 %collective-permute-done.2 = bf16[8192,128]{1,0:T(8,128)(2,1)S(1)} collective-permute-done((bf16[8192,128]{1,0:T(8,128)(2,1)S(1)}, bf16[8192,128]{1,0:T(8,128)(2,1)S(1)}, u32[]{:S(2)}, u32[]{:S(2)}) %collective-permute-start.2) | collective-permute-done | bytes 2097184 | tf_op jit(solution)/shard_map/ppermute | solution.py:46
  218.0 1.3 copy-done.3
  219.4 1.9 slice.37
  221.3 1.9 copy.71
  223.2 3.5 %collective-permute-start.3 = (bf16[8192,64]{0,1:T(8,128)(2,1)S(1)}, bf16[8192,64]{0,1:T(8,128)(2,1)}, u32[]{:S(2)}, u32[]{:S(2)}) collective-permute-start(bf16[8192,64]{0,1:T(8,128)(2,1)S(1)} %copy.71), channel_id=1, source_target_pairs={{0,96},{16,112},{32,0},{48,16},{64,32},{80,48},{96,64},{112,80},{1... | collective-permute-start | bytes 3145736 | tf_op jit(solution)/shard_map/ppermute | solution.py:49
  226.7 2.7 copy.70
  229.4 13.6 %collective-permute-done.3 = bf16[8192,64]{0,1:T(8,128)(2,1)} collective-permute-done((bf16[8192,64]{0,1:T(8,128)(2,1)S(1)}, bf16[8192,64]{0,1:T(8,128)(2,1)}, u32[]{:S(2)}, u32[]{:S(2)}) %collective-permute-start.3) | collective-permute-done | bytes 1048608 | tf_op jit(solution)/shard_map/ppermute | solution.py:49
  243.0 2.7 copy.73
  245.8 3.4 %collective-permute-done.1 = bf16[8192,64]{0,1:T(8,128)(2,1)} collective-permute-done((bf16[8192,64]{0,1:T(8,128)(2,1)}, bf16[8192,64]{0,1:T(8,128)(2,1)}, u32[]{:S(2)}, u32[]{:S(2)}) %collective-permute-start.1) | collective-permute-done | bytes 1048608 | tf_op jit(solution)/shard_map/ppermute | solution.py:48
  249.2 2.7 copy.72
  251.9 14.4 %concatenate.12 = bf16[8192,512]{1,0:T(8,128)(2,1)} concatenate(bf16[8192,128]{1,0:T(8,128)(2,1)S(1)} %bitcast.109, bf16[8192,128]{1,0:T(8,128)(2,1)} %collective-permute-done, bf16[8192,64]{1,0:T(8,128)(2,1)} %copy.72, bf16[8192,64]{1,0:T(8,128)(2,1)} %copy.73, bf16[8192,128]{1,0:T(8,128)(2,1)} %copy-done.3), dimensions={1} | concatenate | bytes 16777216 | tf_op jit(solution)/shard_map/concatenate | solution.py:52
  266.2 7.4 %collective-permute-start.4 = (bf16[8192,512]{1,0:T(8,128)(2,1)}, bf16[8192,512]{1,0:T(8,128)(2,1)}, u32[]{:S(2)}, u32[]{:S(2)}) collective-permute-start(bf16[8192,512]{1,0:T(8,128)(2,1)} %concatenate.12), channel_id=1, source_target_pairs={{0,16},{16,0},{32,48},{48,32},{64,80},{80,64},{96,112},{112,96},{1... | collective-permute-start | bytes 25165832 | tf_op jit(solution)/shard_map/ppermute | solution.py:53
  273.6 0.1 fusion.2
  273.9 11.3 %convolution_bitcast_fusion.3 = f32[512,512]{0,1:T(8,128)} fusion(bf16[8192,512]{1,0:T(8,128)(2,1)} %concatenate.12, bf16[512,8192]{1,0:T(8,128)(2,1)} %param.8), kind=kOutput, calls=%fused_computation.15 | convolution fusion | flops 4294967296 | bytes 17825792 | tf_op jit(solution)/shard_map/dot_general | solution.py:54
  285.1 1.3 copy.85
  286.5 0.6 gather_fusion.5
  287.1 1.2 select_select_fusion
  288.3 4.2 %all-to-all-start.2 = ((f32[8,64,576]{2,1,0:T(8,128)}), f32[8,64,576]{2,1,0:T(8,128)}, u32[]{:S(2)}, u32[]{:S(2)}) async-start(f32[8,64,576]{2,1,0:T(8,128)} %select_select_fusion), calls=%async_computation.2 | async-start | bytes 2621440 | tf_op jit(solution)/shard_map/all_to_all | solution.py:132
  292.6 9.6 %convolution_bitcast_fusion.2 = f32[512,512]{0,1:T(8,128)S(1)} fusion(bf16[8192,512]{1,0:T(8,128)(2,1)} %collective-permute-done.4, bf16[512,8192]{1,0:T(8,128)(2,1)} %param.8), kind=kOutput, calls=%fused_computation.14 | convolution fusion | flops 4294967296 | bytes 17825792 | tf_op jit(solution)/shard_map/dot_general | solution.py:55
  302.2 0.2 pad_maximum_fusion.1
  302.4 2.0 gather_fusion
  304.4 2.0 copy.88
  306.4 1.4 add_convert_fusion
  307.8 2.7 all-to-all-done.2
  310.5 1.5 broadcast_select_fusion
  312.0 0.1 slice.40
  312.2 4.5 %broadcast_in_dim.156 = f32[64,64,512]{2,1,0:T(8,128)} broadcast(f32[]{:T(128)} %constant.200.clone.1), dimensions={} | broadcast | bytes 8388612 | tf_op jit(solution)/shard_map/broadcast_in_dim | solution.py:135
  316.6 3.2 scatter_fusion
  319.8 0.2 broadcast_in_dim.162
  320.1 0.7 slice-done.2
  320.8 0.9 scatter_fusion.1
  321.7 1.3 copy-done.9
  (65 shorter events, 1.3 us)
Async XLA Ops:
  7.2 124.1 %copy-start = (bf16[512,1024]{1,0:T(8,128)(2,1)S(1)}, bf16[512,1024]{1,0:T(8,128)(2,1)}, u32[]{:S(2)}) copy-start(bf16[512,1024]{1,0:T(8,128)(2,1)} %param.9) | copy-start | bytes 3145732
  7.2 1.0 copy-start.2
  14.2 19.3 %copy-start.11 = (s32[1,64]{1,0:T(1,128)S(1)}, s32[1,64]{1,0:T(1,128)}, u32[]{:S(2)}) copy-start(s32[1,64]{1,0:T(1,128)} %param.13) | copy-start | bytes 772
  15.2 16.7 %all-to-all-start.1 = ((bf16[8,64,576]{2,1,0:T(8,128)(2,1)}), bf16[8,64,576]{2,1,0:T(8,128)(2,1)S(1)}, u32[]{:S(2)}, u32[]{:S(2)}) async-start(bf16[8,64,576]{2,1,0:T(8,128)(2,1)} %maximum_select_fusion), calls=%async_computation.1 | async-start | bytes 1310720 | tf_op jit(solution)/shard_map/all_to_all | solution.py:81
  21.0 69.7 %all-gather.2.cloned.1.call-start = ((), (), s32[]{:S(2)}) async-start(), calls=%async_computation.4 | async-start | bytes 5570560 | tf_op jit(solution)/shard_map/all_gather | solution.py:84
  33.4 251.8 %reduce-scatter.4.cloned.1.call-start = ((), (), s32[]{:S(2)}) async-start(), calls=%async_computation.5 | async-start | bytes 10027008
  33.7 12.1 %copy-start.7 = (bf16[512,1024]{1,0:T(8,128)(2,1)S(1)}, bf16[512,1024]{1,0:T(8,128)(2,1)}, u32[]{:S(2)}) copy-start(bf16[512,1024]{1,0:T(8,128)(2,1)} %param.12) | copy-start | bytes 3145732
  93.4 6.8 %slice-start = ((s8[8388608]{0:T(1024)(128)(4,1)}), s8[4194304]{0:T(1024)(128)(4,1)S(1)}, s32[]{:S(2)}) async-start(s8[8388608]{0:T(1024)(128)(4,1)} %bitcast.111), calls=%async_computation.6 | async-start | bytes 8388608
  95.9 4.4 %slice-start.1 = ((s8[8388608]{0:T(1024)(128)(4,1)}), s8[4194304]{0:T(1024)(128)(4,1)S(1)}, s32[]{:S(2)}) async-start(s8[8388608]{0:T(1024)(128)(4,1)} %bitcast.111), calls=%async_computation.7 | async-start | bytes 8388608
  107.8 0.8 copy-start.5
  108.6 5.9 %copy-start.8 = (bf16[512,1024]{0,1:T(8,128)(2,1)S(1)}, bf16[512,1024]{0,1:T(8,128)(2,1)}, u32[]{:S(2)}) copy-start(bf16[512,1024]{0,1:T(8,128)(2,1)} %copy.81) | copy-start | bytes 3145732
  175.9 42.1 %collective-permute-start.2 = (bf16[8192,128]{1,0:T(8,128)(2,1)S(1)}, bf16[8192,128]{1,0:T(8,128)(2,1)S(1)}, u32[]{:S(2)}, u32[]{:S(2)}) collective-permute-start(bf16[8192,128]{1,0:T(8,128)(2,1)S(1)} %bitcast.107), channel_id=1, source_target_pairs={{0,96},{16,112},{32,0},{48,16},{64,32},{80,48},{96,64},{112,80},{1... | collective-permute-start | bytes 6291464 | tf_op jit(solution)/shard_map/ppermute | solution.py:46
  178.3 48.4 %collective-permute-start = (bf16[8192,128]{1,0:T(8,128)(2,1)S(1)}, bf16[8192,128]{1,0:T(8,128)(2,1)}, u32[]{:S(2)}, u32[]{:S(2)}) collective-permute-start(bf16[8192,128]{1,0:T(8,128)(2,1)S(1)} %bitcast.108), channel_id=1, source_target_pairs={{0,32},{16,48},{32,64},{48,80},{64,96},{80,112},{96,0},{112,16},{1... | collective-permute-start | bytes 6291464 | tf_op jit(solution)/shard_map/ppermute | solution.py:45
  218.0 1.3 copy-start.3
  223.2 19.8 %collective-permute-start.3 = (bf16[8192,64]{0,1:T(8,128)(2,1)S(1)}, bf16[8192,64]{0,1:T(8,128)(2,1)}, u32[]{:S(2)}, u32[]{:S(2)}) collective-permute-start(bf16[8192,64]{0,1:T(8,128)(2,1)S(1)} %copy.71), channel_id=1, source_target_pairs={{0,96},{16,112},{32,0},{48,16},{64,32},{80,48},{96,64},{112,80},{1... | collective-permute-start | bytes 3145736 | tf_op jit(solution)/shard_map/ppermute | solution.py:49
  229.4 19.7 %collective-permute-start.1 = (bf16[8192,64]{0,1:T(8,128)(2,1)}, bf16[8192,64]{0,1:T(8,128)(2,1)}, u32[]{:S(2)}, u32[]{:S(2)}) collective-permute-start(bf16[8192,64]{0,1:T(8,128)(2,1)} %copy.70), channel_id=1, source_target_pairs={{0,32},{16,48},{32,64},{48,80},{64,96},{80,112},{96,0},{112,16},{1... | collective-permute-start | bytes 3145736 | tf_op jit(solution)/shard_map/ppermute | solution.py:48
  266.2 26.3 %collective-permute-start.4 = (bf16[8192,512]{1,0:T(8,128)(2,1)}, bf16[8192,512]{1,0:T(8,128)(2,1)}, u32[]{:S(2)}, u32[]{:S(2)}) collective-permute-start(bf16[8192,512]{1,0:T(8,128)(2,1)} %concatenate.12), channel_id=1, source_target_pairs={{0,16},{16,0},{32,48},{48,32},{64,80},{80,64},{96,112},{112,96},{1... | collective-permute-start | bytes 25165832 | tf_op jit(solution)/shard_map/ppermute | solution.py:53
  288.3 22.2 %all-to-all-start.2 = ((f32[8,64,576]{2,1,0:T(8,128)}), f32[8,64,576]{2,1,0:T(8,128)}, u32[]{:S(2)}, u32[]{:S(2)}) async-start(f32[8,64,576]{2,1,0:T(8,128)} %select_select_fusion), calls=%async_computation.2 | async-start | bytes 2621440 | tf_op jit(solution)/shard_map/all_to_all | solution.py:132
  292.6 9.6 %copy-start.10 = (f32[512,512]{0,1:T(8,128)S(1)}, f32[512,512]{0,1:T(8,128)}, u32[]{:S(2)}) copy-start(f32[512,512]{0,1:T(8,128)} %convolution_bitcast_fusion.3) | copy-start | bytes 3145732
  304.4 2.0 copy-start.6
  312.0 4.6 %copy-start.4 = (f32[8,64,576]{2,1,0:T(8,128)}, f32[8,64,576]{2,1,0:T(8,128)S(1)}, u32[]{:S(2)}) copy-start(f32[8,64,576]{2,1,0:T(8,128)S(1)} %broadcast_select_fusion) | copy-start | bytes 3538948
  316.6 6.4 %copy-start.1 = (bf16[512,1024]{1,0:T(8,128)(2,1)S(1)}, bf16[512,1024]{1,0:T(8,128)(2,1)}, u32[]{:S(2)}) copy-start(bf16[512,1024]{1,0:T(8,128)(2,1)} %param.9) | copy-start | bytes 3145732
  319.8 0.9 slice-start.2
  321.7 1.3 copy-start.9
Sparse Core Ops, SparseCore 0:
  33.5 57.1 all-gather.1
  131.3 101.8 reduce-scatter.3

commit v11 on v6

--- a/solution.py
+++ b/solution.py
@@ -37,7 +37,21 @@
     w_part = lax.dynamic_slice_in_dim(
         frozen_value_matrix, group_index * part_cols, part_cols, axis=1
     )
-    w_part_full = lax.all_gather(w_part, "fsdp", axis=0, tiled=True)
+    nz = 4 if fsdp_count % 4 == 0 else 1
+    ny = fsdp_count // nz
+    fz, fy = member_index % nz, member_index // nz
+
+    def shift(dy, dz):
+        return [
+            (j, ((j // nz + dy) % ny) * nz + (j % nz + dz) % nz) for j in range(fsdp_count)
+        ]
+
+    zs = [w_part] + [lax.ppermute(w_part, "fsdp", shift(0, t)) for t in range(1, nz)]
+    z_sorted = jnp.take(jnp.stack(zs), (fz - jnp.arange(nz)) % nz, axis=0)
+    ys = [z_sorted] + [lax.ppermute(z_sorted, "fsdp", shift(t, 0)) for t in range(1, ny)]
+    w_part_full = jnp.take(jnp.stack(ys), (fy - jnp.arange(ny)) % ny, axis=0).reshape(
+        width, part_cols
+    )
     up_x = [(i, (i + 2) % dp_count) for i in range(dp_count)]
     down_x = [(i, (i - 2) % dp_count) for i in range(dp_count)]
     from_left = lax.ppermute(w_part_full, "dp", up_x)
@@ -79,7 +93,9 @@
     got = lax.all_to_all(send, "dp", split_axis=0, concat_axis=0, tiled=True)
     my_owner = lax.dynamic_index_in_dim(list_owner, group_index, 0, keepdims=False)
     slab = jnp.take(got, my_owner, axis=0)
+    w_part_full, slab = lax.optimization_barrier((w_part_full, slab))
     shares = lax.all_gather(slab, "fsdp", axis=0, tiled=False)
+    shares, from_left, from_right = lax.optimization_barrier((shares, from_left, from_right))
     full_down = shares[..., :down_cols].transpose(1, 2, 0, 3).reshape(list_len, rank, width)
     full_up = shares[..., down_cols:].transpose(1, 2, 0, 3).reshape(list_len, rank, value_cols)
 

time: 277 us -> 303 us (1.094)
  local copies, waits for them, and re-layouts: 65.8 us -> 77.7 us
  starting transfers between devices: 20.3 us -> 28.4 us
  matrix products: 28.7 us -> 34 us
  other arithmetic: 15.1 us -> 20.4 us
  waiting for transfers between devices: 132 us -> 127 us
    unnamed x4 -> x3, waiting for transfers between devices: 0.05 us -> 42.5 us
    all_gather x1, waiting for transfers between devices: 42.9 us -> 6.51 us  [body(): shares = lax.all_gather(slab, 'fsdp', axis=0, tiled=False)]
    ppermute x0 -> x6, waiting for transfers between devices: none -> 18.3 us  [the longest x3 18.3 us: body(): lax.ppermute(z_sorted, 'fsdp', shift(t, 0))]
    all_gather x1 -> x0, waiting for transfers between devices: 13.4 us -> none  [body(): w_part_full = lax.all_gather(w_part, 'fsdp', axis=0, tiled=True)]
    ppermute x1, waiting for transfers between devices: 44.4 us -> 31.9 us  [body(): from_left = lax.ppermute(w_part_full, 'dp', up_x)]
    ppermute x0 -> x6, starting transfers between devices: none -> 9.2 us  [the longest x3 5.36 us: body(): lax.ppermute(w_part, 'fsdp', shift(0, t))]
    gather x0 -> x3, local copies, waits for them, and re-layouts: none -> 5.68 us  [the longest x2 5.03 us: body(): jnp.take(jnp.stack(ys), (fy - jnp.arange(ny)) % ny, axis=0)]
    optimization_barrier x0 -> x1, local copies, waits for them, and re-layouts: none -> 5.56 us  [body(): lax.optimization_barrier((shares, from_left, from_right))]
  transfers between devices with their start and end apart: 10 -> 15, of which waited for: 7 -> 8; matrix products, arithmetic and copies ran while one was open for 32% -> 21% of each run, Pallas kernels for 0% -> 0%
where the time goes in v11:
time: 303 us; the launch traced here: 302 us
  waiting for transfers between devices  127 us (42%)
  local copies, waits for them, and re-layouts  77.7 us (26%)
  matrix products  34 us (11%)
  starting transfers between devices  28.4 us (9%)
  other arithmetic  20.4 us (7%)
  between operations  14.6 us (5%)
    unnamed x3, waiting for transfers between devices  42.5 us
    ppermute x1, waiting for transfers between devices, body(): from_left = lax.ppermute(w_part_full, 'dp', up_x)  31.9 us
    ppermute x1, waiting for transfers between devices, body(): far_a = lax.ppermute(from_left[:, :half_part], 'dp', up_x)  19.1 us
    ppermute x3, waiting for transfers between devices, body(): lax.ppermute(z_sorted, 'fsdp', shift(t, 0))  18.3 us
    unnamed x44, local copies, waits for them, and re-layouts  17.2 us
    dot_general x1, local copies, waits for them, and re-layouts, body(): lax.dot_general(masked_back, tokens, contract, preferred_element_type=f32)  12 us
    dot_general x1, matrix products, body(): out_own = jnp.dot(tokens, w_own, preferred_element_type=f32)  12 us
    concatenate x1, local copies, waits for them, and re-layouts, body(): jnp.concatenate([part_down, part_up], axis=2)  10.9 us
  transfers between devices with their start and end apart: 15, of which 8 were waited for; matrix products, arithmetic and copies ran while one was open for 21% of the time, Pallas kernels for 0%

profile of v11, /device:TPU:1, one launch (start us, length us, event | category | flops | bytes accessed | tf_op | source)
XLA Modules:
  0.0 301.9 jit_solution(14540116020483810800)
XLA Ops:
  7.2 1.2 copy-done
  8.4 4.7 %collective-permute-start.2 = (bf16[512,128]{1,0:T(8,128)(2,1)S(1)}, bf16[512,128]{1,0:T(8,128)(2,1)S(1)}, u32[]{:S(2)}, u32[]{:S(2)}) collective-permute-start(bf16[512,128]{1,0:T(8,128)(2,1)S(1)} %constant_dynamic-slice_fusion.2), channel_id=1, source_target_pairs={{0,3},{1,0},{2,1},{3,2},{4,7},{5,4},{6,5},{7,6},{8,11},{9,8},{10,9... | collective-permute-start | bytes 393224 | tf_op jit(solution)/shard_map/ppermute | solution.py:49
  13.1 0.7 collective-permute-start
  13.8 0.8 copy.44
  14.7 0.7 gather_fusion.3
  15.9 1.8 gather_fusion.5
  17.7 2.8 gather_fusion.4
  20.7 1.1 maximum_select_fusion
  21.7 5.8 %all-to-all-start = ((bf16[8,64,576]{2,1,0:T(8,128)(2,1)}), bf16[8,64,576]{2,1,0:T(8,128)(2,1)S(1)}, u32[]{:S(2)}, u32[]{:S(2)}) async-start(bf16[8,64,576]{2,1,0:T(8,128)(2,1)} %maximum_select_fusion), calls=%async_computation | async-start | bytes 1310720 | tf_op jit(solution)/shard_map/all_to_all | solution.py:93
  27.9 0.6 gather_fusion
  28.7 2.8 collective-permute-start.5
  31.8 0.7 collective-permute-start.3
  32.6 5.8 %all-to-all-done = bf16[8,64,576]{2,1,0:T(8,128)(2,1)S(1)} async-done(((bf16[8,64,576]{2,1,0:T(8,128)(2,1)}), bf16[8,64,576]{2,1,0:T(8,128)(2,1)S(1)}, u32[]{:S(2)}, u32[]{:S(2)}) %all-to-all-start) | async-done | bytes 589856 | tf_op jit(solution)/shard_map/all_to_all | solution.py:93
  39.0 0.8 broadcast_select_fusion.4
  39.9 14.0 %collective-permute-done.5 = bf16[4,512,128]{2,1,0:T(8,128)(2,1)S(1)} collective-permute-done((bf16[4,512,128]{2,1,0:T(8,128)(2,1)S(1)}, bf16[4,512,128]{2,1,0:T(8,128)(2,1)S(1)}, u32[]{:S(2)}, u32[]{:S(2)}) %collective-permute-start.5) | collective-permute-done | bytes 524320 | tf_op jit(solution)/shard_map/ppermute | solution.py:51
  53.8 4.3 %collective-permute-done.3 = bf16[4,512,128]{2,1,0:T(8,128)(2,1)} collective-permute-done((bf16[4,512,128]{2,1,0:T(8,128)(2,1)S(1)}, bf16[4,512,128]{2,1,0:T(8,128)(2,1)}, u32[]{:S(2)}, u32[]{:S(2)}) %collective-permute-start.3) | collective-permute-done | bytes 524320 | tf_op jit(solution)/shard_map/ppermute | solution.py:51
  58.2 1.6 pad_maximum_fusion.1
  59.8 2.1 gather_fusion.1
  61.9 2.9 copy.57
  64.8 2.6 constant_dynamic-update-slice_fusion.4
  67.5 1.5 collective-permute-start.6
  69.0 1.3 collective-permute-start.8
  70.5 1.3 copy.50
  71.8 12.0 %copy.59 = bf16[8192,512]{1,0:T(8,128)(2,1)} copy(bf16[8192,512]{0,1:T(8,128)(2,1)} %bitcast.123) | data formatting | bytes 16777216 | tf_op jit(solution)/shard_map/dot_general | solution.py:129
  83.9 31.9 %collective-permute-done.6 = bf16[8192,128]{0,1:T(8,128)(2,1)} collective-permute-done((bf16[8192,128]{0,1:T(8,128)(2,1)}, bf16[8192,128]{0,1:T(8,128)(2,1)}, u32[]{:S(2)}, u32[]{:S(2)}) %collective-permute-start.6) | collective-permute-done | bytes 2097184 | tf_op jit(solution)/shard_map/ppermute | solution.py:57
  115.8 6.5 %all-gather.3.cloned.1.call-done = bf16[64,64,576]{2,1,0:T(8,128)(2,1)} async-done(((bf16[4,64,576]{2,1,0:T(8,128)(2,1)}), bf16[64,64,576]{2,1,0:T(8,128)(2,1)}) %all-gather.3.cloned.1.call-update) | async-done | bytes 4718608 | tf_op jit(solution)/shard_map/all_gather | solution.py:97
  122.3 5.6 %copy.47 = bf16[16,4,64,576]{3,0,2,1:T(8,128)(2,1)S(1)} copy(bf16[16,4,64,576]{3,2,1,0:T(8,128)(2,1)} %bitcast.128) | data formatting | bytes 9437184 | tf_op jit(solution)/shard_map/optimization_barrier | solution.py:98
  127.9 1.2 slice_bitcast_fusion
  129.0 2.6 slice.42
  131.6 2.1 reshape_reshape.7
  133.8 1.9 fusion.27
  135.7 6.7 %copy.63 = bf16[32,8,16,512]{3,1,2,0:T(8,128)(2,1)S(1)} copy(bf16[32,8,16,512]{3,2,1,0:T(8,128)(2,1)} %bitcast.122) | data formatting | bytes 8388608
  142.3 5.9 %fusion.26 = f32[256,512]{1,0:T(8,128)S(1)} fusion(bf16[256,8192]{1,0:T(8,128)(2,1)S(1)} %bitcast.129, bf16[512,8192]{1,0:T(8,128)(2,1)} %param.8), kind=kOutput, calls=%fused_computation.157 | convolution fusion | flops 2147483648 | bytes 13107200 | tf_op jit(solution)/shard_map/dot_general | solution.py:112
  148.4 0.7 broadcast_multiply_fusion
  149.6 0.7 convolution_bitcast_fusion.1
  150.3 2.5 convolution_bitcast_fusion
  152.8 5.2 %pad_maximum_fusion = f32[16,256,576]{2,1,0:T(8,128)} fusion(f32[16,256,64]{2,1,0:T(8,128)S(1)} %convolution_bitcast_fusion.1, f32[16,256,512]{2,1,0:T(8,128)S(1)} %convolution_bitcast_fusion), kind=kLoop, calls=%fused_computation.10 | loop fusion | flops 2359296 | bytes 18874368 | tf_op jit(solution)/shard_map/concatenate | solution.py:137
  158.1 10.9 %copy.53 = f32[16,256,576]{1,2,0:T(8,128)} copy(f32[16,256,576]{2,1,0:T(8,128)} %pad_maximum_fusion) | data formatting | bytes 18874368 | tf_op jit(solution)/shard_map/concatenate | solution.py:137
  168.9 1.3 slice.40
  170.2 1.3 collective-permute-start.7
  171.6 1.7 collective-permute-start.9
  173.4 3.1 %constant_dynamic-update-slice_fusion.3 = bf16[8192,512]{0,1:T(8,128)(2,1)} fusion(bf16[8192,512]{0,1:T(8,128)(2,1)} %get-tuple-element.14, bf16[8192,128]{0,1:T(8,128)(2,1)} %collective-permute-done.6), kind=kLoop, calls=%fused_computation.40 | loop fusion | bytes 4194304
  176.4 19.1 %collective-permute-done.7 = bf16[8192,64]{0,1:T(8,128)(2,1)S(1)} collective-permute-done((bf16[8192,64]{0,1:T(8,128)(2,1)S(1)}, bf16[8192,64]{0,1:T(8,128)(2,1)S(1)}, u32[]{:S(2)}, u32[]{:S(2)}) %collective-permute-start.7) | collective-permute-done | bytes 1048608 | tf_op jit(solution)/shard_map/ppermute | solution.py:60
  195.5 1.0 constant_dynamic-update-slice_fusion.2
  196.6 1.0 constant_dynamic-update-slice_fusion.1
  197.6 1.5 constant_dynamic-update-slice_fusion
  199.1 1.6 collective-permute-start.10
  200.9 12.0 %convolution_bitcast_fusion.3 = f32[512,512]{0,1:T(8,128)} fusion(bf16[8192,512]{0,1:T(8,128)(2,1)} %constant_dynamic-update-slice_fusion, bf16[512,8192]{1,0:T(8,128)(2,1)} %param.8), kind=kOutput, calls=%fused_computation.18 | convolution fusion | flops 4294967296 | bytes 17825792 | tf_op jit(solution)/shard_map/dot_general | solution.py:66
  212.9 42.5 %reduce-scatter.4.cloned.1.call-done = f32[1,256,576]{1,2,0:T(8,128)} async-done(((f32[16,256,576]{1,2,0:T(8,128)}), f32[1,256,576]{1,2,0:T(8,128)}) %reduce-scatter.4.cloned.1.call-update) | async-done | bytes 589840
  255.4 1.3 copy.54
  256.7 0.6 gather_fusion.7
  257.3 1.2 select_select_fusion
  258.6 5.9 %all-to-all-start.1 = ((f32[8,64,576]{2,1,0:T(8,128)}), f32[8,64,576]{2,1,0:T(8,128)}, u32[]{:S(2)}, u32[]{:S(2)}) async-start(f32[8,64,576]{2,1,0:T(8,128)} %select_select_fusion), calls=%async_computation.1 | async-start | bytes 2621440 | tf_op jit(solution)/shard_map/all_to_all | solution.py:146
  264.5 9.6 %convolution_bitcast_fusion.2 = f32[512,512]{0,1:T(8,128)S(1)} fusion(bf16[8192,512]{0,1:T(8,128)(2,1)} %collective-permute-done.10, bf16[512,8192]{1,0:T(8,128)(2,1)} %param.8), kind=kOutput, calls=%fused_computation.17 | convolution fusion | flops 4294967296 | bytes 17825792 | tf_op jit(solution)/shard_map/dot_general | solution.py:67
  274.3 2.0 gather_fusion.2
  276.3 2.0 copy.58
  278.4 1.4 add_convert_fusion
  279.8 2.8 all-to-all-done.1
  282.6 1.5 broadcast_select_fusion.1
  284.2 4.5 %broadcast_in_dim.185 = f32[64,64,512]{2,1,0:T(8,128)} broadcast(f32[]{:T(128)} %constant.259.clone.1), dimensions={} | broadcast | bytes 8388612 | tf_op jit(solution)/shard_map/broadcast_in_dim | solution.py:149
  288.7 3.2 %scatter_fusion = f32[64,64,512]{2,1,0:T(8,128)} fusion(f32[64,64,512]{2,1,0:T(8,128)} %broadcast_in_dim.185, s32[8]{0:T(128)S(1)} %get-tuple-element.19, f32[8,64,512]{2,1,0:T(8,128)S(1)} %slice.44), kind=kCustom, calls=%fused_computation.8 | custom fusion | flops 262144 | bytes 3145760 | tf_op jit(solution)/shard_map/scatter-add | solution.py:149
  292.1 0.7 slice-done.2
  292.8 0.9 scatter_fusion.1
  293.8 1.3 copy-done.8
  (91 shorter events, 4.1 us)
Async XLA Ops:
  7.2 1.2 copy-start
  7.2 7.5 %copy-start.2 = (s32[512]{0:T(512)S(1)}, s32[512]{0:T(512)}, u32[]{:S(2)}) copy-start(s32[512]{0:T(512)} %param.15) | copy-start | bytes 6148
  8.4 19.3 %collective-permute-start.2 = (bf16[512,128]{1,0:T(8,128)(2,1)S(1)}, bf16[512,128]{1,0:T(8,128)(2,1)S(1)}, u32[]{:S(2)}, u32[]{:S(2)}) collective-permute-start(bf16[512,128]{1,0:T(8,128)(2,1)S(1)} %constant_dynamic-slice_fusion.2), channel_id=1, source_target_pairs={{0,3},{1,0},{2,1},{3,2},{4,7},{5,4},{6,5},{7,6},{8,11},{9,8},{10,9... | collective-permute-start | bytes 393224 | tf_op jit(solution)/shard_map/ppermute | solution.py:49
  13.1 14.7 %collective-permute-start.1 = (bf16[512,128]{1,0:T(8,128)(2,1)S(1)}, bf16[512,128]{1,0:T(8,128)(2,1)S(1)}, u32[]{:S(2)}, u32[]{:S(2)}) collective-permute-start(bf16[512,128]{1,0:T(8,128)(2,1)S(1)} %constant_dynamic-slice_fusion.2), channel_id=1, source_target_pairs={{0,2},{1,3},{2,0},{3,1},{4,6},{5,7},{6,4},{7,5},{8,10},{9,11},{10,... | collective-permute-start | bytes 393224 | tf_op jit(solution)/shard_map/ppermute | solution.py:49
  13.1 14.7 %collective-permute-start = (bf16[512,128]{1,0:T(8,128)(2,1)S(1)}, bf16[512,128]{1,0:T(8,128)(2,1)S(1)}, u32[]{:S(2)}, u32[]{:S(2)}) collective-permute-start(bf16[512,128]{1,0:T(8,128)(2,1)S(1)} %constant_dynamic-slice_fusion.2), channel_id=1, source_target_pairs={{0,1},{1,2},{2,3},{3,0},{4,5},{5,6},{6,7},{7,4},{8,9},{9,10},{10,1... | collective-permute-start | bytes 393224 | tf_op jit(solution)/shard_map/ppermute | solution.py:49
  21.7 16.7 %all-to-all-start = ((bf16[8,64,576]{2,1,0:T(8,128)(2,1)}), bf16[8,64,576]{2,1,0:T(8,128)(2,1)S(1)}, u32[]{:S(2)}, u32[]{:S(2)}) async-start(bf16[8,64,576]{2,1,0:T(8,128)(2,1)} %maximum_select_fusion), calls=%async_computation | async-start | bytes 1310720 | tf_op jit(solution)/shard_map/all_to_all | solution.py:93
  27.5 94.8 %all-gather.3.cloned.1.call-start = ((), (), s32[]{:S(2)}) async-start(), calls=%async_computation.3 | async-start | bytes 5570560 | tf_op jit(solution)/shard_map/all_gather | solution.py:97
  28.7 25.2 %collective-permute-start.5 = (bf16[4,512,128]{2,1,0:T(8,128)(2,1)S(1)}, bf16[4,512,128]{2,1,0:T(8,128)(2,1)S(1)}, u32[]{:S(2)}, u32[]{:S(2)}) collective-permute-start(bf16[4,512,128]{2,1,0:T(8,128)(2,1)S(1)} %broadcast_select_fusion.3), channel_id=1, source_target_pairs={{0,12},{1,13},{2,14},{3,15},{4,0},{5,1},{6,2},{7,3},{8,4},{9,5},{1... | collective-permute-start | bytes 1572872 | tf_op jit(solution)/shard_map/ppermute | solution.py:51
  31.5 22.4 %collective-permute-start.4 = (bf16[4,512,128]{2,1,0:T(8,128)(2,1)S(1)}, bf16[4,512,128]{2,1,0:T(8,128)(2,1)S(1)}, u32[]{:S(2)}, u32[]{:S(2)}) collective-permute-start(bf16[4,512,128]{2,1,0:T(8,128)(2,1)S(1)} %broadcast_select_fusion.3), channel_id=1, source_target_pairs={{0,8},{1,9},{2,10},{3,11},{4,12},{5,13},{6,14},{7,15},{8,0},{9,1},... | collective-permute-start | bytes 1572872 | tf_op jit(solution)/shard_map/ppermute | solution.py:51
  31.8 26.3 %collective-permute-start.3 = (bf16[4,512,128]{2,1,0:T(8,128)(2,1)S(1)}, bf16[4,512,128]{2,1,0:T(8,128)(2,1)}, u32[]{:S(2)}, u32[]{:S(2)}) collective-permute-start(bf16[4,512,128]{2,1,0:T(8,128)(2,1)S(1)} %broadcast_select_fusion.3), channel_id=1, source_target_pairs={{0,4},{1,5},{2,6},{3,7},{4,8},{5,9},{6,10},{7,11},{8,12},{9,13},{1... | collective-permute-start | bytes 1572872 | tf_op jit(solution)/shard_map/ppermute | solution.py:51
  53.8 4.3 %copy-start.11 = (bf16[4,512,128]{2,1,0:T(8,128)(2,1)}, bf16[4,512,128]{2,1,0:T(8,128)(2,1)S(1)}, u32[]{:S(2)}) copy-start(bf16[4,512,128]{2,1,0:T(8,128)(2,1)S(1)} %collective-permute-done.5) | copy-start | bytes 1572868
  53.8 4.3 %copy-start.12 = (bf16[4,512,128]{2,1,0:T(8,128)(2,1)}, bf16[4,512,128]{2,1,0:T(8,128)(2,1)S(1)}, u32[]{:S(2)}) copy-start(bf16[4,512,128]{2,1,0:T(8,128)(2,1)S(1)} %collective-permute-done.4) | copy-start | bytes 1572868
  64.8 5.4 %copy-start.13 = (s32[1,64]{1,0:T(1,128)S(1)}, s32[1,64]{1,0:T(1,128)}, u32[]{:S(2)}) copy-start(s32[1,64]{1,0:T(1,128)} %param.13) | copy-start | bytes 772
  64.8 5.7 %copy-start.6 = (bf16[512,1024]{1,0:T(8,128)(2,1)S(1)}, bf16[512,1024]{1,0:T(8,128)(2,1)}, u32[]{:S(2)}) copy-start(bf16[512,1024]{1,0:T(8,128)(2,1)} %param.12) | copy-start | bytes 3145732
  67.5 188.0 %reduce-scatter.4.cloned.1.call-start = ((), (), s32[]{:S(2)}) async-start(), calls=%async_computation.4 | async-start | bytes 10027008
  67.5 48.3 %collective-permute-start.6 = (bf16[8192,128]{0,1:T(8,128)(2,1)}, bf16[8192,128]{0,1:T(8,128)(2,1)}, u32[]{:S(2)}, u32[]{:S(2)}) collective-permute-start(bf16[8192,128]{0,1:T(8,128)(2,1)} %get-tuple-element.15), channel_id=1, source_target_pairs={{0,32},{16,48},{32,64},{48,80},{64,96},{80,112},{96,0},{112,16},{1... | collective-permute-start | bytes 6291464 | tf_op jit(solution)/shard_map/ppermute | solution.py:57
  69.0 46.9 %collective-permute-start.8 = (bf16[8192,128]{0,1:T(8,128)(2,1)}, bf16[8192,128]{0,1:T(8,128)(2,1)S(1)}, u32[]{:S(2)}, u32[]{:S(2)}) collective-permute-start(bf16[8192,128]{0,1:T(8,128)(2,1)} %get-tuple-element.15), channel_id=1, source_target_pairs={{0,96},{16,112},{32,0},{48,16},{64,32},{80,48},{96,64},{112,80},{1... | collective-permute-start | bytes 6291464 | tf_op jit(solution)/shard_map/ppermute | solution.py:58
  133.7 8.6 %copy-start.4 = (bf16[256,1024]{1,0:T(8,128)(2,1)}, bf16[256,1024]{1,0:T(8,128)(2,1)S(1)}, u32[]{:S(2)}) copy-start(bf16[256,1024]{1,0:T(8,128)(2,1)S(1)} %reshape_reshape.7) | copy-start | bytes 1572868
  135.6 14.7 %slice-start = ((s8[8388608]{0:T(1024)(128)(4,1)}), s8[4194304]{0:T(1024)(128)(4,1)S(1)}, s32[]{:S(2)}) async-start(s8[8388608]{0:T(1024)(128)(4,1)} %bitcast.119), calls=%async_computation.5 | async-start | bytes 8388608
  142.3 8.0 %slice-start.1 = ((s8[8388608]{0:T(1024)(128)(4,1)}), s8[4194304]{0:T(1024)(128)(4,1)S(1)}, s32[]{:S(2)}) async-start(s8[8388608]{0:T(1024)(128)(4,1)} %bitcast.119), calls=%async_computation.6 | async-start | bytes 8388608
  148.2 1.3 copy-start.7
  170.2 25.3 %collective-permute-start.7 = (bf16[8192,64]{0,1:T(8,128)(2,1)S(1)}, bf16[8192,64]{0,1:T(8,128)(2,1)S(1)}, u32[]{:S(2)}, u32[]{:S(2)}) collective-permute-start(bf16[8192,64]{0,1:T(8,128)(2,1)S(1)} %slice.40), channel_id=1, source_target_pairs={{0,32},{16,48},{32,64},{48,80},{64,96},{80,112},{96,0},{112,16},{1... | collective-permute-start | bytes 3145736 | tf_op jit(solution)/shard_map/ppermute | solution.py:60
  171.6 25.0 %collective-permute-start.9 = (bf16[8192,64]{0,1:T(8,128)(2,1)S(1)}, bf16[8192,64]{0,1:T(8,128)(2,1)S(1)}, u32[]{:S(2)}, u32[]{:S(2)}) collective-permute-start(bf16[8192,64]{0,1:T(8,128)(2,1)S(1)} %slice.41), channel_id=1, source_target_pairs={{0,96},{16,112},{32,0},{48,16},{64,32},{80,48},{96,64},{112,80},{1... | collective-permute-start | bytes 3145736 | tf_op jit(solution)/shard_map/ppermute | solution.py:61
  199.1 65.5 %collective-permute-start.10 = (bf16[8192,512]{0,1:T(8,128)(2,1)}, bf16[8192,512]{0,1:T(8,128)(2,1)}, u32[]{:S(2)}, u32[]{:S(2)}) collective-permute-start(bf16[8192,512]{0,1:T(8,128)(2,1)} %constant_dynamic-update-slice_fusion), channel_id=1, source_target_pairs={{0,16},{16,0},{32,48},{48,32},{64,80},{80,64},{96,112},{112,96},{1... | collective-permute-start | bytes 25165832 | tf_op jit(solution)/shard_map/ppermute | solution.py:65
  258.6 24.0 %all-to-all-start.1 = ((f32[8,64,576]{2,1,0:T(8,128)}), f32[8,64,576]{2,1,0:T(8,128)}, u32[]{:S(2)}, u32[]{:S(2)}) async-start(f32[8,64,576]{2,1,0:T(8,128)} %select_select_fusion), calls=%async_computation.1 | async-start | bytes 2621440 | tf_op jit(solution)/shard_map/all_to_all | solution.py:146
  264.5 9.6 %copy-start.10 = (f32[512,512]{0,1:T(8,128)S(1)}, f32[512,512]{0,1:T(8,128)}, u32[]{:S(2)}) copy-start(f32[512,512]{0,1:T(8,128)} %convolution_bitcast_fusion.3) | copy-start | bytes 3145732
  276.3 2.0 copy-start.5
  276.3 2.0 copy-start.9
  284.0 4.6 %copy-start.3 = (f32[8,64,576]{2,1,0:T(8,128)}, f32[8,64,576]{2,1,0:T(8,128)S(1)}, u32[]{:S(2)}) copy-start(f32[8,64,576]{2,1,0:T(8,128)S(1)} %broadcast_select_fusion.1) | copy-start | bytes 3538948
  288.7 6.4 %copy-start.1 = (bf16[512,1024]{1,0:T(8,128)(2,1)S(1)}, bf16[512,1024]{1,0:T(8,128)(2,1)}, u32[]{:S(2)}) copy-start(bf16[512,1024]{1,0:T(8,128)(2,1)} %param.9) | copy-start | bytes 3145732
  291.9 0.9 slice-start.2
  293.7 1.3 copy-start.8
Sparse Core Ops, SparseCore 0:
  67.6 54.6 all-gather.2
  169.1 86.2 reduce-scatter.3

commit v12 on v9

--- a/solution.py
+++ b/solution.py
@@ -37,7 +37,21 @@
     w_part = lax.dynamic_slice_in_dim(
         frozen_value_matrix, group_index * part_cols, part_cols, axis=1
     )
+    nz = 4 if fsdp_count % 4 == 0 else 1
+    ny = fsdp_count // nz
+    fz, fy = member_index % nz, member_index // nz
 
+    def shift(dy, dz):
+        return [
+            (j, ((j // nz + dy) % ny) * nz + (j % nz + dz) % nz) for j in range(fsdp_count)
+        ]
+
+    zs = [w_part] + [lax.ppermute(w_part, "fsdp", shift(0, t)) for t in range(1, nz)]
+    z_sorted = jnp.take(jnp.stack(zs), (fz - jnp.arange(nz)) % nz, axis=0)
+    ys = [z_sorted] + [lax.ppermute(z_sorted, "fsdp", shift(t, 0)) for t in range(1, ny)]
+    w_part_full = jnp.take(jnp.stack(ys), (fy - jnp.arange(ny)) % ny, axis=0).reshape(
+        width, part_cols
+    )
     list_slot = jnp.take(composer_storage_index, needed_composers, axis=0)
     list_owner = list_slot // each_owner_rows
     list_local = list_slot % each_owner_rows
@@ -55,29 +69,20 @@
     got = lax.all_to_all(send, "dp", split_axis=0, concat_axis=0, tiled=True)
     my_owner = lax.dynamic_index_in_dim(list_owner, group_index, 0, keepdims=False)
     slab = jnp.take(got, my_owner, axis=0)
-    slab_size = rank * slab.shape[2]
-    w_slabs = -(-w_part.size // slab_size)
-    w_flat = jnp.pad(w_part.reshape(-1), (0, w_slabs * slab_size - w_part.size))
-    buf = jnp.concatenate([slab, w_flat.reshape(w_slabs, rank, slab.shape[2])], axis=0)
-    gathered = lax.all_gather(buf, "fsdp", axis=0, tiled=False)
-    shares = gathered[:, :list_len]
-    w_part_full = (
-        gathered[:, list_len:]
-        .reshape(fsdp_count, w_slabs * slab_size)[:, : w_part.size]
-        .reshape(width, part_cols)
-    )
+    shares = lax.all_gather(slab, "fsdp", axis=0, tiled=False)
+    shares, w_part_ready = lax.optimization_barrier((shares, w_part_full))
     full_down = shares[..., :down_cols].transpose(1, 2, 0, 3).reshape(list_len, rank, width)
     full_up = shares[..., down_cols:].transpose(1, 2, 0, 3).reshape(list_len, rank, value_cols)
 
     up_x = [(i, (i + 2) % dp_count) for i in range(dp_count)]
     down_x = [(i, (i - 2) % dp_count) for i in range(dp_count)]
-    from_left = lax.ppermute(w_part_full, "dp", up_x)
-    from_right = lax.ppermute(w_part_full, "dp", down_x)
+    from_left = lax.ppermute(w_part_ready, "dp", up_x)
+    from_right = lax.ppermute(w_part_ready, "dp", down_x)
     half_part = part_cols // 2
     far_a = lax.ppermute(from_left[:, :half_part], "dp", up_x)
     far_b = lax.ppermute(from_right[:, half_part:], "dp", down_x)
     far = jnp.concatenate([far_a, far_b], axis=1)
-    same_parity = [w_part_full, from_left, far, from_right]
+    same_parity = [w_part_ready, from_left, far, from_right]
     w_own = jnp.concatenate(same_parity, axis=1)
     w_partner = lax.ppermute(w_own, "dp", [(i, i ^ 1) for i in range(dp_count)])
     out_own = jnp.dot(tokens, w_own, preferred_element_type=f32)

time: 318 us -> 294 us (0.925)
  local copies, waits for them, and re-layouts: 97.6 us -> 79 us
  waiting for transfers between devices: 136 us -> 119 us
  starting transfers between devices: 18.8 us -> 27.1 us
    all_gather x1, waiting for transfers between devices: 56.6 us -> 19.8 us  [body(): shares = lax.all_gather(slab, 'fsdp', axis=0, tiled=False)]
    ppermute x2 -> x8, waiting for transfers between devices: 44.3 us -> 67.3 us  [the longest x1 45.1 us: body(): from_left = lax.ppermute(w_part_ready, 'dp', up_x)]
    ppermute x1, waiting for transfers between devices: 18.2 us -> 0.01 us  [body(): far_b = lax.ppermute(from_right[:, half_part:], 'dp', down_x)]
    ppermute x1, waiting for transfers between devices: 3.38 us -> 18.7 us  [body(): far_a = lax.ppermute(from_left[:, :half_part], 'dp', up_x)]
    concatenate x1, local copies, waits for them, and re-layouts: 14.4 us -> 1.46 us  [body(): w_own = jnp.concatenate(same_parity, axis=1)]
    transpose x0 -> x4, local copies, waits for them, and re-layouts: none -> 12.4 us  [the longest x2 9.46 us: body(): shares[..., :down_cols].transpose(1, 2, 0, 3).reshape(list_len, rank, width)]
    slice x4 -> x0, local copies, waits for them, and re-layouts: 9.06 us -> none  [the longest x2 5 us: body(): gathered[:, list_len:].reshape(fsdp_count, w_slabs * slab_size)]
    ppermute x2 -> x8, starting transfers between devices: 2.5 us -> 11.1 us  [the longest x3 4.53 us: body(): lax.ppermute(w_part, 'fsdp', shift(0, t))]
  transfers between devices with their start and end apart: 9 -> 15, of which waited for: 6 -> 9; matrix products, arithmetic and copies ran while one was open for 26% -> 21% of each run, Pallas kernels for 0% -> 0%
where the time goes in v12:
time: 294 us; the launch traced here: 293 us
  waiting for transfers between devices  119 us (40%)
  local copies, waits for them, and re-layouts  79 us (27%)
  matrix products  33.3 us (11%)
  starting transfers between devices  27.1 us (9%)
  other arithmetic  19.7 us (7%)
  between operations  14.6 us (5%)
    ppermute x1, waiting for transfers between devices, body(): from_left = lax.ppermute(w_part_ready, 'dp', up_x)  45.1 us
    all_gather x1, waiting for transfers between devices, body(): shares = lax.all_gather(slab, 'fsdp', axis=0, tiled=False)  19.8 us
    ppermute x1, waiting for transfers between devices, body(): far_a = lax.ppermute(from_left[:, :half_part], 'dp', up_x)  18.7 us
    unnamed x47, local copies, waits for them, and re-layouts  15.5 us
    ppermute x3, waiting for transfers between devices, body(): lax.ppermute(z_sorted, 'fsdp', shift(t, 0))  14.1 us
    dot_general x1, local copies, waits for them, and re-layouts, body(): lax.dot_general(masked_back, tokens, contract, preferred_element_type=f32)  11.9 us
    dot_general x1, matrix products, body(): out_own = jnp.dot(tokens, w_own, preferred_element_type=f32)  11.5 us
    concatenate x1, local copies, waits for them, and re-layouts, body(): jnp.concatenate([part_down, part_up], axis=2)  10.9 us
  transfers between devices with their start and end apart: 15, of which 9 were waited for; matrix products, arithmetic and copies ran while one was open for 21% of the time, Pallas kernels for 0%

profile of v12, /device:TPU:1, one launch (start us, length us, event | category | flops | bytes accessed | tf_op | source)
XLA Modules:
  0.0 293.1 jit_solution(3445082777289511545)
XLA Ops:
  7.2 0.8 copy.42
  8.1 0.7 gather_fusion
  9.4 1.8 gather_fusion.2
  11.2 2.8 gather_fusion.1
  14.2 1.1 maximum_select_fusion
  15.2 5.8 %all-to-all-start = ((bf16[8,64,576]{2,1,0:T(8,128)(2,1)}), bf16[8,64,576]{2,1,0:T(8,128)(2,1)S(1)}, u32[]{:S(2)}, u32[]{:S(2)}) async-start(bf16[8,64,576]{2,1,0:T(8,128)(2,1)} %maximum_select_fusion), calls=%async_computation | async-start | bytes 1310720 | tf_op jit(solution)/shard_map/all_to_all | solution.py:69
  21.1 10.9 %all-to-all-done = bf16[8,64,576]{2,1,0:T(8,128)(2,1)S(1)} async-done(((bf16[8,64,576]{2,1,0:T(8,128)(2,1)}), bf16[8,64,576]{2,1,0:T(8,128)(2,1)S(1)}, u32[]{:S(2)}, u32[]{:S(2)}) %all-to-all-start) | async-done | bytes 589856 | tf_op jit(solution)/shard_map/all_to_all | solution.py:69
  32.5 0.8 bitcast_select_fusion.1
  33.5 3.8 %collective-permute-start.2 = (bf16[512,128]{1,0:T(8,128)(2,1)S(1)}, bf16[512,128]{1,0:T(8,128)(2,1)S(1)}, u32[]{:S(2)}, u32[]{:S(2)}) collective-permute-start(bf16[512,128]{1,0:T(8,128)(2,1)S(1)} %constant_dynamic-slice_fusion.1), channel_id=1, source_target_pairs={{0,3},{1,0},{2,1},{3,2},{4,7},{5,4},{6,5},{7,6},{8,11},{9,8},{10,9... | collective-permute-start | bytes 393224 | tf_op jit(solution)/shard_map/ppermute | solution.py:49
  37.3 0.7 collective-permute-start
  38.3 4.5 %collective-permute-done.2 = bf16[512,128]{1,0:T(8,128)(2,1)S(1)} collective-permute-done((bf16[512,128]{1,0:T(8,128)(2,1)S(1)}, bf16[512,128]{1,0:T(8,128)(2,1)S(1)}, u32[]{:S(2)}, u32[]{:S(2)}) %collective-permute-start.2) | collective-permute-done | bytes 131104 | tf_op jit(solution)/shard_map/ppermute | solution.py:49
  42.9 3.5 %collective-permute-done = bf16[512,128]{1,0:T(8,128)(2,1)S(1)} collective-permute-done((bf16[512,128]{1,0:T(8,128)(2,1)S(1)}, bf16[512,128]{1,0:T(8,128)(2,1)S(1)}, u32[]{:S(2)}, u32[]{:S(2)}) %collective-permute-start) | collective-permute-done | bytes 131104 | tf_op jit(solution)/shard_map/ppermute | solution.py:49
  46.5 0.6 gather_fusion.4
  47.3 2.8 collective-permute-start.5
  50.4 0.7 collective-permute-start.3
  51.2 1.3 copy.50
  52.6 11.9 %copy.59 = bf16[8192,512]{1,0:T(8,128)(2,1)} copy(bf16[8192,512]{0,1:T(8,128)(2,1)} %bitcast.125) | data formatting | bytes 16777216 | tf_op jit(solution)/shard_map/dot_general | solution.py:128
  64.6 10.8 %collective-permute-done.5 = bf16[4,512,128]{2,1,0:T(8,128)(2,1)S(1)} collective-permute-done((bf16[4,512,128]{2,1,0:T(8,128)(2,1)S(1)}, bf16[4,512,128]{2,1,0:T(8,128)(2,1)S(1)}, u32[]{:S(2)}, u32[]{:S(2)}) %collective-permute-start.5) | collective-permute-done | bytes 524320 | tf_op jit(solution)/shard_map/ppermute | solution.py:51
  75.5 3.3 %collective-permute-done.3 = bf16[4,512,128]{2,1,0:T(8,128)(2,1)} collective-permute-done((bf16[4,512,128]{2,1,0:T(8,128)(2,1)S(1)}, bf16[4,512,128]{2,1,0:T(8,128)(2,1)}, u32[]{:S(2)}, u32[]{:S(2)}) %collective-permute-start.3) | collective-permute-done | bytes 524320 | tf_op jit(solution)/shard_map/ppermute | solution.py:51
  78.8 1.6 pad_maximum_fusion.1
  80.4 2.1 gather_fusion.5
  82.5 4.0 %copy.57 = bf16[8192,128]{0,1:T(8,128)(2,1)} copy(bf16[8192,128]{1,0:T(8,128)(2,1)} %bitcast.129) | data formatting | bytes 4194304 | tf_op jit(solution)/shard_map/jit(_take)/gather | solution.py:52
  86.5 1.8 broadcast_select_fusion
  88.4 19.8 %all-gather.2.cloned.1.call-done = bf16[16,4,64,576]{3,2,1,0:T(8,128)(2,1)} async-done(((bf16[1,4,64,576]{3,2,1,0:T(8,128)(2,1)}), bf16[16,4,64,576]{3,2,1,0:T(8,128)(2,1)}) %all-gather.2.cloned.1.call-update) | async-done | bytes 4718608 | tf_op jit(solution)/shard_map/all_gather | solution.py:72
  108.1 1.3 slice_bitcast_fusion.1
  109.5 4.7 %slice_bitcast_fusion = bf16[4,64,16,512]{3,1,0,2:T(8,128)(2,1)} fusion(bf16[16,4,64,576]{3,2,1,0:T(8,128)(2,1)} %all-gather.2.cloned.1.call-done), kind=kLoop, calls=%fused_computation.11 | loop fusion | bytes 8388608 | tf_op jit(solution)/shard_map/transpose | solution.py:74
  114.2 1.6 copy.48
  115.8 2.1 reshape_reshape.7
  118.0 1.9 fusion.27
  119.9 4.7 %copy.47 = bf16[4,64,16,512]{3,2,1,0:T(8,128)(2,1)S(1)} copy(bf16[4,64,16,512]{3,1,0,2:T(8,128)(2,1)} %slice_bitcast_fusion) | data formatting | bytes 8388608 | tf_op jit(solution)/shard_map/transpose | solution.py:74
  124.7 6.3 %copy.63 = bf16[32,8,16,512]{3,1,2,0:T(8,128)(2,1)} copy(bf16[32,8,16,512]{3,2,1,0:T(8,128)(2,1)S(1)} %bitcast.124) | data formatting | bytes 8388608
  131.0 5.4 %fusion.26 = f32[256,512]{1,0:T(8,128)S(1)} fusion(bf16[256,8192]{1,0:T(8,128)(2,1)} %bitcast.132, bf16[512,8192]{1,0:T(8,128)(2,1)S(1)} %bitcast.127), kind=kOutput, calls=%fused_computation.158 | convolution fusion | flops 2147483648 | bytes 13107200 | tf_op jit(solution)/shard_map/dot_general | solution.py:111
  136.6 0.8 broadcast_multiply_fusion
  137.8 0.7 convolution_bitcast_fusion.1
  138.5 2.7 convolution_bitcast_fusion
  141.3 5.2 %pad_maximum_fusion = f32[16,256,576]{2,1,0:T(8,128)} fusion(f32[16,256,64]{2,1,0:T(8,128)S(1)} %convolution_bitcast_fusion.1, f32[16,256,512]{2,1,0:T(8,128)S(1)} %convolution_bitcast_fusion), kind=kLoop, calls=%fused_computation.10 | loop fusion | flops 2359296 | bytes 18874368 | tf_op jit(solution)/shard_map/concatenate | solution.py:136
  146.5 10.9 %copy.53 = f32[16,256,576]{1,2,0:T(8,128)} copy(f32[16,256,576]{2,1,0:T(8,128)} %pad_maximum_fusion) | data formatting | bytes 18874368 | tf_op jit(solution)/shard_map/concatenate | solution.py:136
  157.4 1.2 collective-permute-start.6
  158.6 1.5 collective-permute-start.8
  160.1 45.1 %collective-permute-done.6 = bf16[8192,128]{0,1:T(8,128)(2,1)S(1)} collective-permute-done((bf16[8192,128]{0,1:T(8,128)(2,1)S(1)}, bf16[8192,128]{0,1:T(8,128)(2,1)S(1)}, u32[]{:S(2)}, u32[]{:S(2)}) %collective-permute-start.6) | collective-permute-done | bytes 2097184 | tf_op jit(solution)/shard_map/ppermute | solution.py:79
  205.4 1.5 constant_dynamic-update-slice_fusion.4
  207.0 2.7 collective-permute-start.9
  209.7 1.5 constant_dynamic-update-slice_fusion.3
  211.2 18.7 %collective-permute-done.7 = bf16[8192,64]{0,1:T(8,128)(2,1)S(1)} collective-permute-done((bf16[8192,64]{0,1:T(8,128)(2,1)S(1)}, bf16[8192,64]{0,1:T(8,128)(2,1)S(1)}, u32[]{:S(2)}, u32[]{:S(2)}) %collective-permute-start.7) | collective-permute-done | bytes 1048608 | tf_op jit(solution)/shard_map/ppermute | solution.py:82
  229.8 1.0 constant_dynamic-update-slice_fusion.2
  230.9 1.0 constant_dynamic-update-slice_fusion.1
  231.9 1.5 constant_dynamic-update-slice_fusion
  233.4 2.4 collective-permute-start.10
  236.0 11.5 %convolution_bitcast_fusion.3 = f32[512,512]{0,1:T(8,128)} fusion(bf16[8192,512]{0,1:T(8,128)(2,1)} %constant_dynamic-update-slice_fusion, bf16[512,8192]{1,0:T(8,128)(2,1)} %param.8), kind=kOutput, calls=%fused_computation.19 | convolution fusion | flops 4294967296 | bytes 17825792 | tf_op jit(solution)/shard_map/dot_general | solution.py:88
  247.5 1.3 copy.54
  248.8 0.6 gather_fusion.7
  249.4 1.2 select_select_fusion
  250.7 5.0 %all-to-all-start.1 = ((f32[8,64,576]{2,1,0:T(8,128)}), f32[8,64,576]{2,1,0:T(8,128)}, u32[]{:S(2)}, u32[]{:S(2)}) async-start(f32[8,64,576]{2,1,0:T(8,128)} %select_select_fusion), calls=%async_computation.1 | async-start | bytes 2621440 | tf_op jit(solution)/shard_map/all_to_all | solution.py:145
  255.6 9.6 %convolution_bitcast_fusion.2 = f32[512,512]{0,1:T(8,128)S(1)} fusion(bf16[8192,512]{0,1:T(8,128)(2,1)} %collective-permute-done.10, bf16[512,8192]{1,0:T(8,128)(2,1)} %param.8), kind=kOutput, calls=%fused_computation.18 | convolution fusion | flops 4294967296 | bytes 17825792 | tf_op jit(solution)/shard_map/dot_general | solution.py:89
  265.4 2.0 gather_fusion.6
  267.4 2.0 copy.58
  269.5 1.4 add_convert_fusion
  270.9 2.8 all-to-all-done.1
  273.7 1.5 broadcast_select_fusion.1
  275.3 4.5 %broadcast_in_dim.185 = f32[64,64,512]{2,1,0:T(8,128)} broadcast(f32[]{:T(128)} %constant.259.clone.1), dimensions={} | broadcast | bytes 8388612 | tf_op jit(solution)/shard_map/broadcast_in_dim | solution.py:148
  279.8 3.3 %scatter_fusion = f32[64,64,512]{2,1,0:T(8,128)} fusion(f32[64,64,512]{2,1,0:T(8,128)} %broadcast_in_dim.185, s32[8]{0:T(128)S(1)} %get-tuple-element.17, f32[8,64,512]{2,1,0:T(8,128)S(1)} %slice.42), kind=kCustom, calls=%fused_computation.8 | custom fusion | flops 262144 | bytes 3145760 | tf_op jit(solution)/shard_map/scatter-add | solution.py:148
  283.3 0.7 slice-done.4
  284.0 0.9 scatter_fusion.1
  284.9 1.3 copy-done.8
  (97 shorter events, 4.2 us)
Async XLA Ops:
  7.2 26.3 %copy-start = (bf16[512,1024]{1,0:T(8,128)(2,1)S(1)}, bf16[512,1024]{1,0:T(8,128)(2,1)}, u32[]{:S(2)}) copy-start(bf16[512,1024]{1,0:T(8,128)(2,1)} %param.9) | copy-start | bytes 3145732
  7.2 1.0 copy-start.2
  14.2 23.9 %copy-start.12 = (s32[1,64]{1,0:T(1,128)S(1)}, s32[1,64]{1,0:T(1,128)}, u32[]{:S(2)}) copy-start(s32[1,64]{1,0:T(1,128)} %param.13) | copy-start | bytes 772
  15.2 16.7 %all-to-all-start = ((bf16[8,64,576]{2,1,0:T(8,128)(2,1)}), bf16[8,64,576]{2,1,0:T(8,128)(2,1)S(1)}, u32[]{:S(2)}, u32[]{:S(2)}) async-start(bf16[8,64,576]{2,1,0:T(8,128)(2,1)} %maximum_select_fusion), calls=%async_computation | async-start | bytes 1310720 | tf_op jit(solution)/shard_map/all_to_all | solution.py:69
  21.0 87.1 %all-gather.2.cloned.1.call-start = ((), (), s32[]{:S(2)}) async-start(), calls=%async_computation.3 | async-start | bytes 5570560 | tf_op jit(solution)/shard_map/all_gather | solution.py:72
  33.4 17.9 %copy-start.6 = (bf16[512,1024]{1,0:T(8,128)(2,1)S(1)}, bf16[512,1024]{1,0:T(8,128)(2,1)}, u32[]{:S(2)}) copy-start(bf16[512,1024]{1,0:T(8,128)(2,1)} %param.12) | copy-start | bytes 3145732
  33.4 214.1 %reduce-scatter.4.cloned.1.call-start = ((), (), s32[]{:S(2)}) async-start(), calls=%async_computation.4 | async-start | bytes 10027008
  33.5 9.4 %collective-permute-start.2 = (bf16[512,128]{1,0:T(8,128)(2,1)S(1)}, bf16[512,128]{1,0:T(8,128)(2,1)S(1)}, u32[]{:S(2)}, u32[]{:S(2)}) collective-permute-start(bf16[512,128]{1,0:T(8,128)(2,1)S(1)} %constant_dynamic-slice_fusion.1), channel_id=1, source_target_pairs={{0,3},{1,0},{2,1},{3,2},{4,7},{5,4},{6,5},{7,6},{8,11},{9,8},{10,9... | collective-permute-start | bytes 393224 | tf_op jit(solution)/shard_map/ppermute | solution.py:49
  37.3 5.6 %collective-permute-start.1 = (bf16[512,128]{1,0:T(8,128)(2,1)S(1)}, bf16[512,128]{1,0:T(8,128)(2,1)S(1)}, u32[]{:S(2)}, u32[]{:S(2)}) collective-permute-start(bf16[512,128]{1,0:T(8,128)(2,1)S(1)} %constant_dynamic-slice_fusion.1), channel_id=1, source_target_pairs={{0,2},{1,3},{2,0},{3,1},{4,6},{5,7},{6,4},{7,5},{8,10},{9,11},{10,... | collective-permute-start | bytes 393224 | tf_op jit(solution)/shard_map/ppermute | solution.py:49
  37.3 9.1 %collective-permute-start = (bf16[512,128]{1,0:T(8,128)(2,1)S(1)}, bf16[512,128]{1,0:T(8,128)(2,1)S(1)}, u32[]{:S(2)}, u32[]{:S(2)}) collective-permute-start(bf16[512,128]{1,0:T(8,128)(2,1)S(1)} %constant_dynamic-slice_fusion.1), channel_id=1, source_target_pairs={{0,1},{1,2},{2,3},{3,0},{4,5},{5,6},{6,7},{7,4},{8,9},{9,10},{10,1... | collective-permute-start | bytes 393224 | tf_op jit(solution)/shard_map/ppermute | solution.py:49
  47.3 28.2 %collective-permute-start.5 = (bf16[4,512,128]{2,1,0:T(8,128)(2,1)S(1)}, bf16[4,512,128]{2,1,0:T(8,128)(2,1)S(1)}, u32[]{:S(2)}, u32[]{:S(2)}) collective-permute-start(bf16[4,512,128]{2,1,0:T(8,128)(2,1)S(1)} %broadcast_select_fusion.2), channel_id=1, source_target_pairs={{0,12},{1,13},{2,14},{3,15},{4,0},{5,1},{6,2},{7,3},{8,4},{9,5},{1... | collective-permute-start | bytes 1572872 | tf_op jit(solution)/shard_map/ppermute | solution.py:51
  50.1 25.4 %collective-permute-start.4 = (bf16[4,512,128]{2,1,0:T(8,128)(2,1)S(1)}, bf16[4,512,128]{2,1,0:T(8,128)(2,1)}, u32[]{:S(2)}, u32[]{:S(2)}) collective-permute-start(bf16[4,512,128]{2,1,0:T(8,128)(2,1)S(1)} %broadcast_select_fusion.2), channel_id=1, source_target_pairs={{0,8},{1,9},{2,10},{3,11},{4,12},{5,13},{6,14},{7,15},{8,0},{9,1},... | collective-permute-start | bytes 1572872 | tf_op jit(solution)/shard_map/ppermute | solution.py:51
  50.4 28.4 %collective-permute-start.3 = (bf16[4,512,128]{2,1,0:T(8,128)(2,1)S(1)}, bf16[4,512,128]{2,1,0:T(8,128)(2,1)}, u32[]{:S(2)}, u32[]{:S(2)}) collective-permute-start(bf16[4,512,128]{2,1,0:T(8,128)(2,1)S(1)} %broadcast_select_fusion.2), channel_id=1, source_target_pairs={{0,4},{1,5},{2,6},{3,7},{4,8},{5,9},{6,10},{7,11},{8,12},{9,13},{1... | collective-permute-start | bytes 1572872 | tf_op jit(solution)/shard_map/ppermute | solution.py:51
  75.5 3.3 %copy-start.11 = (bf16[4,512,128]{2,1,0:T(8,128)(2,1)}, bf16[4,512,128]{2,1,0:T(8,128)(2,1)S(1)}, u32[]{:S(2)}) copy-start(bf16[4,512,128]{2,1,0:T(8,128)(2,1)S(1)} %collective-permute-done.5) | copy-start | bytes 1572868
  118.0 6.7 %copy-start.4 = (bf16[256,1024]{1,0:T(8,128)(2,1)}, bf16[256,1024]{1,0:T(8,128)(2,1)S(1)}, u32[]{:S(2)}) copy-start(bf16[256,1024]{1,0:T(8,128)(2,1)S(1)} %reshape_reshape.7) | copy-start | bytes 1572868
  118.0 13.0 %slice-start.2 = ((s8[8388608]{0:T(1024)(128)(4,1)}), s8[4194304]{0:T(1024)(128)(4,1)S(1)}, s32[]{:S(2)}) async-start(s8[8388608]{0:T(1024)(128)(4,1)} %bitcast.126), calls=%async_computation.7 | async-start | bytes 8388608
  119.9 11.1 %slice-start.3 = ((s8[8388608]{0:T(1024)(128)(4,1)}), s8[4194304]{0:T(1024)(128)(4,1)S(1)}, s32[]{:S(2)}) async-start(s8[8388608]{0:T(1024)(128)(4,1)} %bitcast.126), calls=%async_computation.8 | async-start | bytes 8388608
  124.7 13.8 %slice-start = ((s8[8388608]{0:T(1024)(128)(4,1)}), s8[4194304]{0:T(1024)(128)(4,1)S(1)}, s32[]{:S(2)}) async-start(s8[8388608]{0:T(1024)(128)(4,1)} %bitcast.121), calls=%async_computation.5 | async-start | bytes 8388608
  131.0 7.5 %slice-start.1 = ((s8[8388608]{0:T(1024)(128)(4,1)}), s8[4194304]{0:T(1024)(128)(4,1)S(1)}, s32[]{:S(2)}) async-start(s8[8388608]{0:T(1024)(128)(4,1)} %bitcast.121), calls=%async_computation.6 | async-start | bytes 8388608
  136.4 1.3 copy-start.7
  157.4 47.9 %collective-permute-start.6 = (bf16[8192,128]{0,1:T(8,128)(2,1)S(1)}, bf16[8192,128]{0,1:T(8,128)(2,1)S(1)}, u32[]{:S(2)}, u32[]{:S(2)}) collective-permute-start(bf16[8192,128]{0,1:T(8,128)(2,1)S(1)} %broadcast_select_fusion), channel_id=1, source_target_pairs={{0,32},{16,48},{32,64},{48,80},{64,96},{80,112},{96,0},{112,16},{1... | collective-permute-start | bytes 6291464 | tf_op jit(solution)/shard_map/ppermute | solution.py:79
  158.6 48.3 %collective-permute-start.8 = (bf16[8192,128]{0,1:T(8,128)(2,1)S(1)}, bf16[8192,128]{0,1:T(8,128)(2,1)S(1)}, u32[]{:S(2)}, u32[]{:S(2)}) collective-permute-start(bf16[8192,128]{0,1:T(8,128)(2,1)S(1)} %broadcast_select_fusion), channel_id=1, source_target_pairs={{0,96},{16,112},{32,0},{48,16},{64,32},{80,48},{96,64},{112,80},{1... | collective-permute-start | bytes 6291464 | tf_op jit(solution)/shard_map/ppermute | solution.py:80
  205.3 24.5 %collective-permute-start.7 = (bf16[8192,64]{0,1:T(8,128)(2,1)S(1)}, bf16[8192,64]{0,1:T(8,128)(2,1)S(1)}, u32[]{:S(2)}, u32[]{:S(2)}) collective-permute-start(bf16[8192,64]{0,1:T(8,128)(2,1)S(1)} %slice.40), channel_id=1, source_target_pairs={{0,32},{16,48},{32,64},{48,80},{64,96},{80,112},{96,0},{112,16},{1... | collective-permute-start | bytes 3145736 | tf_op jit(solution)/shard_map/ppermute | solution.py:82
  207.0 23.9 %collective-permute-start.9 = (bf16[8192,64]{0,1:T(8,128)(2,1)S(1)}, bf16[8192,64]{0,1:T(8,128)(2,1)S(1)}, u32[]{:S(2)}, u32[]{:S(2)}) collective-permute-start(bf16[8192,64]{0,1:T(8,128)(2,1)S(1)} %slice.41), channel_id=1, source_target_pairs={{0,96},{16,112},{32,0},{48,16},{64,32},{80,48},{96,64},{112,80},{1... | collective-permute-start | bytes 3145736 | tf_op jit(solution)/shard_map/ppermute | solution.py:83
  233.4 22.3 %collective-permute-start.10 = (bf16[8192,512]{0,1:T(8,128)(2,1)}, bf16[8192,512]{0,1:T(8,128)(2,1)}, u32[]{:S(2)}, u32[]{:S(2)}) collective-permute-start(bf16[8192,512]{0,1:T(8,128)(2,1)} %constant_dynamic-update-slice_fusion), channel_id=1, source_target_pairs={{0,16},{16,0},{32,48},{48,32},{64,80},{80,64},{96,112},{112,96},{1... | collective-permute-start | bytes 25165832 | tf_op jit(solution)/shard_map/ppermute | solution.py:87
  250.7 23.0 %all-to-all-start.1 = ((f32[8,64,576]{2,1,0:T(8,128)}), f32[8,64,576]{2,1,0:T(8,128)}, u32[]{:S(2)}, u32[]{:S(2)}) async-start(f32[8,64,576]{2,1,0:T(8,128)} %select_select_fusion), calls=%async_computation.1 | async-start | bytes 2621440 | tf_op jit(solution)/shard_map/all_to_all | solution.py:145
  255.6 9.6 %copy-start.10 = (f32[512,512]{0,1:T(8,128)S(1)}, f32[512,512]{0,1:T(8,128)}, u32[]{:S(2)}) copy-start(f32[512,512]{0,1:T(8,128)} %convolution_bitcast_fusion.3) | copy-start | bytes 3145732
  267.4 2.0 copy-start.5
  267.4 2.0 copy-start.9
  275.1 4.6 %copy-start.3 = (f32[8,64,576]{2,1,0:T(8,128)}, f32[8,64,576]{2,1,0:T(8,128)S(1)}, u32[]{:S(2)}) copy-start(f32[8,64,576]{2,1,0:T(8,128)S(1)} %broadcast_select_fusion.1) | copy-start | bytes 3538948
  279.8 6.5 %copy-start.1 = (bf16[512,1024]{1,0:T(8,128)(2,1)S(1)}, bf16[512,1024]{1,0:T(8,128)(2,1)}, u32[]{:S(2)}) copy-start(bf16[512,1024]{1,0:T(8,128)(2,1)} %param.9) | copy-start | bytes 3145732
  283.1 0.9 slice-start.4
  284.9 1.3 copy-start.8
Sparse Core Ops, SparseCore 0:
  33.5 74.5 all-gather.1
  157.5 86.2 reduce-scatter.3

commit v13 on v6

--- a/solution.py
+++ b/solution.py
@@ -129,7 +129,7 @@
     send_grad = jnp.where(owner_has[:, None, None], send_grad, 0.0)
     back_grad = lax.all_to_all(send_grad, "dp", split_axis=0, concat_axis=0, tiled=True)
     land = jnp.where(owned_any, locally_owned_slots, 0)
-    arrived = jnp.where(owned_any[:, None, None], back_grad, 0.0)
+    arrived = back_grad
     grad_down = jnp.zeros((each_owner_rows, rank, down_cols), f32).at[land].add(
         arrived[:, :, :down_cols]
     )

time: 277 us -> 278 us (level)
  no operation moved by 1% of the time
where the time goes in v13:
time: 278 us; the launch traced here: 277 us
  waiting for transfers between devices  132 us (47%)
  local copies, waits for them, and re-layouts  68 us (24%)
  matrix products  28.7 us (10%)
  starting transfers between devices  20.3 us (7%)
  between operations  14.2 us (5%)
  other arithmetic  13.6 us (5%)
    ppermute x1, waiting for transfers between devices, body(): from_left = lax.ppermute(w_part_full, 'dp', up_x)  44.4 us
    all_gather x1, waiting for transfers between devices, body(): shares = lax.all_gather(slab, 'fsdp', axis=0, tiled=False)  42.9 us
    ppermute x1, waiting for transfers between devices, body(): far_a = lax.ppermute(from_left[:, :half_part], 'dp', up_x)  16 us
    unnamed x40, local copies, waits for them, and re-layouts  15.8 us
    all_gather x1, waiting for transfers between devices, body(): w_part_full = lax.all_gather(w_part, 'fsdp', axis=0, tiled=True)  13.4 us
    dot_general x1, local copies, waits for them, and re-layouts, body(): lax.dot_general(masked_back, tokens, contract, preferred_element_type=f32)  11.9 us
    dot_general x1, matrix products, body(): out_own = jnp.dot(tokens, w_own, preferred_element_type=f32)  11.5 us
    concatenate x1, local copies, waits for them, and re-layouts, body(): jnp.concatenate([part_down, part_up], axis=2)  10.9 us
  transfers between devices with their start and end apart: 10, of which 7 were waited for; matrix products, arithmetic and copies ran while one was open for 32% of the time, Pallas kernels for 0%

profile of v13, /device:TPU:1, one launch (start us, length us, event | category | flops | bytes accessed | tf_op | source)
XLA Modules:
  0.0 276.8 jit_solution(7642405571058655671)
XLA Ops:
  7.2 0.8 copy.44
  8.0 0.1 reshape.434
  8.1 1.4 gather_fusion.1
  9.6 0.1 fusion.19
  9.7 0.1 fusion.1
  9.9 0.1 select_reduce_fusion
  10.0 1.8 gather_fusion.3
  11.8 2.8 %gather_fusion.2 = bf16[8,64,512]{2,1,0:T(8,128)(2,1)S(1)} fusion(bf16[64,64,512]{2,1,0:T(8,128)(2,1)} %param.10, s32[1024]{0:T(1024)S(1)} %pad_clamp_fusion.2), kind=kCustom, calls=%fused_computation.2 | custom fusion | bytes 1048608 | tf_op jit(solution)/shard_map/jit(_take)/gather | solution.py:73
  14.7 0.1 broadcast_select_fusion
  14.8 1.1 maximum_select_fusion
  15.9 5.8 %all-to-all-start = ((bf16[8,64,576]{2,1,0:T(8,128)(2,1)}), bf16[8,64,576]{2,1,0:T(8,128)(2,1)S(1)}, u32[]{:S(2)}, u32[]{:S(2)}) async-start(bf16[8,64,576]{2,1,0:T(8,128)(2,1)} %maximum_select_fusion), calls=%async_computation | async-start | bytes 1310720 | tf_op jit(solution)/shard_map/all_to_all | solution.py:79
  21.7 10.9 %all-to-all-done = bf16[8,64,576]{2,1,0:T(8,128)(2,1)S(1)} async-done(((bf16[8,64,576]{2,1,0:T(8,128)(2,1)}), bf16[8,64,576]{2,1,0:T(8,128)(2,1)S(1)}, u32[]{:S(2)}, u32[]{:S(2)}) %all-to-all-start) | async-done | bytes 589856 | tf_op jit(solution)/shard_map/all_to_all | solution.py:79
  32.6 0.6 gather_fusion.4
  33.2 0.8 bitcast_select_fusion
  34.2 0.8 copy.60
  35.3 1.3 copy.50
  36.6 11.9 %copy.58 = bf16[8192,512]{1,0:T(8,128)(2,1)} copy(bf16[8192,512]{0,1:T(8,128)(2,1)} %bitcast.107) | data formatting | bytes 16777216 | tf_op jit(solution)/shard_map/dot_general | solution.py:113
  48.5 42.9 %all-gather.5.cloned.1.call-done = bf16[16,4,64,576]{3,2,1,0:T(8,128)(2,1)} async-done(((bf16[1,4,64,576]{3,2,1,0:T(8,128)(2,1)}), bf16[16,4,64,576]{3,2,1,0:T(8,128)(2,1)}) %all-gather.5.cloned.1.call-update) | async-done | bytes 4718608 | tf_op jit(solution)/shard_map/all_gather | solution.py:82
  91.4 1.3 slice_bitcast_fusion.1
  92.7 0.7 copy.48
  93.4 0.7 reshape_reshape.7
  94.1 2.9 %slice_bitcast_fusion = bf16[4,64,16,512]{3,1,0,2:T(8,128)(2,1)S(1)} fusion(bf16[16,4,64,576]{3,2,1,0:T(8,128)(2,1)} %all-gather.5.cloned.1.call-done), kind=kLoop, calls=%fused_computation.9 | loop fusion | bytes 8388608 | tf_op jit(solution)/shard_map/transpose | solution.py:83
  97.0 2.4 copy.47
  99.5 4.4 %copy.62 = bf16[32,8,16,512]{3,1,2,0:T(8,128)(2,1)S(1)} copy(bf16[32,8,16,512]{3,2,1,0:T(8,128)(2,1)S(1)} %bitcast.106) | data formatting | bytes 8388608
  103.9 0.5 fusion.21
  104.4 2.4 fusion.20
  106.8 0.1 multiply_reduce_fusion
  107.0 0.9 convolution_bitcast_fusion.1
  108.0 0.2 slice-done.1
  108.1 2.4 convolution_bitcast_fusion
  110.5 5.2 %pad_maximum_fusion = f32[16,256,576]{2,1,0:T(8,128)} fusion(f32[16,256,64]{2,1,0:T(8,128)S(1)} %convolution_bitcast_fusion.1, f32[16,256,512]{2,1,0:T(8,128)S(1)} %convolution_bitcast_fusion), kind=kLoop, calls=%fused_computation.8 | loop fusion | flops 2359296 | bytes 18874368 | tf_op jit(solution)/shard_map/concatenate | solution.py:121
  115.7 10.9 %copy.53 = f32[16,256,576]{1,2,0:T(8,128)} copy(f32[16,256,576]{2,1,0:T(8,128)} %pad_maximum_fusion) | data formatting | bytes 18874368 | tf_op jit(solution)/shard_map/concatenate | solution.py:121
  126.6 13.4 %all-gather.3.cloned.1.call-done = bf16[8192,128]{0,1:T(8,128)(2,1)} async-done(((bf16[512,128]{0,1:T(8,128)(2,1)}), bf16[8192,128]{0,1:T(8,128)(2,1)}) %all-gather.3.cloned.1.call-update) | async-done | bytes 2097168 | tf_op jit(solution)/shard_map/all_gather | solution.py:40
  140.1 1.2 collective-permute-start
  141.3 1.5 collective-permute-start.2
  142.8 44.4 %collective-permute-done = bf16[8192,128]{0,1:T(8,128)(2,1)S(1)} collective-permute-done((bf16[8192,128]{0,1:T(8,128)(2,1)}, bf16[8192,128]{0,1:T(8,128)(2,1)S(1)}, u32[]{:S(2)}, u32[]{:S(2)}) %collective-permute-start) | collective-permute-done | bytes 2097184 | tf_op jit(solution)/shard_map/ppermute | solution.py:43
  187.3 3.2 %constant_dynamic-update-slice_fusion.4 = bf16[8192,512]{0,1:T(8,128)(2,1)} fusion(bf16[8192,128]{0,1:T(8,128)(2,1)} %all-gather.3.cloned.1.call-done), kind=kLoop, calls=%fused_computation.33 | loop fusion | bytes 4194304
  190.6 2.7 collective-permute-start.3
  193.4 1.5 constant_dynamic-update-slice_fusion.3
  194.8 16.0 %collective-permute-done.1 = bf16[8192,64]{0,1:T(8,128)(2,1)S(1)} collective-permute-done((bf16[8192,64]{0,1:T(8,128)(2,1)S(1)}, bf16[8192,64]{0,1:T(8,128)(2,1)S(1)}, u32[]{:S(2)}, u32[]{:S(2)}) %collective-permute-start.1) | collective-permute-done | bytes 1048608 | tf_op jit(solution)/shard_map/ppermute | solution.py:46
  210.8 1.0 constant_dynamic-update-slice_fusion.2
  211.9 1.4 collective-permute-done.3
  213.3 1.0 constant_dynamic-update-slice_fusion.1
  214.3 1.5 constant_dynamic-update-slice_fusion
  215.8 3.5 %collective-permute-start.4 = (bf16[8192,512]{0,1:T(8,128)(2,1)}, bf16[8192,512]{0,1:T(8,128)(2,1)}, u32[]{:S(2)}, u32[]{:S(2)}) collective-permute-start(bf16[8192,512]{0,1:T(8,128)(2,1)} %constant_dynamic-update-slice_fusion), channel_id=1, source_target_pairs={{0,16},{16,0},{32,48},{48,32},{64,80},{80,64},{96,112},{112,96},{1... | collective-permute-start | bytes 25165832 | tf_op jit(solution)/shard_map/ppermute | solution.py:51
  219.3 0.1 fusion.2
  219.5 11.5 %convolution_bitcast_fusion.3 = f32[512,512]{0,1:T(8,128)} fusion(bf16[8192,512]{0,1:T(8,128)(2,1)} %constant_dynamic-update-slice_fusion, bf16[512,8192]{1,0:T(8,128)(2,1)} %param.8), kind=kOutput, calls=%fused_computation.15 | convolution fusion | flops 4294967296 | bytes 17825792 | tf_op jit(solution)/shard_map/dot_general | solution.py:52
  231.1 1.3 copy.54
  232.4 0.6 gather_fusion.5
  233.0 1.2 select_select_fusion
  234.2 5.5 %all-to-all-start.1 = ((f32[8,64,576]{2,1,0:T(8,128)}), f32[8,64,576]{2,1,0:T(8,128)}, u32[]{:S(2)}, u32[]{:S(2)}) async-start(f32[8,64,576]{2,1,0:T(8,128)} %select_select_fusion), calls=%async_computation.1 | async-start | bytes 2621440 | tf_op jit(solution)/shard_map/all_to_all | solution.py:130
  239.7 9.6 %convolution_bitcast_fusion.2 = f32[512,512]{0,1:T(8,128)S(1)} fusion(bf16[8192,512]{0,1:T(8,128)(2,1)} %collective-permute-done.4, bf16[512,8192]{1,0:T(8,128)(2,1)} %param.8), kind=kOutput, calls=%fused_computation.14 | convolution fusion | flops 4294967296 | bytes 17825792 | tf_op jit(solution)/shard_map/dot_general | solution.py:53
  249.3 0.2 pad_maximum_fusion.1
  249.5 2.0 gather_fusion
  251.5 1.9 copy.57
  253.5 1.4 add_convert_fusion
  254.9 2.8 %all-to-all-done.1 = f32[8,64,576]{2,1,0:T(8,128)} async-done(((f32[8,64,576]{2,1,0:T(8,128)}), f32[8,64,576]{2,1,0:T(8,128)}, u32[]{:S(2)}, u32[]{:S(2)}) %all-to-all-start.1) | async-done | bytes 1179680 | tf_op jit(solution)/shard_map/all_to_all | solution.py:130
  257.7 1.3 slice.40
  259.1 4.5 %broadcast_in_dim.144 = f32[64,64,512]{2,1,0:T(8,128)} broadcast(f32[]{:T(128)} %constant.200.clone.1), dimensions={} | broadcast | bytes 8388612 | tf_op jit(solution)/shard_map/broadcast_in_dim | solution.py:133
  263.5 3.2 %scatter_fusion = f32[64,64,512]{2,1,0:T(8,128)} fusion(f32[64,64,512]{2,1,0:T(8,128)} %broadcast_in_dim.144, s32[8]{0:T(128)S(1)} %get-tuple-element.13, f32[8,64,512]{2,1,0:T(8,128)S(1)} %slice.40), kind=kCustom, calls=%fused_computation.6 | custom fusion | flops 262144 | bytes 3145760 | tf_op jit(solution)/shard_map/scatter-add | solution.py:133
  266.8 1.0 slice.41
  267.7 0.2 broadcast_in_dim.150
  268.0 0.9 scatter_fusion.1
  268.9 1.3 copy-done.7
  (65 shorter events, 1.1 us)
Async XLA Ops:
  7.2 26.9 %copy-start = (bf16[512,1024]{1,0:T(8,128)(2,1)S(1)}, bf16[512,1024]{1,0:T(8,128)(2,1)}, u32[]{:S(2)}) copy-start(bf16[512,1024]{1,0:T(8,128)(2,1)} %param.9) | copy-start | bytes 3145732
  9.5 25.5 %copy-start.9 = (s32[1,64]{1,0:T(1,128)S(1)}, s32[1,64]{1,0:T(1,128)}, u32[]{:S(2)}) copy-start(s32[1,64]{1,0:T(1,128)} %param.13) | copy-start | bytes 772
  9.5 25.7 %copy-start.4 = (bf16[512,1024]{1,0:T(8,128)(2,1)S(1)}, bf16[512,1024]{1,0:T(8,128)(2,1)}, u32[]{:S(2)}) copy-start(bf16[512,1024]{1,0:T(8,128)(2,1)} %param.12) | copy-start | bytes 3145732
  15.9 16.7 %all-to-all-start = ((bf16[8,64,576]{2,1,0:T(8,128)(2,1)}), bf16[8,64,576]{2,1,0:T(8,128)(2,1)S(1)}, u32[]{:S(2)}, u32[]{:S(2)}) async-start(bf16[8,64,576]{2,1,0:T(8,128)(2,1)} %maximum_select_fusion), calls=%async_computation | async-start | bytes 1310720 | tf_op jit(solution)/shard_map/all_to_all | solution.py:79
  21.7 69.7 %all-gather.5.cloned.1.call-start = ((), (), s32[]{:S(2)}) async-start(), calls=%async_computation.4 | async-start | bytes 5570560 | tf_op jit(solution)/shard_map/all_gather | solution.py:82
  34.1 106.0 %all-gather.3.cloned.1.call-start = ((), (), s32[]{:S(2)}) async-start(), calls=%async_computation.3 | async-start | bytes 2228224 | tf_op jit(solution)/shard_map/all_gather | solution.py:40
  35.0 196.1 %reduce-scatter.4.cloned.1.call-start = ((), (), s32[]{:S(2)}) async-start(), calls=%async_computation.5 | async-start | bytes 10027008
  94.1 9.7 %copy-start.2 = (bf16[256,1024]{1,0:T(8,128)(2,1)}, bf16[256,1024]{1,0:T(8,128)(2,1)S(1)}, u32[]{:S(2)}) copy-start(bf16[256,1024]{1,0:T(8,128)(2,1)S(1)} %reshape_reshape.7) | copy-start | bytes 1572868
  97.0 7.4 %slice-start.2 = ((s8[8388608]{0:T(1024)(128)(4,1)}), s8[4194304]{0:T(1024)(128)(4,1)S(1)}, s32[]{:S(2)}) async-start(s8[8388608]{0:T(1024)(128)(4,1)} %bitcast.108), calls=%async_computation.8 | async-start | bytes 8388608
  99.5 4.4 %copy-start.5 = (bf16[512,1024]{1,0:T(8,128)(2,1)S(1)}, bf16[512,1024]{1,0:T(8,128)(2,1)}, u32[]{:S(2)}) copy-start(bf16[512,1024]{1,0:T(8,128)(2,1)} %param.12) | copy-start | bytes 3145732
  99.5 4.9 %slice-start.3 = ((s8[8388608]{0:T(1024)(128)(4,1)}), s8[4194304]{0:T(1024)(128)(4,1)S(1)}, s32[]{:S(2)}) async-start(s8[8388608]{0:T(1024)(128)(4,1)} %bitcast.108), calls=%async_computation.9 | async-start | bytes 8388608
  104.4 3.6 %slice-start = ((s8[8388608]{0:T(1024)(128)(4,1)}), s8[4194304]{0:T(1024)(128)(4,1)S(1)}, s32[]{:S(2)}) async-start(s8[8388608]{0:T(1024)(128)(4,1)} %bitcast.103), calls=%async_computation.6 | async-start | bytes 8388608
  104.4 2.6 copy-start.6
  104.4 3.7 %slice-start.1 = ((s8[8388608]{0:T(1024)(128)(4,1)}), s8[4194304]{0:T(1024)(128)(4,1)S(1)}, s32[]{:S(2)}) async-start(s8[8388608]{0:T(1024)(128)(4,1)} %bitcast.103), calls=%async_computation.7 | async-start | bytes 8388608
  140.1 47.1 %collective-permute-start = (bf16[8192,128]{0,1:T(8,128)(2,1)}, bf16[8192,128]{0,1:T(8,128)(2,1)S(1)}, u32[]{:S(2)}, u32[]{:S(2)}) collective-permute-start(bf16[8192,128]{0,1:T(8,128)(2,1)} %all-gather.3.cloned.1.call-done), channel_id=1, source_target_pairs={{0,32},{16,48},{32,64},{48,80},{64,96},{80,112},{96,0},{112,16},{1... | collective-permute-start | bytes 6291464 | tf_op jit(solution)/shard_map/ppermute | solution.py:43
  141.3 49.3 %collective-permute-start.2 = (bf16[8192,128]{0,1:T(8,128)(2,1)}, bf16[8192,128]{0,1:T(8,128)(2,1)S(1)}, u32[]{:S(2)}, u32[]{:S(2)}) collective-permute-start(bf16[8192,128]{0,1:T(8,128)(2,1)} %all-gather.3.cloned.1.call-done), channel_id=1, source_target_pairs={{0,96},{16,112},{32,0},{48,16},{64,32},{80,48},{96,64},{112,80},{1... | collective-permute-start | bytes 6291464 | tf_op jit(solution)/shard_map/ppermute | solution.py:44
  187.3 23.6 %collective-permute-start.1 = (bf16[8192,64]{0,1:T(8,128)(2,1)S(1)}, bf16[8192,64]{0,1:T(8,128)(2,1)S(1)}, u32[]{:S(2)}, u32[]{:S(2)}) collective-permute-start(bf16[8192,64]{0,1:T(8,128)(2,1)S(1)} %slice.36), channel_id=1, source_target_pairs={{0,32},{16,48},{32,64},{48,80},{64,96},{80,112},{96,0},{112,16},{1... | collective-permute-start | bytes 3145736 | tf_op jit(solution)/shard_map/ppermute | solution.py:46
  190.6 22.6 %collective-permute-start.3 = (bf16[8192,64]{0,1:T(8,128)(2,1)S(1)}, bf16[8192,64]{0,1:T(8,128)(2,1)S(1)}, u32[]{:S(2)}, u32[]{:S(2)}) collective-permute-start(bf16[8192,64]{0,1:T(8,128)(2,1)S(1)} %slice.37), channel_id=1, source_target_pairs={{0,96},{16,112},{32,0},{48,16},{64,32},{80,48},{96,64},{112,80},{1... | collective-permute-start | bytes 3145736 | tf_op jit(solution)/shard_map/ppermute | solution.py:47
  215.8 23.9 %collective-permute-start.4 = (bf16[8192,512]{0,1:T(8,128)(2,1)}, bf16[8192,512]{0,1:T(8,128)(2,1)}, u32[]{:S(2)}, u32[]{:S(2)}) collective-permute-start(bf16[8192,512]{0,1:T(8,128)(2,1)} %constant_dynamic-update-slice_fusion), channel_id=1, source_target_pairs={{0,16},{16,0},{32,48},{48,32},{64,80},{80,64},{96,112},{112,96},{1... | collective-permute-start | bytes 25165832 | tf_op jit(solution)/shard_map/ppermute | solution.py:51
  234.2 23.5 %all-to-all-start.1 = ((f32[8,64,576]{2,1,0:T(8,128)}), f32[8,64,576]{2,1,0:T(8,128)}, u32[]{:S(2)}, u32[]{:S(2)}) async-start(f32[8,64,576]{2,1,0:T(8,128)} %select_select_fusion), calls=%async_computation.1 | async-start | bytes 2621440 | tf_op jit(solution)/shard_map/all_to_all | solution.py:130
  239.7 9.6 %copy-start.8 = (f32[512,512]{0,1:T(8,128)S(1)}, f32[512,512]{0,1:T(8,128)}, u32[]{:S(2)}) copy-start(f32[512,512]{0,1:T(8,128)} %convolution_bitcast_fusion.3) | copy-start | bytes 3145732
  249.5 3.9 %copy-start.3 = (bf16[256,1024]{1,0:T(8,128)(2,1)S(1)}, bf16[256,1024]{1,0:T(8,128)(2,1)}, u32[]{:S(2)}) copy-start(bf16[256,1024]{1,0:T(8,128)(2,1)} %copy-done.2) | copy-start | bytes 1572868
  259.1 11.2 %copy-start.1 = (bf16[512,1024]{1,0:T(8,128)(2,1)S(1)}, bf16[512,1024]{1,0:T(8,128)(2,1)}, u32[]{:S(2)}) copy-start(bf16[512,1024]{1,0:T(8,128)(2,1)} %param.9) | copy-start | bytes 3145732
  268.9 1.3 copy-start.7
Sparse Core Ops, SparseCore 0:
  34.2 57.1 all-gather.4
  93.5 46.5 all-gather.2
  143.6 86.9 reduce-scatter.3

commit v14 on v6

--- a/solution.py
+++ b/solution.py
@@ -68,14 +68,17 @@
     owned_here = list_owner == group_index
     locally_owned_slots = jnp.sum(jnp.where(owned_here, list_local, 0), axis=1)
     owned_any = jnp.any(owned_here, axis=1)
+    pick = (
+        (locally_owned_slots[:, None] == jnp.arange(each_owner_rows, dtype=jnp.int32)[None, :])
+        & owned_any[:, None]
+    ).astype(adapter_down_maps.dtype)
     send = jnp.concatenate(
         [
-            jnp.take(adapter_down_maps, locally_owned_slots, axis=0),
-            jnp.take(adapter_up_maps, locally_owned_slots, axis=0),
+            jnp.einsum("sk,krd->srd", pick, adapter_down_maps, preferred_element_type=f32),
+            jnp.einsum("sk,krd->srd", pick, adapter_up_maps, preferred_element_type=f32),
         ],
         axis=2,
-    )
-    send = jnp.where(owned_any[:, None, None], send, jnp.zeros((), send.dtype))
+    ).astype(adapter_down_maps.dtype)
     got = lax.all_to_all(send, "dp", split_axis=0, concat_axis=0, tiled=True)
     my_owner = lax.dynamic_index_in_dim(list_owner, group_index, 0, keepdims=False)
     slab = jnp.take(got, my_owner, axis=0)

time: 277 us -> 279 us (level)
  matrix products: 28.7 us -> 36 us
  local copies, waits for them, and re-layouts: 65.8 us -> 62.2 us
    dot_general x0 -> x2, matrix products: none -> 7.33 us  [the longest x1 6.67 us: body(): jnp.einsum('sk,krd->srd', pick, adapter_down_maps, preferred_element_type...]
    gather x2 -> x0, local copies, waits for them, and re-layouts: 4.57 us -> none  [the longest x1 2.77 us: body(): jnp.take(adapter_down_maps, locally_owned_slots, axis=0)]
    unnamed x40 -> x42, local copies, waits for them, and re-layouts: 15.8 us -> 15.8 us
where the time goes in v14:
time: 279 us; the launch traced here: 278 us
  waiting for transfers between devices  132 us (47%)
  local copies, waits for them, and re-layouts  62.2 us (22%)
  matrix products  36 us (13%)
  starting transfers between devices  19.9 us (7%)
  between operations  14.2 us (5%)
  other arithmetic  13.9 us (5%)
    ppermute x1, waiting for transfers between devices, body(): from_left = lax.ppermute(w_part_full, 'dp', up_x)  44.4 us
    all_gather x1, waiting for transfers between devices, body(): shares = lax.all_gather(slab, 'fsdp', axis=0, tiled=False)  42.9 us
    ppermute x1, waiting for transfers between devices, body(): far_a = lax.ppermute(from_left[:, :half_part], 'dp', up_x)  16 us
    unnamed x42, local copies, waits for them, and re-layouts  15.8 us
    all_gather x1, waiting for transfers between devices, body(): w_part_full = lax.all_gather(w_part, 'fsdp', axis=0, tiled=True)  13.4 us
    dot_general x1, local copies, waits for them, and re-layouts, body(): lax.dot_general(masked_back, tokens, contract, preferred_element_type=f32)  12 us
    dot_general x1, matrix products, body(): out_own = jnp.dot(tokens, w_own, preferred_element_type=f32)  11.5 us
    concatenate x1, local copies, waits for them, and re-layouts, body(): jnp.concatenate([part_down, part_up], axis=2)  10.9 us
  transfers between devices with their start and end apart: 10, of which 7 were waited for; matrix products, arithmetic and copies ran while one was open for 32% of the time, Pallas kernels for 0%

profile of v14, /device:TPU:1, one launch (start us, length us, event | category | flops | bytes accessed | tf_op | source)
XLA Modules:
  0.0 278.1 jit_solution(8908582778822299762)
XLA Ops:
  7.2 0.9 copy.52
  8.1 0.1 reshape.420
  8.2 1.4 gather_fusion.1
  9.6 0.1 reshape.419
  9.7 0.1 fusion.32
  9.8 0.1 fusion.7
  9.9 0.7 convolution_convert_fusion
  10.6 6.7 %fusion.2 = bf16[8,64,512]{2,0,1:T(8,128)(2,1)S(1)} fusion(bf16[64,64,512]{2,1,0:T(8,128)(2,1)} %param.10, s32[8]{0:T(128)S(1)} %fusion.7, pred[8]{0:T(512)(128)(4,1)S(1)} %get-tuple-element.7), kind=kOutput, calls=%fused_computation.17 | convolution fusion | flops 33817600 | bytes 4718632 | tf_op jit(solution)/shard_map/sk,krd->srd/dot_general | solution.py:77
  17.3 0.9 copy.57
  18.2 5.8 %all-to-all-start = ((bf16[8,64,576]{2,1,0:T(8,128)(2,1)}), bf16[8,64,576]{2,1,0:T(8,128)(2,1)S(1)}, u32[]{:S(2)}, u32[]{:S(2)}) async-start(bf16[8,64,576]{2,1,0:T(8,128)(2,1)} %copy.57), calls=%async_computation | async-start | bytes 1310720 | tf_op jit(solution)/shard_map/all_to_all | solution.py:82
  24.1 10.8 %all-to-all-done = bf16[8,64,576]{2,1,0:T(8,128)(2,1)S(1)} async-done(((bf16[8,64,576]{2,1,0:T(8,128)(2,1)}), bf16[8,64,576]{2,1,0:T(8,128)(2,1)S(1)}, u32[]{:S(2)}, u32[]{:S(2)}) %all-to-all-start) | async-done | bytes 589856 | tf_op jit(solution)/shard_map/all_to_all | solution.py:82
  34.9 0.6 gather_fusion.2
  35.5 0.8 bitcast_select_fusion
  36.5 0.8 copy.71
  37.6 1.3 copy.61
  38.9 12.0 %copy.69 = bf16[8192,512]{1,0:T(8,128)(2,1)} copy(bf16[8192,512]{0,1:T(8,128)(2,1)} %bitcast.100) | data formatting | bytes 16777216 | tf_op jit(solution)/shard_map/dot_general | solution.py:116
  50.9 42.9 %all-gather.5.cloned.1.call-done = bf16[16,4,64,576]{3,2,1,0:T(8,128)(2,1)} async-done(((bf16[1,4,64,576]{3,2,1,0:T(8,128)(2,1)}), bf16[16,4,64,576]{3,2,1,0:T(8,128)(2,1)}) %all-gather.5.cloned.1.call-update) | async-done | bytes 4718608 | tf_op jit(solution)/shard_map/all_gather | solution.py:85
  93.8 1.3 slice_bitcast_fusion.1
  95.1 0.7 copy.59
  95.8 0.7 reshape_reshape.7
  96.5 2.9 %slice_bitcast_fusion = bf16[4,64,16,512]{3,1,0,2:T(8,128)(2,1)S(1)} fusion(bf16[16,4,64,576]{3,2,1,0:T(8,128)(2,1)} %all-gather.5.cloned.1.call-done), kind=kLoop, calls=%fused_computation.7 | loop fusion | bytes 8388608 | tf_op jit(solution)/shard_map/transpose | solution.py:86
  99.4 2.4 copy.58
  101.8 4.4 %copy.73 = bf16[32,8,16,512]{3,1,2,0:T(8,128)(2,1)S(1)} copy(bf16[32,8,16,512]{3,2,1,0:T(8,128)(2,1)S(1)} %bitcast.99) | data formatting | bytes 8388608
  106.2 0.5 fusion.34
  106.8 2.4 fusion.33
  109.1 0.1 multiply_reduce_fusion
  109.4 1.0 convolution_bitcast_fusion.1
  110.4 0.1 slice-done.1
  110.5 2.4 convolution_bitcast_fusion
  112.9 5.2 %pad_maximum_fusion = f32[16,256,576]{2,1,0:T(8,128)} fusion(f32[16,256,64]{2,1,0:T(8,128)S(1)} %convolution_bitcast_fusion.1, f32[16,256,512]{2,1,0:T(8,128)S(1)} %convolution_bitcast_fusion), kind=kLoop, calls=%fused_computation.6 | loop fusion | flops 2359296 | bytes 18874368 | tf_op jit(solution)/shard_map/concatenate | solution.py:124
  118.1 10.9 %copy.64 = f32[16,256,576]{1,2,0:T(8,128)} copy(f32[16,256,576]{2,1,0:T(8,128)} %pad_maximum_fusion) | data formatting | bytes 18874368 | tf_op jit(solution)/shard_map/concatenate | solution.py:124
  129.0 13.4 %all-gather.3.cloned.1.call-done = bf16[8192,128]{0,1:T(8,128)(2,1)} async-done(((bf16[512,128]{0,1:T(8,128)(2,1)}), bf16[8192,128]{0,1:T(8,128)(2,1)}) %all-gather.3.cloned.1.call-update) | async-done | bytes 2097168 | tf_op jit(solution)/shard_map/all_gather | solution.py:40
  142.4 1.2 collective-permute-start
  143.6 1.5 collective-permute-start.2
  145.1 44.4 %collective-permute-done = bf16[8192,128]{0,1:T(8,128)(2,1)S(1)} collective-permute-done((bf16[8192,128]{0,1:T(8,128)(2,1)}, bf16[8192,128]{0,1:T(8,128)(2,1)S(1)}, u32[]{:S(2)}, u32[]{:S(2)}) %collective-permute-start) | collective-permute-done | bytes 2097184 | tf_op jit(solution)/shard_map/ppermute | solution.py:43
  189.7 3.2 %constant_dynamic-update-slice_fusion.4 = bf16[8192,512]{0,1:T(8,128)(2,1)} fusion(bf16[8192,128]{0,1:T(8,128)(2,1)} %all-gather.3.cloned.1.call-done), kind=kLoop, calls=%fused_computation.35 | loop fusion | bytes 4194304
  193.0 2.7 collective-permute-start.3
  195.7 1.5 constant_dynamic-update-slice_fusion.3
  197.2 16.0 %collective-permute-done.1 = bf16[8192,64]{0,1:T(8,128)(2,1)S(1)} collective-permute-done((bf16[8192,64]{0,1:T(8,128)(2,1)S(1)}, bf16[8192,64]{0,1:T(8,128)(2,1)S(1)}, u32[]{:S(2)}, u32[]{:S(2)}) %collective-permute-start.1) | collective-permute-done | bytes 1048608 | tf_op jit(solution)/shard_map/ppermute | solution.py:46
  213.2 1.0 constant_dynamic-update-slice_fusion.2
  214.2 1.4 collective-permute-done.3
  215.6 1.0 constant_dynamic-update-slice_fusion.1
  216.7 1.5 constant_dynamic-update-slice_fusion
  218.1 3.5 %collective-permute-start.4 = (bf16[8192,512]{0,1:T(8,128)(2,1)}, bf16[8192,512]{0,1:T(8,128)(2,1)}, u32[]{:S(2)}, u32[]{:S(2)}) collective-permute-start(bf16[8192,512]{0,1:T(8,128)(2,1)} %constant_dynamic-update-slice_fusion), channel_id=1, source_target_pairs={{0,16},{16,0},{32,48},{48,32},{64,80},{80,64},{96,112},{112,96},{1... | collective-permute-start | bytes 25165832 | tf_op jit(solution)/shard_map/ppermute | solution.py:51
  221.7 0.1 fusion.8
  221.8 0.1 select_reduce_fusion
  222.0 11.5 %convolution_bitcast_fusion.3 = f32[512,512]{0,1:T(8,128)} fusion(bf16[8192,512]{0,1:T(8,128)(2,1)} %constant_dynamic-update-slice_fusion, bf16[512,8192]{1,0:T(8,128)(2,1)} %param.8), kind=kOutput, calls=%fused_computation.15 | convolution fusion | flops 4294967296 | bytes 17825792 | tf_op jit(solution)/shard_map/dot_general | solution.py:52
  233.5 1.3 copy.65
  234.8 0.6 gather_fusion.3
  235.5 1.2 select_select_fusion
  236.7 5.1 %all-to-all-start.1 = ((f32[8,64,576]{2,1,0:T(8,128)}), f32[8,64,576]{2,1,0:T(8,128)}, u32[]{:S(2)}, u32[]{:S(2)}) async-start(f32[8,64,576]{2,1,0:T(8,128)} %select_select_fusion), calls=%async_computation.1 | async-start | bytes 2621440 | tf_op jit(solution)/shard_map/all_to_all | solution.py:133
  241.8 9.6 %convolution_bitcast_fusion.2 = f32[512,512]{0,1:T(8,128)S(1)} fusion(bf16[8192,512]{0,1:T(8,128)(2,1)} %collective-permute-done.4, bf16[512,8192]{1,0:T(8,128)(2,1)} %param.8), kind=kOutput, calls=%fused_computation.14 | convolution fusion | flops 4294967296 | bytes 17825792 | tf_op jit(solution)/shard_map/dot_general | solution.py:53
  251.4 0.2 pad_maximum_fusion.1
  251.6 2.0 gather_fusion
  253.6 1.9 copy.68
  255.5 1.4 add_convert_fusion
  256.9 2.8 %all-to-all-done.1 = f32[8,64,576]{2,1,0:T(8,128)} async-done(((f32[8,64,576]{2,1,0:T(8,128)}), f32[8,64,576]{2,1,0:T(8,128)}, u32[]{:S(2)}, u32[]{:S(2)}) %all-to-all-start.1) | async-done | bytes 1179680 | tf_op jit(solution)/shard_map/all_to_all | solution.py:133
  259.8 1.5 broadcast_select_fusion
  261.3 0.1 slice.36
  261.4 4.5 %broadcast_in_dim.115 = f32[64,64,512]{2,1,0:T(8,128)} broadcast(f32[]{:T(128)} %constant.174.clone.1), dimensions={} | broadcast | bytes 8388612 | tf_op jit(solution)/shard_map/broadcast_in_dim | solution.py:136
  265.9 3.2 %scatter_fusion = f32[64,64,512]{2,1,0:T(8,128)} fusion(f32[64,64,512]{2,1,0:T(8,128)} %broadcast_in_dim.115, s32[8]{0:T(128)S(1)} %fusion.28, f32[8,64,512]{2,1,0:T(8,128)S(1)} %slice.36), kind=kCustom, calls=%fused_computation.4 | custom fusion | flops 262144 | bytes 3145760 | tf_op jit(solution)/shard_map/scatter-add | solution.py:136
  269.1 0.2 broadcast_in_dim.122
  269.3 0.9 scatter_fusion.1
  270.3 1.3 copy-done.7
  (66 shorter events, 1.1 us)
Async XLA Ops:
  7.2 29.3 %copy-start = (bf16[512,1024]{1,0:T(8,128)(2,1)S(1)}, bf16[512,1024]{1,0:T(8,128)(2,1)}, u32[]{:S(2)}) copy-start(bf16[512,1024]{1,0:T(8,128)(2,1)} %param.9) | copy-start | bytes 3145732
  7.2 2.7 copy-start.8
  17.3 20.1 %copy-start.10 = (s32[1,64]{1,0:T(1,128)S(1)}, s32[1,64]{1,0:T(1,128)}, u32[]{:S(2)}) copy-start(s32[1,64]{1,0:T(1,128)} %param.13) | copy-start | bytes 772
  17.3 20.3 %copy-start.4 = (bf16[512,1024]{1,0:T(8,128)(2,1)S(1)}, bf16[512,1024]{1,0:T(8,128)(2,1)}, u32[]{:S(2)}) copy-start(bf16[512,1024]{1,0:T(8,128)(2,1)} %param.12) | copy-start | bytes 3145732
  18.2 16.7 %all-to-all-start = ((bf16[8,64,576]{2,1,0:T(8,128)(2,1)}), bf16[8,64,576]{2,1,0:T(8,128)(2,1)S(1)}, u32[]{:S(2)}, u32[]{:S(2)}) async-start(bf16[8,64,576]{2,1,0:T(8,128)(2,1)} %copy.57), calls=%async_computation | async-start | bytes 1310720 | tf_op jit(solution)/shard_map/all_to_all | solution.py:82
  24.0 69.7 %all-gather.5.cloned.1.call-start = ((), (), s32[]{:S(2)}) async-start(), calls=%async_computation.4 | async-start | bytes 5570560 | tf_op jit(solution)/shard_map/all_gather | solution.py:85
  36.4 106.0 %all-gather.3.cloned.1.call-start = ((), (), s32[]{:S(2)}) async-start(), calls=%async_computation.3 | async-start | bytes 2228224 | tf_op jit(solution)/shard_map/all_gather | solution.py:40
  37.3 196.2 %reduce-scatter.4.cloned.1.call-start = ((), (), s32[]{:S(2)}) async-start(), calls=%async_computation.5 | async-start | bytes 10027008
  96.5 9.7 %copy-start.2 = (bf16[256,1024]{1,0:T(8,128)(2,1)}, bf16[256,1024]{1,0:T(8,128)(2,1)S(1)}, u32[]{:S(2)}) copy-start(bf16[256,1024]{1,0:T(8,128)(2,1)S(1)} %reshape_reshape.7) | copy-start | bytes 1572868
  99.4 7.4 %slice-start.2 = ((s8[8388608]{0:T(1024)(128)(4,1)}), s8[4194304]{0:T(1024)(128)(4,1)S(1)}, s32[]{:S(2)}) async-start(s8[8388608]{0:T(1024)(128)(4,1)} %bitcast.101), calls=%async_computation.8 | async-start | bytes 8388608
  101.8 4.4 %copy-start.5 = (bf16[512,1024]{1,0:T(8,128)(2,1)S(1)}, bf16[512,1024]{1,0:T(8,128)(2,1)}, u32[]{:S(2)}) copy-start(bf16[512,1024]{1,0:T(8,128)(2,1)} %param.12) | copy-start | bytes 3145732
  101.8 4.9 %slice-start.3 = ((s8[8388608]{0:T(1024)(128)(4,1)}), s8[4194304]{0:T(1024)(128)(4,1)S(1)}, s32[]{:S(2)}) async-start(s8[8388608]{0:T(1024)(128)(4,1)} %bitcast.101), calls=%async_computation.9 | async-start | bytes 8388608
  106.7 3.6 %slice-start = ((s8[8388608]{0:T(1024)(128)(4,1)}), s8[4194304]{0:T(1024)(128)(4,1)S(1)}, s32[]{:S(2)}) async-start(s8[8388608]{0:T(1024)(128)(4,1)} %bitcast.96), calls=%async_computation.6 | async-start | bytes 8388608
  106.8 2.6 copy-start.6
  106.8 3.7 %slice-start.1 = ((s8[8388608]{0:T(1024)(128)(4,1)}), s8[4194304]{0:T(1024)(128)(4,1)S(1)}, s32[]{:S(2)}) async-start(s8[8388608]{0:T(1024)(128)(4,1)} %bitcast.96), calls=%async_computation.7 | async-start | bytes 8388608
  142.4 47.1 %collective-permute-start = (bf16[8192,128]{0,1:T(8,128)(2,1)}, bf16[8192,128]{0,1:T(8,128)(2,1)S(1)}, u32[]{:S(2)}, u32[]{:S(2)}) collective-permute-start(bf16[8192,128]{0,1:T(8,128)(2,1)} %all-gather.3.cloned.1.call-done), channel_id=1, source_target_pairs={{0,32},{16,48},{32,64},{48,80},{64,96},{80,112},{96,0},{112,16},{1... | collective-permute-start | bytes 6291464 | tf_op jit(solution)/shard_map/ppermute | solution.py:43
  143.6 49.3 %collective-permute-start.2 = (bf16[8192,128]{0,1:T(8,128)(2,1)}, bf16[8192,128]{0,1:T(8,128)(2,1)S(1)}, u32[]{:S(2)}, u32[]{:S(2)}) collective-permute-start(bf16[8192,128]{0,1:T(8,128)(2,1)} %all-gather.3.cloned.1.call-done), channel_id=1, source_target_pairs={{0,96},{16,112},{32,0},{48,16},{64,32},{80,48},{96,64},{112,80},{1... | collective-permute-start | bytes 6291464 | tf_op jit(solution)/shard_map/ppermute | solution.py:44
  189.6 23.6 %collective-permute-start.1 = (bf16[8192,64]{0,1:T(8,128)(2,1)S(1)}, bf16[8192,64]{0,1:T(8,128)(2,1)S(1)}, u32[]{:S(2)}, u32[]{:S(2)}) collective-permute-start(bf16[8192,64]{0,1:T(8,128)(2,1)S(1)} %slice.32), channel_id=1, source_target_pairs={{0,32},{16,48},{32,64},{48,80},{64,96},{80,112},{96,0},{112,16},{1... | collective-permute-start | bytes 3145736 | tf_op jit(solution)/shard_map/ppermute | solution.py:46
  193.0 22.6 %collective-permute-start.3 = (bf16[8192,64]{0,1:T(8,128)(2,1)S(1)}, bf16[8192,64]{0,1:T(8,128)(2,1)S(1)}, u32[]{:S(2)}, u32[]{:S(2)}) collective-permute-start(bf16[8192,64]{0,1:T(8,128)(2,1)S(1)} %slice.33), channel_id=1, source_target_pairs={{0,96},{16,112},{32,0},{48,16},{64,32},{80,48},{96,64},{112,80},{1... | collective-permute-start | bytes 3145736 | tf_op jit(solution)/shard_map/ppermute | solution.py:47
  218.1 23.6 %collective-permute-start.4 = (bf16[8192,512]{0,1:T(8,128)(2,1)}, bf16[8192,512]{0,1:T(8,128)(2,1)}, u32[]{:S(2)}, u32[]{:S(2)}) collective-permute-start(bf16[8192,512]{0,1:T(8,128)(2,1)} %constant_dynamic-update-slice_fusion), channel_id=1, source_target_pairs={{0,16},{16,0},{32,48},{48,32},{64,80},{80,64},{96,112},{112,96},{1... | collective-permute-start | bytes 25165832 | tf_op jit(solution)/shard_map/ppermute | solution.py:51
  236.7 23.1 %all-to-all-start.1 = ((f32[8,64,576]{2,1,0:T(8,128)}), f32[8,64,576]{2,1,0:T(8,128)}, u32[]{:S(2)}, u32[]{:S(2)}) async-start(f32[8,64,576]{2,1,0:T(8,128)} %select_select_fusion), calls=%async_computation.1 | async-start | bytes 2621440 | tf_op jit(solution)/shard_map/all_to_all | solution.py:133
  241.8 9.6 %copy-start.9 = (f32[512,512]{0,1:T(8,128)S(1)}, f32[512,512]{0,1:T(8,128)}, u32[]{:S(2)}) copy-start(f32[512,512]{0,1:T(8,128)} %convolution_bitcast_fusion.3) | copy-start | bytes 3145732
  251.6 3.9 %copy-start.3 = (bf16[256,1024]{1,0:T(8,128)(2,1)S(1)}, bf16[256,1024]{1,0:T(8,128)(2,1)}, u32[]{:S(2)}) copy-start(bf16[256,1024]{1,0:T(8,128)(2,1)} %copy-done.2) | copy-start | bytes 1572868
  261.4 10.1 %copy-start.1 = (bf16[512,1024]{1,0:T(8,128)(2,1)S(1)}, bf16[512,1024]{1,0:T(8,128)(2,1)}, u32[]{:S(2)}) copy-start(bf16[512,1024]{1,0:T(8,128)(2,1)} %param.9) | copy-start | bytes 3145732
  270.2 1.3 copy-start.7
Sparse Core Ops, SparseCore 0:
  36.5 57.1 all-gather.4
  95.9 46.5 all-gather.2
  145.9 86.5 reduce-scatter.3

commit v15 on v6

--- a/solution.py
+++ b/solution.py
@@ -126,7 +126,6 @@
     pick_index = jnp.sum(jnp.where(to_owner, slot_range[None, :], 0), axis=1)
     owner_has = jnp.any(to_owner, axis=1)
     send_grad = jnp.take(summed.reshape(list_len, rank, down_cols + up_cols), pick_index, axis=0)
-    send_grad = jnp.where(owner_has[:, None, None], send_grad, 0.0)
     back_grad = lax.all_to_all(send_grad, "dp", split_axis=0, concat_axis=0, tiled=True)
     land = jnp.where(owned_any, locally_owned_slots, 0)
     arrived = jnp.where(owned_any[:, None, None], back_grad, 0.0)

time: 277 us -> 277 us (level)
  no operation moved by 1% of the time
where the time goes in v15:
time: 277 us; the launch traced here: 276 us
  waiting for transfers between devices  132 us (48%)
  local copies, waits for them, and re-layouts  65.8 us (24%)
  matrix products  28.7 us (10%)
  starting transfers between devices  20.1 us (7%)
  other arithmetic  15 us (5%)
  between operations  14.3 us (5%)
    ppermute x1, waiting for transfers between devices, body(): from_left = lax.ppermute(w_part_full, 'dp', up_x)  44.4 us
    all_gather x1, waiting for transfers between devices, body(): shares = lax.all_gather(slab, 'fsdp', axis=0, tiled=False)  42.9 us
    ppermute x1, waiting for transfers between devices, body(): far_a = lax.ppermute(from_left[:, :half_part], 'dp', up_x)  16 us
    unnamed x40, local copies, waits for them, and re-layouts  15.8 us
    all_gather x1, waiting for transfers between devices, body(): w_part_full = lax.all_gather(w_part, 'fsdp', axis=0, tiled=True)  13.4 us
    dot_general x1, local copies, waits for them, and re-layouts, body(): lax.dot_general(masked_back, tokens, contract, preferred_element_type=f32)  11.9 us
    dot_general x1, matrix products, body(): out_own = jnp.dot(tokens, w_own, preferred_element_type=f32)  11.5 us
    concatenate x1, local copies, waits for them, and re-layouts, body(): jnp.concatenate([part_down, part_up], axis=2)  10.9 us
  transfers between devices with their start and end apart: 10, of which 7 were waited for; matrix products, arithmetic and copies ran while one was open for 32% of the time, Pallas kernels for 0%

profile of v15, /device:TPU:1, one launch (start us, length us, event | category | flops | bytes accessed | tf_op | source)
XLA Modules:
  0.0 275.8 jit_solution(4694963161859849630)
XLA Ops:
  7.2 0.8 copy.44
  8.0 0.1 reshape.433
  8.1 1.4 gather_fusion.1
  9.6 0.1 fusion.18
  9.7 0.1 fusion.1
  9.9 0.1 select_reduce_fusion
  10.0 1.8 gather_fusion.3
  11.8 2.8 %gather_fusion.2 = bf16[8,64,512]{2,1,0:T(8,128)(2,1)S(1)} fusion(bf16[64,64,512]{2,1,0:T(8,128)(2,1)} %param.10, s32[1024]{0:T(1024)S(1)} %pad_clamp_fusion.2), kind=kCustom, calls=%fused_computation.2 | custom fusion | bytes 1048608 | tf_op jit(solution)/shard_map/jit(_take)/gather | solution.py:73
  14.6 0.1 broadcast_select_fusion.3
  14.7 0.1 broadcast_select_fusion.2
  14.8 1.1 maximum_select_fusion
  15.9 5.8 %all-to-all-start = ((bf16[8,64,576]{2,1,0:T(8,128)(2,1)}), bf16[8,64,576]{2,1,0:T(8,128)(2,1)S(1)}, u32[]{:S(2)}, u32[]{:S(2)}) async-start(bf16[8,64,576]{2,1,0:T(8,128)(2,1)} %maximum_select_fusion), calls=%async_computation | async-start | bytes 1310720 | tf_op jit(solution)/shard_map/all_to_all | solution.py:79
  21.7 10.9 %all-to-all-done = bf16[8,64,576]{2,1,0:T(8,128)(2,1)S(1)} async-done(((bf16[8,64,576]{2,1,0:T(8,128)(2,1)}), bf16[8,64,576]{2,1,0:T(8,128)(2,1)S(1)}, u32[]{:S(2)}, u32[]{:S(2)}) %all-to-all-start) | async-done | bytes 589856 | tf_op jit(solution)/shard_map/all_to_all | solution.py:79
  32.6 0.6 gather_fusion.4
  33.2 0.8 bitcast_select_fusion
  34.2 0.8 copy.60
  35.3 1.3 copy.50
  36.6 11.9 %copy.58 = bf16[8192,512]{1,0:T(8,128)(2,1)} copy(bf16[8192,512]{0,1:T(8,128)(2,1)} %bitcast.107) | data formatting | bytes 16777216 | tf_op jit(solution)/shard_map/dot_general | solution.py:113
  48.5 42.9 %all-gather.5.cloned.1.call-done = bf16[16,4,64,576]{3,2,1,0:T(8,128)(2,1)} async-done(((bf16[1,4,64,576]{3,2,1,0:T(8,128)(2,1)}), bf16[16,4,64,576]{3,2,1,0:T(8,128)(2,1)}) %all-gather.5.cloned.1.call-update) | async-done | bytes 4718608 | tf_op jit(solution)/shard_map/all_gather | solution.py:82
  91.4 1.3 slice_bitcast_fusion.1
  92.7 0.7 copy.48
  93.4 0.7 reshape_reshape.7
  94.1 2.9 %slice_bitcast_fusion = bf16[4,64,16,512]{3,1,0,2:T(8,128)(2,1)S(1)} fusion(bf16[16,4,64,576]{3,2,1,0:T(8,128)(2,1)} %all-gather.5.cloned.1.call-done), kind=kLoop, calls=%fused_computation.9 | loop fusion | bytes 8388608 | tf_op jit(solution)/shard_map/transpose | solution.py:83
  97.0 2.4 copy.47
  99.5 4.4 %copy.62 = bf16[32,8,16,512]{3,1,2,0:T(8,128)(2,1)S(1)} copy(bf16[32,8,16,512]{3,2,1,0:T(8,128)(2,1)S(1)} %bitcast.106) | data formatting | bytes 8388608
  103.9 0.5 fusion.20
  104.4 2.4 fusion.19
  106.8 0.1 multiply_reduce_fusion
  107.0 0.9 convolution_bitcast_fusion.1
  108.0 0.2 slice-done.1
  108.1 2.4 convolution_bitcast_fusion
  110.5 5.2 %pad_maximum_fusion = f32[16,256,576]{2,1,0:T(8,128)} fusion(f32[16,256,64]{2,1,0:T(8,128)S(1)} %convolution_bitcast_fusion.1, f32[16,256,512]{2,1,0:T(8,128)S(1)} %convolution_bitcast_fusion), kind=kLoop, calls=%fused_computation.8 | loop fusion | flops 2359296 | bytes 18874368 | tf_op jit(solution)/shard_map/concatenate | solution.py:121
  115.7 10.9 %copy.53 = f32[16,256,576]{1,2,0:T(8,128)} copy(f32[16,256,576]{2,1,0:T(8,128)} %pad_maximum_fusion) | data formatting | bytes 18874368 | tf_op jit(solution)/shard_map/concatenate | solution.py:121
  126.7 13.4 %all-gather.3.cloned.1.call-done = bf16[8192,128]{0,1:T(8,128)(2,1)} async-done(((bf16[512,128]{0,1:T(8,128)(2,1)}), bf16[8192,128]{0,1:T(8,128)(2,1)}) %all-gather.3.cloned.1.call-update) | async-done | bytes 2097168 | tf_op jit(solution)/shard_map/all_gather | solution.py:40
  140.1 1.2 collective-permute-start
  141.3 1.5 collective-permute-start.2
  142.8 44.4 %collective-permute-done = bf16[8192,128]{0,1:T(8,128)(2,1)S(1)} collective-permute-done((bf16[8192,128]{0,1:T(8,128)(2,1)}, bf16[8192,128]{0,1:T(8,128)(2,1)S(1)}, u32[]{:S(2)}, u32[]{:S(2)}) %collective-permute-start) | collective-permute-done | bytes 2097184 | tf_op jit(solution)/shard_map/ppermute | solution.py:43
  187.3 3.2 %constant_dynamic-update-slice_fusion.4 = bf16[8192,512]{0,1:T(8,128)(2,1)} fusion(bf16[8192,128]{0,1:T(8,128)(2,1)} %all-gather.3.cloned.1.call-done), kind=kLoop, calls=%fused_computation.34 | loop fusion | bytes 4194304
  190.7 2.7 collective-permute-start.3
  193.4 1.5 constant_dynamic-update-slice_fusion.3
  194.8 16.0 %collective-permute-done.1 = bf16[8192,64]{0,1:T(8,128)(2,1)S(1)} collective-permute-done((bf16[8192,64]{0,1:T(8,128)(2,1)S(1)}, bf16[8192,64]{0,1:T(8,128)(2,1)S(1)}, u32[]{:S(2)}, u32[]{:S(2)}) %collective-permute-start.1) | collective-permute-done | bytes 1048608 | tf_op jit(solution)/shard_map/ppermute | solution.py:46
  210.8 1.0 constant_dynamic-update-slice_fusion.2
  211.9 1.4 collective-permute-done.3
  213.3 1.0 constant_dynamic-update-slice_fusion.1
  214.3 1.5 constant_dynamic-update-slice_fusion
  215.8 3.5 %collective-permute-start.4 = (bf16[8192,512]{0,1:T(8,128)(2,1)}, bf16[8192,512]{0,1:T(8,128)(2,1)}, u32[]{:S(2)}, u32[]{:S(2)}) collective-permute-start(bf16[8192,512]{0,1:T(8,128)(2,1)} %constant_dynamic-update-slice_fusion), channel_id=1, source_target_pairs={{0,16},{16,0},{32,48},{48,32},{64,80},{80,64},{96,112},{112,96},{1... | collective-permute-start | bytes 25165832 | tf_op jit(solution)/shard_map/ppermute | solution.py:51
  219.4 11.5 %convolution_bitcast_fusion.3 = f32[512,512]{0,1:T(8,128)} fusion(bf16[8192,512]{0,1:T(8,128)(2,1)} %constant_dynamic-update-slice_fusion, bf16[512,8192]{1,0:T(8,128)(2,1)} %param.8), kind=kOutput, calls=%fused_computation.15 | convolution fusion | flops 4294967296 | bytes 17825792 | tf_op jit(solution)/shard_map/dot_general | solution.py:52
  230.9 1.3 copy.54
  232.3 0.6 gather_fusion.5
  232.9 1.2 broadcast_select_fusion.1
  234.1 5.3 %all-to-all-start.1 = ((f32[8,64,576]{2,1,0:T(8,128)}), f32[8,64,576]{2,1,0:T(8,128)}, u32[]{:S(2)}, u32[]{:S(2)}) async-start(f32[8,64,576]{2,1,0:T(8,128)} %broadcast_select_fusion.1), calls=%async_computation.1 | async-start | bytes 2621440 | tf_op jit(solution)/shard_map/all_to_all | solution.py:129
  239.4 9.6 %convolution_bitcast_fusion.2 = f32[512,512]{0,1:T(8,128)S(1)} fusion(bf16[8192,512]{0,1:T(8,128)(2,1)} %collective-permute-done.4, bf16[512,8192]{1,0:T(8,128)(2,1)} %param.8), kind=kOutput, calls=%fused_computation.14 | convolution fusion | flops 4294967296 | bytes 17825792 | tf_op jit(solution)/shard_map/dot_general | solution.py:53
  249.0 0.2 pad_maximum_fusion.1
  249.2 2.0 gather_fusion
  251.2 1.9 copy.57
  253.1 1.4 add_convert_fusion
  254.6 2.8 %all-to-all-done.1 = f32[8,64,576]{2,1,0:T(8,128)} async-done(((f32[8,64,576]{2,1,0:T(8,128)}), f32[8,64,576]{2,1,0:T(8,128)}, u32[]{:S(2)}, u32[]{:S(2)}) %all-to-all-start.1) | async-done | bytes 1179680 | tf_op jit(solution)/shard_map/all_to_all | solution.py:129
  257.4 1.5 broadcast_select_fusion
  258.9 0.1 slice.40
  259.1 4.5 %broadcast_in_dim.142 = f32[64,64,512]{2,1,0:T(8,128)} broadcast(f32[]{:T(128)} %constant.200.clone.1), dimensions={} | broadcast | bytes 8388612 | tf_op jit(solution)/shard_map/broadcast_in_dim | solution.py:132
  263.5 3.3 %scatter_fusion = f32[64,64,512]{2,1,0:T(8,128)} fusion(f32[64,64,512]{2,1,0:T(8,128)} %broadcast_in_dim.142, s32[8]{0:T(128)S(1)} %get-tuple-element.13, f32[8,64,512]{2,1,0:T(8,128)S(1)} %slice.40), kind=kCustom, calls=%fused_computation.6 | custom fusion | flops 262144 | bytes 3145760 | tf_op jit(solution)/shard_map/scatter-add | solution.py:132
  266.8 0.2 broadcast_in_dim.147
  267.1 0.9 scatter_fusion.1
  268.0 1.3 copy-done.7
  (65 shorter events, 1.1 us)
Async XLA Ops:
  7.2 26.9 %copy-start = (bf16[512,1024]{1,0:T(8,128)(2,1)S(1)}, bf16[512,1024]{1,0:T(8,128)(2,1)}, u32[]{:S(2)}) copy-start(bf16[512,1024]{1,0:T(8,128)(2,1)} %param.9) | copy-start | bytes 3145732
  9.5 25.5 %copy-start.9 = (s32[1,64]{1,0:T(1,128)S(1)}, s32[1,64]{1,0:T(1,128)}, u32[]{:S(2)}) copy-start(s32[1,64]{1,0:T(1,128)} %param.13) | copy-start | bytes 772
  9.5 25.7 %copy-start.4 = (bf16[512,1024]{1,0:T(8,128)(2,1)S(1)}, bf16[512,1024]{1,0:T(8,128)(2,1)}, u32[]{:S(2)}) copy-start(bf16[512,1024]{1,0:T(8,128)(2,1)} %param.12) | copy-start | bytes 3145732
  15.9 16.7 %all-to-all-start = ((bf16[8,64,576]{2,1,0:T(8,128)(2,1)}), bf16[8,64,576]{2,1,0:T(8,128)(2,1)S(1)}, u32[]{:S(2)}, u32[]{:S(2)}) async-start(bf16[8,64,576]{2,1,0:T(8,128)(2,1)} %maximum_select_fusion), calls=%async_computation | async-start | bytes 1310720 | tf_op jit(solution)/shard_map/all_to_all | solution.py:79
  21.7 69.7 %all-gather.5.cloned.1.call-start = ((), (), s32[]{:S(2)}) async-start(), calls=%async_computation.4 | async-start | bytes 5570560 | tf_op jit(solution)/shard_map/all_gather | solution.py:82
  34.1 106.0 %all-gather.3.cloned.1.call-start = ((), (), s32[]{:S(2)}) async-start(), calls=%async_computation.3 | async-start | bytes 2228224 | tf_op jit(solution)/shard_map/all_gather | solution.py:40
  35.0 196.0 %reduce-scatter.4.cloned.1.call-start = ((), (), s32[]{:S(2)}) async-start(), calls=%async_computation.5 | async-start | bytes 10027008
  94.1 9.7 %copy-start.2 = (bf16[256,1024]{1,0:T(8,128)(2,1)}, bf16[256,1024]{1,0:T(8,128)(2,1)S(1)}, u32[]{:S(2)}) copy-start(bf16[256,1024]{1,0:T(8,128)(2,1)S(1)} %reshape_reshape.7) | copy-start | bytes 1572868
  97.0 7.4 %slice-start.2 = ((s8[8388608]{0:T(1024)(128)(4,1)}), s8[4194304]{0:T(1024)(128)(4,1)S(1)}, s32[]{:S(2)}) async-start(s8[8388608]{0:T(1024)(128)(4,1)} %bitcast.108), calls=%async_computation.8 | async-start | bytes 8388608
  99.5 4.4 %copy-start.5 = (bf16[512,1024]{1,0:T(8,128)(2,1)S(1)}, bf16[512,1024]{1,0:T(8,128)(2,1)}, u32[]{:S(2)}) copy-start(bf16[512,1024]{1,0:T(8,128)(2,1)} %param.12) | copy-start | bytes 3145732
  99.5 4.9 %slice-start.3 = ((s8[8388608]{0:T(1024)(128)(4,1)}), s8[4194304]{0:T(1024)(128)(4,1)S(1)}, s32[]{:S(2)}) async-start(s8[8388608]{0:T(1024)(128)(4,1)} %bitcast.108), calls=%async_computation.9 | async-start | bytes 8388608
  104.4 3.6 %slice-start = ((s8[8388608]{0:T(1024)(128)(4,1)}), s8[4194304]{0:T(1024)(128)(4,1)S(1)}, s32[]{:S(2)}) async-start(s8[8388608]{0:T(1024)(128)(4,1)} %bitcast.103), calls=%async_computation.6 | async-start | bytes 8388608
  104.4 2.6 copy-start.6
  104.4 3.7 %slice-start.1 = ((s8[8388608]{0:T(1024)(128)(4,1)}), s8[4194304]{0:T(1024)(128)(4,1)S(1)}, s32[]{:S(2)}) async-start(s8[8388608]{0:T(1024)(128)(4,1)} %bitcast.103), calls=%async_computation.7 | async-start | bytes 8388608
  140.1 47.1 %collective-permute-start = (bf16[8192,128]{0,1:T(8,128)(2,1)}, bf16[8192,128]{0,1:T(8,128)(2,1)S(1)}, u32[]{:S(2)}, u32[]{:S(2)}) collective-permute-start(bf16[8192,128]{0,1:T(8,128)(2,1)} %all-gather.3.cloned.1.call-done), channel_id=1, source_target_pairs={{0,32},{16,48},{32,64},{48,80},{64,96},{80,112},{96,0},{112,16},{1... | collective-permute-start | bytes 6291464 | tf_op jit(solution)/shard_map/ppermute | solution.py:43
  141.3 49.3 %collective-permute-start.2 = (bf16[8192,128]{0,1:T(8,128)(2,1)}, bf16[8192,128]{0,1:T(8,128)(2,1)S(1)}, u32[]{:S(2)}, u32[]{:S(2)}) collective-permute-start(bf16[8192,128]{0,1:T(8,128)(2,1)} %all-gather.3.cloned.1.call-done), channel_id=1, source_target_pairs={{0,96},{16,112},{32,0},{48,16},{64,32},{80,48},{96,64},{112,80},{1... | collective-permute-start | bytes 6291464 | tf_op jit(solution)/shard_map/ppermute | solution.py:44
  187.3 23.6 %collective-permute-start.1 = (bf16[8192,64]{0,1:T(8,128)(2,1)S(1)}, bf16[8192,64]{0,1:T(8,128)(2,1)S(1)}, u32[]{:S(2)}, u32[]{:S(2)}) collective-permute-start(bf16[8192,64]{0,1:T(8,128)(2,1)S(1)} %slice.36), channel_id=1, source_target_pairs={{0,32},{16,48},{32,64},{48,80},{64,96},{80,112},{96,0},{112,16},{1... | collective-permute-start | bytes 3145736 | tf_op jit(solution)/shard_map/ppermute | solution.py:46
  190.7 22.6 %collective-permute-start.3 = (bf16[8192,64]{0,1:T(8,128)(2,1)S(1)}, bf16[8192,64]{0,1:T(8,128)(2,1)S(1)}, u32[]{:S(2)}, u32[]{:S(2)}) collective-permute-start(bf16[8192,64]{0,1:T(8,128)(2,1)S(1)} %slice.37), channel_id=1, source_target_pairs={{0,96},{16,112},{32,0},{48,16},{64,32},{80,48},{96,64},{112,80},{1... | collective-permute-start | bytes 3145736 | tf_op jit(solution)/shard_map/ppermute | solution.py:47
  215.8 23.6 %collective-permute-start.4 = (bf16[8192,512]{0,1:T(8,128)(2,1)}, bf16[8192,512]{0,1:T(8,128)(2,1)}, u32[]{:S(2)}, u32[]{:S(2)}) collective-permute-start(bf16[8192,512]{0,1:T(8,128)(2,1)} %constant_dynamic-update-slice_fusion), channel_id=1, source_target_pairs={{0,16},{16,0},{32,48},{48,32},{64,80},{80,64},{96,112},{112,96},{1... | collective-permute-start | bytes 25165832 | tf_op jit(solution)/shard_map/ppermute | solution.py:51
  234.1 23.3 %all-to-all-start.1 = ((f32[8,64,576]{2,1,0:T(8,128)}), f32[8,64,576]{2,1,0:T(8,128)}, u32[]{:S(2)}, u32[]{:S(2)}) async-start(f32[8,64,576]{2,1,0:T(8,128)} %broadcast_select_fusion.1), calls=%async_computation.1 | async-start | bytes 2621440 | tf_op jit(solution)/shard_map/all_to_all | solution.py:129
  239.4 9.6 %copy-start.8 = (f32[512,512]{0,1:T(8,128)S(1)}, f32[512,512]{0,1:T(8,128)}, u32[]{:S(2)}) copy-start(f32[512,512]{0,1:T(8,128)} %convolution_bitcast_fusion.3) | copy-start | bytes 3145732
  249.2 3.9 %copy-start.3 = (bf16[256,1024]{1,0:T(8,128)(2,1)S(1)}, bf16[256,1024]{1,0:T(8,128)(2,1)}, u32[]{:S(2)}) copy-start(bf16[256,1024]{1,0:T(8,128)(2,1)} %copy-done.2) | copy-start | bytes 1572868
  259.0 10.2 %copy-start.1 = (bf16[512,1024]{1,0:T(8,128)(2,1)S(1)}, bf16[512,1024]{1,0:T(8,128)(2,1)}, u32[]{:S(2)}) copy-start(bf16[512,1024]{1,0:T(8,128)(2,1)} %param.9) | copy-start | bytes 3145732
  268.0 1.3 copy-start.7
Sparse Core Ops, SparseCore 0:
  34.2 57.1 all-gather.4
  93.5 46.5 all-gather.2
  143.6 86.6 reduce-scatter.3
